TPU v7x, 256 devices: a whole 4x4x8 slice. The times are simulated.
256 devices in a mesh: row: 8 (over x, core), col: 32 (over z, y).
Axes of the slice: x: 4, y: 4, z: 8, core: 2. Of those that a mesh axis runs over, the one named last changes fastest.
Arguments:
- leaf_rhs: bfloat16 [6144, 128, 512], P(('row', 'col')), may hold values from -6 to 6
- leaf_inverse: bfloat16 [6144, 128, 128], P(('row', 'col')), as said below
- leaf_link: bfloat16 [6144, 128, 128], P(('row', 'col')), may hold values from -0.109375 to 0.109375
- leaf_parent: int32 [6144], P(('row', 'col')), may hold values from 0 to 255, as said below
- node_rhs: bfloat16 [256, 128, 512], P(('row', 'col')), may hold values from -6 to 6
- node_inverse: bfloat16 [256, 128, 128], P(('row', 'col')), as said below
- node_link: bfloat16 [256, 128, 128], P(('row', 'col')), may hold values from -0.25 to 0.25
- node_parent: int32 [256], P('row'), may hold values from 0 to 63, as said below
- middle_rhs: bfloat16 [64, 128, 512], P('row'), may hold values from -6 to 6
- middle_inverse: bfloat16 [64, 128, 128], P('row'), as said below
- middle_link: bfloat16 [64, 128, 128], P('row'), may hold values from -0.125 to 0.125
- middle_parent: int32 [64], P('row'), may hold values from 0 to 3
- top_rhs: bfloat16 [4, 128, 512], replicated, may hold values from -6 to 6
- top_inverse: bfloat16 [4, 128, 128], replicated, as said below
Outputs:
- leaf_result: bfloat16 [6144, 128, 512], P(('row', 'col'))
- node_result: bfloat16 [256, 128, 512], P(('row', 'col'))
- middle_result: bfloat16 [64, 128, 512], P('row')
- top_result: bfloat16 [4, 128, 512], replicated
Inputs may be any that keep to these rules, and one draw needn't show every extreme that they name: `leaf_parent`: the parent of a leaf held by the device at grid row r lies in block row r: it is r * 32 + c for some c below 32. `node_parent`: the parent of second-level supernode r * 32 + c is r * 8 + j for some j below 8. `leaf_inverse`: each block is lower triangular. `node_inverse`: each block is lower triangular. `middle_inverse`: each block is lower triangular. `top_inverse`: each block is lower triangular.
All inputs are finite; a program needn't handle non-finite values.
Results may differ from a plain program's by a relative error of at most 0.017.
Values may be sent and summed in bfloat16 or wider, within the bound.
No kernel may reach another device: no remote copies, remote signals or barrier semaphores. Data moves between devices by JAX's collectives and lax.ppermute only.
A program may use at most 128 MiB of HBM per device.

v0:
```python
import jax
import jax.numpy as jnp
from jax import lax
from jax.sharding import PartitionSpec as P


def apply_block(matrix, vectors):
    return jnp.einsum("nij,njr->nir", matrix, vectors, preferred_element_type=jnp.float32)


def apply_transposed(matrix, vectors):
    return jnp.einsum("nij,nir->njr", matrix, vectors, preferred_element_type=jnp.float32)


def slot_sums(targets, count, values):
    slots = lax.iota(jnp.int32, count)
    select = (slots[:, None] == targets[None, :]).astype(jnp.float32)
    return jnp.einsum("sk,kwr->swr", select, values, precision=lax.Precision.HIGHEST)


def local(
    leaf_rhs,
    leaf_inverse,
    leaf_link,
    leaf_parent,
    node_rhs,
    node_inverse,
    node_link,
    node_parent,
    middle_rhs,
    middle_inverse,
    middle_link,
    middle_parent,
    top_rhs,
    top_inverse,
):
    peers = lax.axis_size("col")
    col_index = lax.axis_index("col")
    middle_count = middle_rhs.shape[0]
    top_count = top_rhs.shape[0]
    leaf_target = leaf_parent % peers
    middle_target = node_parent % middle_count
    leaf_solved = apply_block(leaf_inverse, leaf_rhs).astype(jnp.bfloat16)
    leaf_update = apply_block(leaf_link, leaf_solved)
    node_sum = lax.psum_scatter(
        slot_sums(leaf_target, lax.axis_size("col") * 1, leaf_update),
        "col",
        scatter_dimension=0,
        tiled=True,
    )
    node_y = (node_rhs.astype(jnp.float32) - node_sum).astype(jnp.bfloat16)
    node_solved = apply_block(node_inverse, node_y).astype(jnp.bfloat16)
    own_target = lax.dynamic_slice_in_dim(middle_target, col_index, 1)
    middle_term = slot_sums(own_target, middle_count, apply_block(node_link, node_solved))
    middle_sum = lax.psum(middle_term, "col")
    middle_y = (middle_rhs.astype(jnp.float32) - middle_sum).astype(jnp.bfloat16)
    middle_solved = apply_block(middle_inverse, middle_y).astype(jnp.bfloat16)
    top_term = slot_sums(middle_parent, top_count, apply_block(middle_link, middle_solved))
    top_sum = lax.psum(top_term, "row")
    top_y = (top_rhs.astype(jnp.float32) - top_sum).astype(jnp.bfloat16)
    top_solved = apply_block(top_inverse, top_y).astype(jnp.bfloat16)
    top_result = apply_transposed(top_inverse, top_solved).astype(jnp.bfloat16)
    middle_w = (
        middle_solved.astype(jnp.float32) - apply_transposed(middle_link, top_result[middle_parent])
    ).astype(jnp.bfloat16)
    middle_result = apply_transposed(middle_inverse, middle_w).astype(jnp.bfloat16)
    node_w = (
        node_solved.astype(jnp.float32) - apply_transposed(node_link, middle_result[own_target])
    ).astype(jnp.bfloat16)
    node_result = apply_transposed(node_inverse, node_w).astype(jnp.bfloat16)
    row_result = lax.all_gather(node_result, "col", axis=0, tiled=True)
    leaf_w = (
        leaf_solved.astype(jnp.float32) - apply_transposed(leaf_link, row_result[leaf_target])
    ).astype(jnp.bfloat16)
    leaf_result = apply_transposed(leaf_inverse, leaf_w).astype(jnp.bfloat16)
    return (leaf_result, node_result, middle_result, top_result)


def solution(mesh):
    placed = (
        P(("row", "col"), None, None),
        P(("row", "col"), None, None),
        P(("row", "col"), None, None),
        P(("row", "col")),
        P(("row", "col"), None, None),
        P(("row", "col"), None, None),
        P(("row", "col"), None, None),
        P("row"),
        P("row", None, None),
        P("row", None, None),
        P("row", None, None),
        P("row"),
        P(),
        P(),
    )
    return jax.shard_map(
        local,
        mesh=mesh,
        in_specs=placed,
        out_specs=(
            P(("row", "col"), None, None),
            P(("row", "col"), None, None),
            P("row", None, None),
            P(),
        ),
        check_vma=False,
    )
```

profile of v0, /device:TPU:1, one launch (start us, length us, event | category | flops | bytes accessed | tf_op | source)
XLA Modules:
  0.0 616.8 jit_solution(1758936488983695656)
XLA Ops:
  7.2 1.8 copy-done
  9.1 2.2 convolution_convert_fusion
  11.2 1.7 copy-done.2
  12.9 3.7 convolution_bitcast_fusion
  16.6 6.7 %copy.50 = f32[24,128,512]{2,0,1:T(8,128)} copy(f32[24,128,512]{1,2,0:T(8,128)} %convolution_bitcast_fusion) | data formatting | bytes 12582912 | tf_op jit(solution)/shard_map/nij,njr->nir/dot_general | solution.py:8
  23.3 7.5 %fusion.22 = f32[32,128,512]{2,0,1:T(8,128)S(1)} fusion(f32[24,128,512]{2,0,1:T(8,128)} %copy.50, s32[24]{0:T(128)S(1)} %get-tuple-element.32), kind=kOutput, calls=%fused_computation.35 | convolution fusion | flops 603980544 | bytes 14680160 | tf_op jit(solution)/shard_map/sk,kwr->swr/dot_general | solution.py:18
  30.9 8.1 %copy.51 = f32[32,128,512]{2,1,0:T(8,128)} copy(f32[32,128,512]{2,0,1:T(8,128)S(1)} %fusion.22) | data formatting | bytes 16777216 | tf_op jit(solution)/shard_map/sk,kwr->swr/dot_general | solution.py:18
  39.1 0.5 copy-done.17
  39.6 0.6 dynamic_slice.3
  40.2 0.6 compare_convert_fusion
  40.9 227.1 %reduce-scatter.2.cloned.1.call-done = f32[1,128,512]{2,1,0:T(8,128)} async-done(((f32[32,128,512]{2,1,0:T(8,128)}), f32[1,128,512]{2,1,0:T(8,128)}) %reduce-scatter.2.cloned.1.call-update) | async-done | bytes 262160 | tf_op jit(solution)/shard_map/reduce_scatter | solution.py:45
  268.0 1.2 convolution_convert_fusion.6
  269.5 1.6 broadcast_multiply_fusion
  271.4 152.7 %all-reduce.3.cloned.1.call-done = f32[8,128,512]{2,1,0:T(8,128)} async-done(((f32[8,128,512]{2,1,0:T(8,128)}), f32[8,128,512]{2,1,0:T(8,128)}) %all-reduce.3.cloned.1.call-update) | async-done | bytes 2097168 | tf_op jit(solution)/shard_map/psum | solution.py:55
  424.1 2.1 convolution_convert_fusion.2
  426.3 1.8 convolution_bitcast_fusion.1
  428.0 2.2 copy.54
  430.3 1.1 fusion.26
  431.4 1.3 copy.55
  434.8 64.9 %all-reduce.5.cloned.1.call-done = f32[4,128,512]{2,1,0:T(8,128)} async-done(((f32[4,128,512]{2,1,0:T(8,128)}), f32[4,128,512]{2,1,0:T(8,128)}) %all-reduce.5.cloned.1.call-update) | async-done | bytes 1048592 | tf_op jit(solution)/shard_map/psum | solution.py:59
  499.7 1.7 fusion.7
  501.4 1.7 gather_fusion
  503.1 1.9 convolution_convert_fusion.1
  505.0 1.0 convolution_convert_fusion.5
  506.1 1.0 copy.64
  507.1 1.7 copy.62
  508.7 1.3 copy.63
  510.0 77.5 %all-gather.3.cloned.1.call-done = bf16[4096,512]{0,1:T(8,128)(2,1)} async-done(((bf16[128,512]{0,1:T(8,128)(2,1)}), bf16[4096,512]{0,1:T(8,128)(2,1)}) %all-gather.3.cloned.1.call-update) | async-done | bytes 4194320 | tf_op jit(solution)/shard_map/all_gather | solution.py:71
  587.6 6.5 %copy.71 = bf16[4096,512]{1,0:T(8,128)(2,1)} copy(bf16[4096,512]{0,1:T(8,128)(2,1)} %all-gather.3.cloned.1.call-done) | data formatting | bytes 8388608 | tf_op jit(solution)/shard_map/all_gather | solution.py:71
  594.1 4.7 gather_fusion.1
  598.7 6.9 %convert_bitcast_fusion = bf16[24,128,512]{1,2,0:T(8,128)(2,1)} fusion(bf16[24,128,128]{2,1,0:T(8,128)(2,1)} %param.15, bf16[24,128,512]{2,1,0:T(8,128)(2,1)} %copy-done.2, bf16[24,128,512]{2,1,0:T(8,128)(2,1)} %gather_fusion.1, bf16[24,128,128]{2,1,0:T(8,128)(2,1)} %param.16), kind=kOutput, calls=%fused_computation.5 | convolution fusion | flops 811597824 | bytes 11010048 | tf_op jit(solution)/shard_map/nij,nir->njr/dot_general | solution.py:12
  605.6 4.6 copy.61
  (48 shorter events, 0.8 us)
Async XLA Ops:
  7.2 1.9 copy-start
  7.2 260.8 %reduce-scatter.2.cloned.1.call-start = ((), (), s32[]{:S(2)}) async-start(), calls=%async_computation.1 | async-start | bytes 8650752 | tf_op jit(solution)/shard_map/reduce_scatter | solution.py:45
  9.1 3.8 copy-start.3
  11.2 1.7 copy-start.2
  16.6 6.7 %copy-start.16 = (s32[24]{0:T(128)S(1)}, s32[24]{0:T(128)}, u32[]{:S(2)}) copy-start(s32[24]{0:T(128)} %param.17) | copy-start | bytes 292
  39.0 0.7 copy-start.17
  39.0 229.0 %copy-start.10 = (bf16[1,128,512]{2,1,0:T(8,128)(2,1)S(1)}, bf16[1,128,512]{2,1,0:T(8,128)(2,1)}, u32[]{:S(2)}) copy-start(bf16[1,128,512]{2,1,0:T(8,128)(2,1)} %param.18) | copy-start | bytes 393220
  39.0 229.0 %copy-start.11 = (bf16[1,128,128]{2,1,0:T(8,128)(2,1)S(1)}, bf16[1,128,128]{2,1,0:T(8,128)(2,1)}, u32[]{:S(2)}) copy-start(bf16[1,128,128]{2,1,0:T(8,128)(2,1)} %param.19) | copy-start | bytes 98308
  39.0 230.2 %copy-start.13 = (bf16[1,128,128]{2,1,0:T(8,128)(2,1)S(1)}, bf16[1,128,128]{2,1,0:T(8,128)(2,1)}, u32[]{:S(2)}) copy-start(bf16[1,128,128]{2,1,0:T(8,128)(2,1)} %param.20) | copy-start | bytes 98308
  39.0 385.1 %copy-start.4 = (bf16[8,128,128]{2,1,0:T(8,128)(2,1)S(1)}, bf16[8,128,128]{2,1,0:T(8,128)(2,1)}, u32[]{:S(2)}) copy-start(bf16[8,128,128]{2,1,0:T(8,128)(2,1)} %param.23) | copy-start | bytes 786436
  39.0 385.1 %copy-start.5 = (bf16[8,128,512]{2,1,0:T(8,128)(2,1)S(1)}, bf16[8,128,512]{2,1,0:T(8,128)(2,1)}, u32[]{:S(2)}) copy-start(bf16[8,128,512]{2,1,0:T(8,128)(2,1)} %param.22) | copy-start | bytes 3145732
  39.0 385.1 %all-reduce.3.cloned.1.call-start = ((), (), s32[]{:S(2)}) async-start(), calls=%async_computation.2 | async-start | bytes 4194304 | tf_op jit(solution)/shard_map/psum | solution.py:55
  271.1 155.1 %copy-start.6 = (bf16[8,128,128]{2,1,0:T(8,128)(2,1)S(1)}, bf16[8,128,128]{2,1,0:T(8,128)(2,1)}, u32[]{:S(2)}) copy-start(bf16[8,128,128]{2,1,0:T(8,128)(2,1)} %param.24) | copy-start | bytes 786436
  271.2 228.5 %all-reduce.5.cloned.1.call-start = ((), (), s32[]{:S(2)}) async-start(), calls=%async_computation.3 | async-start | bytes 2097152 | tf_op jit(solution)/shard_map/psum | solution.py:59
  426.3 4.0 copy-start.15
  431.4 68.3 %copy-start.8 = (bf16[4,128,128]{2,1,0:T(8,128)(2,1)S(1)}, bf16[4,128,128]{2,1,0:T(8,128)(2,1)}, u32[]{:S(2)}) copy-start(bf16[4,128,128]{2,1,0:T(8,128)(2,1)} %param.27) | copy-start | bytes 393220
  431.4 68.3 %copy-start.9 = (bf16[4,128,512]{2,1,0:T(8,128)(2,1)S(1)}, bf16[4,128,512]{2,1,0:T(8,128)(2,1)}, u32[]{:S(2)}) copy-start(bf16[4,128,512]{2,1,0:T(8,128)(2,1)} %param.26) | copy-start | bytes 1572868
  432.7 70.4 %copy-start.7 = (bf16[8,128,128]{2,1,0:T(8,128)(2,1)S(1)}, bf16[8,128,128]{2,1,0:T(8,128)(2,1)}, u32[]{:S(2)}) copy-start(bf16[8,128,128]{2,1,0:T(8,128)(2,1)} %param.24) | copy-start | bytes 786436
  432.7 154.8 %all-gather.3.cloned.1.call-start = ((), (), s32[]{:S(2)}) async-start(), calls=%async_computation.4 | async-start | bytes 4325376 | tf_op jit(solution)/shard_map/all_gather | solution.py:71
  501.4 3.6 copy-start.12
  501.4 3.6 copy-start.14
  598.7 11.5 %copy-start.1 = (bf16[24,128,512]{2,1,0:T(8,128)(2,1)S(1)}, bf16[24,128,512]{2,1,0:T(8,128)(2,1)}, u32[]{:S(2)}) copy-start(bf16[24,128,512]{2,1,0:T(8,128)(2,1)} %param.14) | copy-start | bytes 9437188
Sparse Core Ops, SparseCore 0:
  39.1 228.8 reduce-scatter.1
  271.9 152.1 all-reduce.2
  432.9 66.7 all-reduce.4
  506.2 81.3 all-gather.2
where the time goes:
time: 621 us; the launch traced here: 617 us
  waiting for transfers between devices  522 us (84%)
  local copies, waits for them, and re-layouts  44.6 us (7%)
  matrix products  31.2 us (5%)
  between operations  16 us (3%)
    reduce_scatter x1, waiting for transfers between devices, local(): lax.psum_scatter(slot_sums(leaf_target, lax.axis_size('col') * 1, leaf_up...  227 us
    psum x1, waiting for transfers between devices, local(): middle_sum = lax.psum(middle_term, 'col')  153 us
    all_gather x1, waiting for transfers between devices, local(): row_result = lax.all_gather(node_result, 'col', axis=0, tiled=True)  77.5 us
    psum x1, waiting for transfers between devices, local(): top_sum = lax.psum(top_term, 'row')  64.9 us
    unnamed x40, local copies, waits for them, and re-layouts  12.7 us
  transfers between devices with their start and end apart: 4, of which 4 were waited for; matrix products, arithmetic and copies ran while one was open for 1% of the time, Pallas kernels for 0%

commit v1 on v0

--- a/solution.py
+++ b/solution.py
@@ -36,34 +36,47 @@
 ):
     peers = lax.axis_size("col")
     col_index = lax.axis_index("col")
+    width = leaf_rhs.shape[1]
+    columns = leaf_rhs.shape[2]
+    chunk = columns // peers
     middle_count = middle_rhs.shape[0]
     top_count = top_rhs.shape[0]
     leaf_target = leaf_parent % peers
     middle_target = node_parent % middle_count
+
     leaf_solved = apply_block(leaf_inverse, leaf_rhs).astype(jnp.bfloat16)
     leaf_update = apply_block(leaf_link, leaf_solved)
-    node_sum = lax.psum_scatter(
-        slot_sums(leaf_target, lax.axis_size("col") * 1, leaf_update),
-        "col",
-        scatter_dimension=0,
-        tiled=True,
-    )
+    outgoing = slot_sums(leaf_target, peers, leaf_update).astype(jnp.bfloat16)
+    incoming = lax.all_to_all(outgoing, "col", 0, 0, tiled=True)
+    node_sum = jnp.sum(incoming.astype(jnp.float32), axis=0, keepdims=True)
     node_y = (node_rhs.astype(jnp.float32) - node_sum).astype(jnp.bfloat16)
     node_solved = apply_block(node_inverse, node_y).astype(jnp.bfloat16)
-    own_target = lax.dynamic_slice_in_dim(middle_target, col_index, 1)
-    middle_term = slot_sums(own_target, middle_count, apply_block(node_link, node_solved))
-    middle_sum = lax.psum(middle_term, "col")
-    middle_y = (middle_rhs.astype(jnp.float32) - middle_sum).astype(jnp.bfloat16)
+
+    node_update = apply_block(node_link, node_solved)[0]
+    pieces = node_update.reshape(width, peers, chunk).transpose(1, 0, 2)
+    row_updates = lax.all_to_all(pieces, "col", 0, 0, tiled=True)
+    middle_sum = slot_sums(middle_target, middle_count, row_updates)
+    start = col_index * chunk
+    middle_piece = lax.dynamic_slice_in_dim(middle_rhs, start, chunk, 2)
+    middle_y = (middle_piece.astype(jnp.float32) - middle_sum).astype(jnp.bfloat16)
     middle_solved = apply_block(middle_inverse, middle_y).astype(jnp.bfloat16)
     top_term = slot_sums(middle_parent, top_count, apply_block(middle_link, middle_solved))
     top_sum = lax.psum(top_term, "row")
-    top_y = (top_rhs.astype(jnp.float32) - top_sum).astype(jnp.bfloat16)
+    top_piece = lax.dynamic_slice_in_dim(top_rhs, start, chunk, 2)
+    top_y = (top_piece.astype(jnp.float32) - top_sum).astype(jnp.bfloat16)
     top_solved = apply_block(top_inverse, top_y).astype(jnp.bfloat16)
-    top_result = apply_transposed(top_inverse, top_solved).astype(jnp.bfloat16)
+    top_part = apply_transposed(top_inverse, top_solved).astype(jnp.bfloat16)
     middle_w = (
-        middle_solved.astype(jnp.float32) - apply_transposed(middle_link, top_result[middle_parent])
+        middle_solved.astype(jnp.float32) - apply_transposed(middle_link, top_part[middle_parent])
     ).astype(jnp.bfloat16)
-    middle_result = apply_transposed(middle_inverse, middle_w).astype(jnp.bfloat16)
+    middle_part = apply_transposed(middle_inverse, middle_w).astype(jnp.bfloat16)
+    parts = jnp.concatenate([middle_part, top_part], axis=0)
+    gathered = lax.all_gather(parts, "col", axis=0, tiled=False)
+    whole = gathered.transpose(1, 2, 0, 3).reshape(middle_count + top_count, width, columns)
+    middle_result = whole[:middle_count]
+    top_result = whole[middle_count:]
+
+    own_target = lax.dynamic_slice_in_dim(middle_target, col_index, 1)
     node_w = (
         node_solved.astype(jnp.float32) - apply_transposed(node_link, middle_result[own_target])
     ).astype(jnp.bfloat16)

time: 621 us -> 384 us (0.62)
  waiting for transfers between devices: 522 us -> 239 us
  blocking collectives: 0 us -> 22.7 us
  starting transfers between devices: 0.34 us -> 20.8 us
    reduce_scatter x1 -> x0, waiting for transfers between devices: 227 us -> none  [local(): lax.psum_scatter(slot_sums(leaf_target, lax.axis_size('col') * 1, leaf_up...]
    psum x2 -> x0, waiting for transfers between devices: 218 us -> none  [the longest x1 153 us: local(): middle_sum = lax.psum(middle_term, 'col')]
    all_to_all x0 -> x2, waiting for transfers between devices: none -> 99.5 us  [the longest x1 90 us: local(): incoming = lax.all_to_all(outgoing, 'col', 0, 0, tiled=True)]
    all_gather x0 -> x1, waiting for transfers between devices: none -> 66.5 us  [local(): gathered = lax.all_gather(parts, 'col', axis=0, tiled=False)]
    psum x0 -> x1, blocking collectives: none -> 22.7 us  [local(): top_sum = lax.psum(top_term, 'row')]
    all_to_all x0 -> x2, starting transfers between devices: none -> 20.6 us  [the longest x1 12.2 us: local(): incoming = lax.all_to_all(outgoing, 'col', 0, 0, tiled=True)]
    dot_general x2 -> x0, local copies, waits for them, and re-layouts: 9.4 us -> none  [slot_sums(): jnp.einsum('sk,kwr->swr', select, values, precision=lax.Precision.HIGHEST)]
    slice x0 -> x4, local copies, waits for them, and re-layouts: none -> 6.32 us  [the longest x2 3.74 us: local(): top_result = whole[middle_count:]]
  transfers between devices with their start and end apart: 4 -> 4, of which waited for: 4 -> 4; matrix products, arithmetic and copies ran while one was open for 1% -> 4% of each run, Pallas kernels for 0% -> 0%
where the time goes in v1:
time: 384 us; the launch traced here: 380 us
  waiting for transfers between devices  239 us (62%)
  local copies, waits for them, and re-layouts  46.9 us (12%)
  matrix products  28.5 us (7%)
  blocking collectives  22.7 us (6%)
  starting transfers between devices  20.8 us (5%)
  between operations  16.2 us (4%)
  other arithmetic  5.91 us (2%)
    all_to_all x1, waiting for transfers between devices, local(): incoming = lax.all_to_all(outgoing, 'col', 0, 0, tiled=True)  90 us
    all_gather x1, waiting for transfers between devices, local(): row_result = lax.all_gather(node_result, 'col', axis=0, tiled=True)  73 us
    all_gather x1, waiting for transfers between devices, local(): gathered = lax.all_gather(parts, 'col', axis=0, tiled=False)  66.5 us
    psum x1, blocking collectives, local(): top_sum = lax.psum(top_term, 'row')  22.7 us
    unnamed x30, local copies, waits for them, and re-layouts  14.1 us
    all_to_all x1, starting transfers between devices, local(): incoming = lax.all_to_all(outgoing, 'col', 0, 0, tiled=True)  12.2 us
    dot_general x4, matrix products, apply_transposed(): jnp.einsum('nij,nir->njr', matrix, vectors, preferred_element_type=jnp.fl...  10.2 us
    dot_general x6, matrix products, apply_block(): jnp.einsum('nij,njr->nir', matrix, vectors, preferred_element_type=jnp.fl...  10.2 us
  transfers between devices with their start and end apart: 4, of which 4 were waited for; matrix products, arithmetic and copies ran while one was open for 4% of the time, Pallas kernels for 0%

profile of v1, /device:TPU:1, one launch (start us, length us, event | category | flops | bytes accessed | tf_op | source)
XLA Modules:
  0.0 380.0 jit_solution(12176339282254675530)
XLA Ops:
  7.2 1.9 copy-done
  9.1 2.1 convolution_convert_fusion.1
  11.2 1.7 copy-done.1
  12.8 3.7 convolution_bitcast_fusion
  16.5 6.7 %copy.50 = f32[24,128,512]{2,0,1:T(8,128)} copy(f32[24,128,512]{1,2,0:T(8,128)} %convolution_bitcast_fusion) | data formatting | bytes 12582912 | tf_op jit(solution)/shard_map/nij,njr->nir/dot_general | solution.py:8
  23.8 6.0 %convolution_convert_fusion = bf16[32,128,512]{2,0,1:T(8,128)(2,1)S(1)} fusion(f32[24,128,512]{2,0,1:T(8,128)} %copy.50, s32[24]{0:T(128)S(1)} %get-tuple-element.32), kind=kOutput, calls=%fused_computation.8 | convolution fusion | flops 606077696 | bytes 10485856 | tf_op jit(solution)/shard_map/sk,kwr->swr/dot_general | solution.py:18
  29.8 4.4 %copy.51 = bf16[32,128,512]{2,1,0:T(8,128)(2,1)} copy(bf16[32,128,512]{2,0,1:T(8,128)(2,1)S(1)} %convolution_convert_fusion) | data formatting | bytes 8388608 | tf_op jit(solution)/shard_map/convert_element_type | solution.py:49
  34.1 12.2 %all-to-all-start = ((bf16[32,128,512]{2,1,0:T(8,128)(2,1)}), bf16[32,128,512]{2,1,0:T(8,128)(2,1)}, u32[]{:S(2)}, u32[]{:S(2)}) async-start(bf16[32,128,512]{2,1,0:T(8,128)(2,1)} %copy.51), calls=%async_computation | async-start | bytes 8388608 | tf_op jit(solution)/shard_map/all_to_all | solution.py:50
  49.3 90.0 %all-to-all-done = bf16[32,128,512]{2,1,0:T(8,128)(2,1)} async-done(((bf16[32,128,512]{2,1,0:T(8,128)(2,1)}), bf16[32,128,512]{2,1,0:T(8,128)(2,1)}, u32[]{:S(2)}, u32[]{:S(2)}) %all-to-all-start) | async-done | bytes 4194336 | tf_op jit(solution)/shard_map/all_to_all | solution.py:50
  139.4 2.8 convert_reduce_fusion
  142.2 1.1 convolution_convert_fusion.3
  144.2 8.4 %all-to-all-start.1 = ((f32[32,128,16]{1,2,0:T(8,128)}), f32[32,128,16]{1,2,0:T(8,128)}, u32[]{:S(2)}, u32[]{:S(2)}) async-start(f32[32,128,16]{1,2,0:T(8,128)} %convolution_bitcast_fusion.1), calls=%async_computation.1 | async-start | bytes 524288 | tf_op jit(solution)/shard_map/all_to_all | solution.py:57
  154.6 9.5 %all-to-all-done.1 = f32[32,128,16]{1,2,0:T(8,128)} async-done(((f32[32,128,16]{1,2,0:T(8,128)}), f32[32,128,16]{1,2,0:T(8,128)}, u32[]{:S(2)}, u32[]{:S(2)}) %all-to-all-start.1) | async-done | bytes 262176 | tf_op jit(solution)/shard_map/all_to_all | solution.py:57
  164.1 1.2 fusion.8
  165.3 1.2 convolution_convert_fusion.5
  166.5 1.2 convolution_bitcast_fusion.2
  168.5 22.7 %psum.7 = f32[4,128,16]{1,0,2:T(4,128)S(1)} all-reduce(f32[4,128,16]{1,0,2:T(4,128)S(1)} %fusion.21), channel_id=1, replica_groups=mesh['row'=8,'col'=32] {'row'}, use_global_device_ids=true, to_apply=%region_1.2 | all-reduce | flops 8192 | bytes 65536 | tf_op jit(solution)/shard_map/psum | solution.py:64
  192.4 1.3 fusion.10
  194.6 1.2 dynamic_slice.11
  197.8 66.5 %all-gather.5.cloned.1.call-done = bf16[384,128,16]{1,2,0:T(8,128)(2,1)} async-done(((bf16[12,128,16]{1,2,0:T(8,128)(2,1)}), bf16[384,128,16]{1,2,0:T(8,128)(2,1)}) %all-gather.5.cloned.1.call-update) | async-done | bytes 1572880 | tf_op jit(solution)/shard_map/all_gather | solution.py:74
  264.2 1.4 slice.29
  265.6 1.2 copy.58
  266.8 1.9 convolution_convert_fusion.2
  268.7 2.3 copy.66
  271.0 1.9 slice.30
  273.7 1.9 copy.63
  275.5 2.0 copy.67
  277.6 73.0 %all-gather.7.cloned.1.call-done = bf16[4096,512]{0,1:T(8,128)(2,1)} async-done(((bf16[128,512]{0,1:T(8,128)(2,1)}), bf16[4096,512]{0,1:T(8,128)(2,1)}) %all-gather.7.cloned.1.call-update) | async-done | bytes 4194320 | tf_op jit(solution)/shard_map/all_gather | solution.py:84
  350.6 6.5 %copy.72 = bf16[4096,512]{1,0:T(8,128)(2,1)} copy(bf16[4096,512]{0,1:T(8,128)(2,1)} %all-gather.7.cloned.1.call-done) | data formatting | bytes 8388608 | tf_op jit(solution)/shard_map/all_gather | solution.py:84
  357.1 4.7 %gather_fusion.1 = bf16[24,128,512]{2,1,0:T(8,128)(2,1)} fusion(bf16[32,128,512]{2,1,0:T(8,128)(2,1)} %bitcast.82, s32[1024]{0:T(1024)S(1)} %pad_clamp_fusion), kind=kCustom, calls=%fused_computation.1 | custom fusion | bytes 6291552 | tf_op jit(solution)/shard_map/gather | solution.py:86
  361.8 6.8 %convert_bitcast_fusion = bf16[24,128,512]{1,2,0:T(8,128)(2,1)} fusion(bf16[24,128,128]{2,1,0:T(8,128)(2,1)} %param.15, bf16[24,128,512]{2,1,0:T(8,128)(2,1)} %copy-done.1, bf16[24,128,512]{2,1,0:T(8,128)(2,1)} %gather_fusion.1, bf16[24,128,128]{2,1,0:T(8,128)(2,1)} %param.16), kind=kOutput, calls=%fused_computation.6 | convolution fusion | flops 811597824 | bytes 11010048 | tf_op jit(solution)/shard_map/nij,nir->njr/dot_general | solution.py:12
  368.6 4.6 %copy.64 = bf16[24,128,512]{2,1,0:T(8,128)(2,1)} copy(bf16[24,128,512]{1,2,0:T(8,128)(2,1)} %convert_bitcast_fusion) | data formatting | bytes 6291456
  (42 shorter events, 10.0 us)
Async XLA Ops:
  7.2 1.9 copy-start
  7.2 5.7 %copy-start.2 = (bf16[24,128,128]{2,1,0:T(8,128)(2,1)S(1)}, bf16[24,128,128]{2,1,0:T(8,128)(2,1)}, u32[]{:S(2)}) copy-start(bf16[24,128,128]{2,1,0:T(8,128)(2,1)} %param.16) | copy-start | bytes 2359300
  11.2 1.7 copy-start.1
  16.5 6.7 %copy-start.11 = (s32[24]{0:T(128)S(1)}, s32[24]{0:T(128)}, u32[]{:S(2)}) copy-start(s32[24]{0:T(128)} %param.17) | copy-start | bytes 292
  34.1 105.2 %all-to-all-start = ((bf16[32,128,512]{2,1,0:T(8,128)(2,1)}), bf16[32,128,512]{2,1,0:T(8,128)(2,1)}, u32[]{:S(2)}, u32[]{:S(2)}) async-start(bf16[32,128,512]{2,1,0:T(8,128)(2,1)} %copy.51), calls=%async_computation | async-start | bytes 8388608 | tf_op jit(solution)/shard_map/all_to_all | solution.py:50
  46.3 95.8 %copy-start.5 = (bf16[1,128,128]{2,1,0:T(8,128)(2,1)S(1)}, bf16[1,128,128]{2,1,0:T(8,128)(2,1)}, u32[]{:S(2)}) copy-start(bf16[1,128,128]{2,1,0:T(8,128)(2,1)} %param.19) | copy-start | bytes 98308
  46.3 97.0 %copy-start.6 = (bf16[1,128,128]{2,1,0:T(8,128)(2,1)S(1)}, bf16[1,128,128]{2,1,0:T(8,128)(2,1)}, u32[]{:S(2)}) copy-start(bf16[1,128,128]{2,1,0:T(8,128)(2,1)} %param.20) | copy-start | bytes 98308
  49.3 142.0 %copy-start.8 = (bf16[4,128,16]{1,0,2:T(4,128)(2,1)S(1)}, bf16[4,128,16]{1,0,2:T(4,128)(2,1)}, u32[]{:S(2)}) copy-start(bf16[4,128,16]{1,0,2:T(4,128)(2,1)} %copy.74) | copy-start | bytes 49156
  49.3 142.0 %copy-start.4 = (bf16[4,128,128]{2,1,0:T(8,128)(2,1)S(1)}, bf16[4,128,128]{2,1,0:T(8,128)(2,1)}, u32[]{:S(2)}) copy-start(bf16[4,128,128]{2,1,0:T(8,128)(2,1)} %param.27) | copy-start | bytes 393220
  144.2 19.9 %all-to-all-start.1 = ((f32[32,128,16]{1,2,0:T(8,128)}), f32[32,128,16]{1,2,0:T(8,128)}, u32[]{:S(2)}, u32[]{:S(2)}) async-start(f32[32,128,16]{1,2,0:T(8,128)} %convolution_bitcast_fusion.1), calls=%async_computation.1 | async-start | bytes 524288 | tf_op jit(solution)/shard_map/all_to_all | solution.py:57
  152.6 111.6 %all-gather.5.cloned.1.call-start = ((), (), s32[]{:S(2)}) async-start(), calls=%async_computation.2 | async-start | bytes 1622016 | tf_op jit(solution)/shard_map/all_gather | solution.py:74
  154.6 11.9 %copy-start.9 = (s32[32]{0:T(128)}, s32[32]{0:T(128)S(1)}, u32[]{:S(2)}) copy-start(s32[32]{0:T(128)S(1)} %and_select_fusion) | copy-start | bytes 388
  191.3 75.5 %copy-start.7 = (bf16[1,128,128]{2,1,0:T(8,128)(2,1)S(1)}, bf16[1,128,128]{2,1,0:T(8,128)(2,1)}, u32[]{:S(2)}) copy-start(bf16[1,128,128]{2,1,0:T(8,128)(2,1)} %param.20) | copy-start | bytes 98308
  191.6 77.1 %copy-start.10 = (s32[24]{0:T(128)S(1)}, s32[24]{0:T(128)}, u32[]{:S(2)}) copy-start(s32[24]{0:T(128)} %get-tuple-element.31) | copy-start | bytes 292
  194.4 156.2 %all-gather.7.cloned.1.call-start = ((), (), s32[]{:S(2)}) async-start(), calls=%async_computation.3 | async-start | bytes 4325376 | tf_op jit(solution)/shard_map/all_gather | solution.py:84
  268.7 4.2 %copy-start.3 = (bf16[512,128]{1,0:T(8,128)(2,1)S(1)}, bf16[512,128]{1,0:T(8,128)(2,1)}, u32[]{:S(2)}) copy-start(bf16[512,128]{1,0:T(8,128)(2,1)} %convolution_convert_fusion.2) | copy-start | bytes 393220
Sparse Core Ops, SparseCore 0:
  194.5 69.6 all-gather.4
  268.8 81.7 all-gather.6

commit v2 on v0

v2 whole, which is shorter than its diff:
```python
import jax
import jax.numpy as jnp
from jax import lax
from jax.sharding import PartitionSpec as P


def apply_block(matrix, vectors):
    return jnp.einsum("nij,njr->nir", matrix, vectors, preferred_element_type=jnp.float32)


def apply_transposed(matrix, vectors):
    return jnp.einsum("nij,nir->njr", matrix, vectors, preferred_element_type=jnp.float32)


def piece_block(matrix, pieces):
    return jnp.einsum("nij,ncj->nci", matrix, pieces, preferred_element_type=jnp.float32)


def piece_transposed(matrix, pieces):
    return jnp.einsum("nij,nci->ncj", matrix, pieces, preferred_element_type=jnp.float32)


def slot_sums(targets, count, values):
    slots = lax.iota(jnp.int32, count)
    select = (slots[:, None] == targets[None, :]).astype(jnp.float32)
    return jnp.einsum("sk,k...->s...", select, values, precision=lax.Precision.HIGHEST)


def local(
    leaf_rhs,
    leaf_inverse,
    leaf_link,
    leaf_parent,
    node_rhs,
    node_inverse,
    node_link,
    node_parent,
    middle_rhs,
    middle_inverse,
    middle_link,
    middle_parent,
    top_rhs,
    top_inverse,
):
    peers = lax.axis_size("col")
    col_index = lax.axis_index("col")
    width = leaf_rhs.shape[1]
    columns = leaf_rhs.shape[2]
    chunk = columns // peers
    middle_count = middle_rhs.shape[0]
    top_count = top_rhs.shape[0]
    leaf_target = leaf_parent % peers
    middle_target = node_parent % middle_count
    start = col_index * chunk

    node_mats = lax.all_gather(jnp.concatenate([node_inverse, node_link], axis=0), "col", axis=0, tiled=False)
    row_inverse = node_mats[:, 0]
    row_link = node_mats[:, 1]

    leaf_solved = apply_block(leaf_inverse, leaf_rhs).astype(jnp.bfloat16)
    leaf_update = jnp.einsum("kij,kjr->kri", leaf_link, leaf_solved, preferred_element_type=jnp.float32)
    outgoing = jnp.concatenate(
        [slot_sums(leaf_target, peers, leaf_update).astype(jnp.bfloat16), node_rhs.transpose(0, 2, 1)], axis=0
    )
    outgoing = outgoing.reshape(peers + 1, peers, chunk, width).transpose(1, 0, 2, 3)
    incoming = lax.all_to_all(outgoing, "col", 0, 0, tiled=True)
    node_sum = jnp.sum(incoming[:, :peers].astype(jnp.float32), axis=0)
    node_y = (incoming[:, peers].astype(jnp.float32) - node_sum).astype(jnp.bfloat16)
    node_solved = piece_block(row_inverse, node_y).astype(jnp.bfloat16)
    middle_sum = slot_sums(middle_target, middle_count, piece_block(row_link, node_solved))
    middle_piece = lax.dynamic_slice_in_dim(middle_rhs, start, chunk, 2).transpose(0, 2, 1)
    middle_y = (middle_piece.astype(jnp.float32) - middle_sum).astype(jnp.bfloat16)
    middle_solved = piece_block(middle_inverse, middle_y).astype(jnp.bfloat16)
    top_term = slot_sums(middle_parent, top_count, piece_block(middle_link, middle_solved))
    top_sum = lax.psum(top_term, "row")
    top_piece = lax.dynamic_slice_in_dim(top_rhs, start, chunk, 2).transpose(0, 2, 1)
    top_y = (top_piece.astype(jnp.float32) - top_sum).astype(jnp.bfloat16)
    top_solved = piece_block(top_inverse, top_y).astype(jnp.bfloat16)
    top_part = piece_transposed(top_inverse, top_solved).astype(jnp.bfloat16)
    middle_w = (
        middle_solved.astype(jnp.float32) - piece_transposed(middle_link, top_part[middle_parent])
    ).astype(jnp.bfloat16)
    middle_part = piece_transposed(middle_inverse, middle_w).astype(jnp.bfloat16)
    node_w = (
        node_solved.astype(jnp.float32) - piece_transposed(row_link, middle_part[middle_target])
    ).astype(jnp.bfloat16)
    node_part = piece_transposed(row_inverse, node_w).astype(jnp.bfloat16)

    parts = jnp.concatenate([node_part, middle_part, top_part], axis=0)
    gathered = lax.all_gather(parts, "col", axis=0, tiled=False)
    whole = gathered.transpose(1, 3, 0, 2).reshape(parts.shape[0], width, columns)
    row_result = whole[:peers]
    middle_result = whole[peers : peers + middle_count]
    top_result = whole[peers + middle_count :]
    node_result = lax.dynamic_slice_in_dim(row_result, col_index, 1)

    leaf_w = (
        leaf_solved.astype(jnp.float32) - apply_transposed(leaf_link, row_result[leaf_target])
    ).astype(jnp.bfloat16)
    leaf_result = apply_transposed(leaf_inverse, leaf_w).astype(jnp.bfloat16)
    return (leaf_result, node_result, middle_result, top_result)


def solution(mesh):
    placed = (
        P(("row", "col"), None, None),
        P(("row", "col"), None, None),
        P(("row", "col"), None, None),
        P(("row", "col")),
        P(("row", "col"), None, None),
        P(("row", "col"), None, None),
        P(("row", "col"), None, None),
        P("row"),
        P("row", None, None),
        P("row", None, None),
        P("row", None, None),
        P("row"),
        P(),
        P(),
    )
    return jax.shard_map(
        local,
        mesh=mesh,
        in_specs=placed,
        out_specs=(
            P(("row", "col"), None, None),
            P(("row", "col"), None, None),
            P("row", None, None),
            P(),
        ),
        check_vma=False,
    )
```

time: 621 us -> 308 us (0.50)
  waiting for transfers between devices: 522 us -> 189 us
  blocking collectives: 0 us -> 23.8 us
  starting transfers between devices: 0.34 us -> 12.4 us
  local copies, waits for them, and re-layouts: 44.6 us -> 34.2 us
    reduce_scatter x1 -> x0, waiting for transfers between devices: 227 us -> none  [local(): lax.psum_scatter(slot_sums(leaf_target, lax.axis_size('col') * 1, leaf_up...]
    psum x2 -> x0, waiting for transfers between devices: 218 us -> none  [the longest x1 153 us: local(): middle_sum = lax.psum(middle_term, 'col')]
    all_to_all x0 -> x1, waiting for transfers between devices: none -> 104 us  [local(): incoming = lax.all_to_all(outgoing, 'col', 0, 0, tiled=True)]
    psum x0 -> x1, blocking collectives: none -> 23.8 us  [local(): top_sum = lax.psum(top_term, 'row')]
    dot_general x5 -> x0, local copies, waits for them, and re-layouts: 18.5 us -> none  [the longest x2 9.4 us: slot_sums(): jnp.einsum('sk,kwr->swr', select, values, precision=lax.Precision.HIGHEST)]
    slice x0 -> x6, local copies, waits for them, and re-layouts: none -> 13.5 us  [the longest x2 10.7 us: local(): row_result = whole[:peers]]
    all_to_all x0 -> x1, starting transfers between devices: none -> 12.3 us  [local(): incoming = lax.all_to_all(outgoing, 'col', 0, 0, tiled=True)]
    dot_general x6 -> x1, matrix products: 11.1 us -> 2.17 us  [apply_block(): jnp.einsum('nij,njr->nir', matrix, vectors, preferred_element_type=jnp.fl...]
  transfers between devices with their start and end apart: 4 -> 3, of which waited for: 4 -> 2; matrix products, arithmetic and copies ran while one was open for 1% -> 2% of each run, Pallas kernels for 0% -> 0%
where the time goes in v2:
time: 308 us; the launch traced here: 307 us
  waiting for transfers between devices  189 us (61%)
  local copies, waits for them, and re-layouts  34.2 us (11%)
  matrix products  26.1 us (8%)
  blocking collectives  23.8 us (8%)
  between operations  14.3 us (5%)
  starting transfers between devices  12.4 us (4%)
  other arithmetic  7.17 us (2%)
    all_to_all x1, waiting for transfers between devices, local(): incoming = lax.all_to_all(outgoing, 'col', 0, 0, tiled=True)  104 us
    all_gather x1, waiting for transfers between devices, local(): gathered = lax.all_gather(parts, 'col', axis=0, tiled=False)  85.2 us
    psum x1, blocking collectives, local(): top_sum = lax.psum(top_term, 'row')  23.8 us
    all_to_all x1, starting transfers between devices, local(): incoming = lax.all_to_all(outgoing, 'col', 0, 0, tiled=True)  12.3 us
    slice x2, local copies, waits for them, and re-layouts, local(): row_result = whole[:peers]  10.7 us
    dot_general x3, matrix products, slot_sums(): jnp.einsum('sk,k...->s...', select, values, precision=lax.Precision.HIGHEST)  10.3 us
    unnamed x31, local copies, waits for them, and re-layouts  9.82 us
    dot_general x1, matrix products, apply_transposed(): jnp.einsum('nij,nir->njr', matrix, vectors, preferred_element_type=jnp.fl...  6.88 us
  transfers between devices with their start and end apart: 3, of which 2 were waited for; matrix products, arithmetic and copies ran while one was open for 2% of the time, Pallas kernels for 0%

profile of v2, /device:TPU:1, one launch (start us, length us, event | category | flops | bytes accessed | tf_op | source)
XLA Modules:
  0.0 306.9 jit_solution(18374568763429175698)
XLA Ops:
  7.2 0.8 compare_select_fusion
  8.0 1.2 copy.56
  9.2 2.2 convolution_convert_fusion
  11.4 1.0 fusion.38
  12.5 0.6 copy-done.2
  13.1 9.9 %fusion.5 = bf16[32,512,128]{2,0,1:T(8,128)(2,1)S(1)} fusion(f32[24,512,128]{2,1,0:T(8,128)S(1)} %fusion.38, s32[24]{0:T(128)S(1)} %get-tuple-element.21), kind=kOutput, calls=%fused_computation.12 | convolution fusion | flops 606077696 | bytes 10485856 | tf_op jit(solution)/shard_map/sk,k...->s.../dot_general | solution.py:26
  22.9 1.1 pad_maximum_fusion
  24.1 2.7 copy.97
  26.8 12.3 %all-to-all-start = ((bf16[32,33,16,128]{3,2,1,0:T(8,128)(2,1)}), bf16[32,33,16,128]{3,2,1,0:T(8,128)(2,1)}, u32[]{:S(2)}, u32[]{:S(2)}) async-start(bf16[32,33,16,128]{3,2,1,0:T(8,128)(2,1)} %bitcast.73), calls=%async_computation | async-start | bytes 8650752 | tf_op jit(solution)/shard_map/all_to_all | solution.py:66
  39.2 0.6 pad_maximum_fusion.2
  39.9 1.1 constant_dynamic-slice_fusion.1
  41.1 1.1 dynamic-slice_convert_fusion
  42.4 103.7 %all-to-all-done = bf16[32,33,16,128]{3,2,1,0:T(8,128)(2,1)} async-done(((bf16[32,33,16,128]{3,2,1,0:T(8,128)(2,1)}), bf16[32,33,16,128]{3,2,1,0:T(8,128)(2,1)}, u32[]{:S(2)}, u32[]{:S(2)}) %all-to-all-start) | async-done | bytes 4325408 | tf_op jit(solution)/shard_map/all_to_all | solution.py:66
  146.1 2.8 convert_reduce_fusion
  148.9 2.1 convolution_convert_fusion.2
  151.0 1.9 fusion.15
  153.8 23.8 %psum.7 = f32[4,16,128]{2,0,1:T(4,128)S(1)} all-reduce(f32[4,16,128]{2,0,1:T(4,128)S(1)} %fusion.20), channel_id=1, replica_groups=mesh['row'=8,'col'=32] {'row'}, use_global_device_ids=true, to_apply=%region_1.2 | all-reduce | flops 8192 | bytes 65536 | tf_op jit(solution)/shard_map/psum | solution.py:75
  178.9 0.6 gather_fusion.1
  179.5 0.6 convolution_convert_fusion.1
  180.1 0.7 pad_maximum_fusion.1
  180.9 85.2 %all-gather.7.cloned.1.call-done = bf16[1408,16,128]{2,1,0:T(8,128)(2,1)} async-done(((bf16[44,16,128]{2,1,0:T(8,128)(2,1)}), bf16[1408,16,128]{2,1,0:T(8,128)(2,1)}) %all-gather.7.cloned.1.call-update) | async-done | bytes 5767184 | tf_op jit(solution)/shard_map/all_gather | solution.py:90
  266.1 1.1 slice.52
  267.2 1.5 slice.51
  268.7 5.4 %slice.50 = bf16[32,128,32,16]{1,3,0,2:T(8,128)(2,1)} slice(bf16[44,128,32,16]{1,3,0,2:T(8,128)(2,1)} %bitcast.81), slice={[0:32], [0:128], [0:32], [0:16]} | slice | bytes 8388608 | tf_op jit(solution)/shard_map/slice | solution.py:92
  274.1 1.0 copy.74
  275.1 5.3 %copy.66 = bf16[32,128,32,16]{1,3,2,0:T(8,128)(2,1)} copy(bf16[32,128,32,16]{1,3,0,2:T(8,128)(2,1)} %slice.50) | data formatting | bytes 8388608 | tf_op jit(solution)/shard_map/slice | solution.py:92
  280.7 1.3 copy.73
  282.0 0.9 constant_dynamic-slice_fusion
  282.9 4.9 %gather_fusion.2 = bf16[24,128,512]{1,2,0:T(8,128)(2,1)} fusion(bf16[32,128,512]{1,2,0:T(8,128)(2,1)} %bitcast.75, s32[1024]{0:T(1024)S(1)} %pad_clamp_fusion), kind=kCustom, calls=%fused_computation.2 | custom fusion | bytes 6291552 | tf_op jit(solution)/shard_map/gather | solution.py:98
  287.8 6.9 %convert_bitcast_fusion = bf16[24,128,512]{1,2,0:T(8,128)(2,1)} fusion(bf16[24,128,128]{2,1,0:T(8,128)(2,1)} %param.15, bf16[24,128,512]{2,1,0:T(8,128)(2,1)} %copy-done.2, bf16[24,128,512]{1,2,0:T(8,128)(2,1)} %gather_fusion.2, bf16[24,128,128]{2,1,0:T(8,128)(2,1)} %param.16), kind=kOutput, calls=%fused_computation.11 | convolution fusion | flops 811597824 | bytes 11010048 | tf_op jit(solution)/shard_map/nij,nir->njr/dot_general | solution.py:12
  294.7 4.6 %copy.71 = bf16[24,128,512]{2,1,0:T(8,128)(2,1)} copy(bf16[24,128,512]{1,2,0:T(8,128)(2,1)} %convert_bitcast_fusion) | data formatting | bytes 6291456
  299.3 0.8 copy.72
  (45 shorter events, 2.8 us)
Async XLA Ops:
  7.2 2.0 copy-start
  9.2 2.2 copy-start.4
  11.4 1.7 copy-start.2
  26.8 12.4 %copy-start.8 = (bf16[1,128,128]{2,1,0:T(8,128)(2,1)S(1)}, bf16[1,128,128]{2,1,0:T(8,128)(2,1)}, u32[]{:S(2)}) copy-start(bf16[1,128,128]{2,1,0:T(8,128)(2,1)} %param.20) | copy-start | bytes 98308
  26.8 12.4 %copy-start.9 = (bf16[1,128,128]{2,1,0:T(8,128)(2,1)S(1)}, bf16[1,128,128]{2,1,0:T(8,128)(2,1)}, u32[]{:S(2)}) copy-start(bf16[1,128,128]{2,1,0:T(8,128)(2,1)} %param.19) | copy-start | bytes 98308
  26.8 15.5 %copy-start.11 = (s32[32]{0:T(128)S(1)}, s32[32]{0:T(128)}, u32[]{:S(2)}) copy-start(s32[32]{0:T(128)} %param.21) | copy-start | bytes 388
  26.8 15.5 %copy-start.10 = (s32[8]{0:T(128)S(1)}, s32[8]{0:T(128)}, u32[]{:S(2)}) copy-start(s32[8]{0:T(128)} %param.25) | copy-start | bytes 100
  26.8 119.3 %all-to-all-start = ((bf16[32,33,16,128]{3,2,1,0:T(8,128)(2,1)}), bf16[32,33,16,128]{3,2,1,0:T(8,128)(2,1)}, u32[]{:S(2)}, u32[]{:S(2)}) async-start(bf16[32,33,16,128]{3,2,1,0:T(8,128)(2,1)} %bitcast.73), calls=%async_computation | async-start | bytes 8650752 | tf_op jit(solution)/shard_map/all_to_all | solution.py:66
  39.1 109.8 %all-gather.5.cloned.1.call-start = ((), (), s32[]{:S(2)}) async-start(), calls=%async_computation.1 | async-start | bytes 2162688 | tf_op jit(solution)/shard_map/all_gather | solution.py:56
  39.8 226.3 %all-gather.7.cloned.1.call-start = ((), (), s32[]{:S(2)}) async-start(), calls=%async_computation.2 | async-start | bytes 5947392 | tf_op jit(solution)/shard_map/all_gather | solution.py:90
  41.1 112.0 %copy-start.5 = (bf16[8,128,128]{2,1,0:T(8,128)(2,1)S(1)}, bf16[8,128,128]{2,1,0:T(8,128)(2,1)}, u32[]{:S(2)}) copy-start(bf16[8,128,128]{2,1,0:T(8,128)(2,1)} %param.23) | copy-start | bytes 786436
  42.2 111.2 %copy-start.6 = (bf16[8,128,128]{2,1,0:T(8,128)(2,1)S(1)}, bf16[8,128,128]{2,1,0:T(8,128)(2,1)}, u32[]{:S(2)}) copy-start(bf16[8,128,128]{2,1,0:T(8,128)(2,1)} %param.24) | copy-start | bytes 786436
  42.4 135.3 %copy-start.7 = (bf16[4,128,128]{2,1,0:T(8,128)(2,1)S(1)}, bf16[4,128,128]{2,1,0:T(8,128)(2,1)}, u32[]{:S(2)}) copy-start(bf16[4,128,128]{2,1,0:T(8,128)(2,1)} %param.27) | copy-start | bytes 393220
  148.9 30.6 %copy-start.3 = (bf16[64,128,128]{2,1,0:T(8,128)(2,1)S(1)}, bf16[64,128,128]{2,1,0:T(8,128)(2,1)}, u32[]{:S(2)}) copy-start(bf16[64,128,128]{2,1,0:T(8,128)(2,1)} %all-gather.5.cloned.1.call-done) | copy-start | bytes 6291460
  287.8 12.3 %copy-start.1 = (bf16[24,128,512]{2,1,0:T(8,128)(2,1)S(1)}, bf16[24,128,512]{2,1,0:T(8,128)(2,1)}, u32[]{:S(2)}) copy-start(bf16[24,128,512]{2,1,0:T(8,128)(2,1)} %param.14) | copy-start | bytes 9437188
Sparse Core Ops, SparseCore 0:
  43.1 102.8 all-gather.4
  181.0 85.0 all-gather.6

commit v3 on v2

--- a/solution.py
+++ b/solution.py
@@ -1,7 +1,11 @@
 import jax
 import jax.numpy as jnp
 from jax import lax
+from jax.sharding import Mesh
 from jax.sharding import PartitionSpec as P
+
+ROW = ("x", "core")
+COL = ("z", "y")
 
 
 def apply_block(matrix, vectors):
@@ -42,8 +46,10 @@
     top_rhs,
     top_inverse,
 ):
-    peers = lax.axis_size("col")
-    col_index = lax.axis_index("col")
+    y_size = lax.axis_size("y")
+    z_size = lax.axis_size("z")
+    peers = y_size * z_size
+    col_index = lax.axis_index(COL)
     width = leaf_rhs.shape[1]
     columns = leaf_rhs.shape[2]
     chunk = columns // peers
@@ -53,7 +59,7 @@
     middle_target = node_parent % middle_count
     start = col_index * chunk
 
-    node_mats = lax.all_gather(jnp.concatenate([node_inverse, node_link], axis=0), "col", axis=0, tiled=False)
+    node_mats = lax.all_gather(jnp.concatenate([node_inverse, node_link], axis=0), COL, axis=0, tiled=False)
     row_inverse = node_mats[:, 0]
     row_link = node_mats[:, 1]
 
@@ -62,17 +68,26 @@
     outgoing = jnp.concatenate(
         [slot_sums(leaf_target, peers, leaf_update).astype(jnp.bfloat16), node_rhs.transpose(0, 2, 1)], axis=0
     )
-    outgoing = outgoing.reshape(peers + 1, peers, chunk, width).transpose(1, 0, 2, 3)
-    incoming = lax.all_to_all(outgoing, "col", 0, 0, tiled=True)
+    outgoing = outgoing.reshape(peers + 1, z_size, y_size, chunk, width).transpose(1, 2, 0, 3, 4)
+    first = lax.all_to_all(outgoing, "y", 1, 1, tiled=True)
+    partial = jnp.sum(first[:, :, :peers].astype(jnp.float32), axis=1).astype(jnp.bfloat16)
+    second = jnp.concatenate([partial, first[:, :, peers]], axis=1)
+    incoming = lax.all_to_all(second, "z", 0, 0, tiled=True)
     node_sum = jnp.sum(incoming[:, :peers].astype(jnp.float32), axis=0)
-    node_y = (incoming[:, peers].astype(jnp.float32) - node_sum).astype(jnp.bfloat16)
+    own_rhs = incoming[:, peers:].reshape(peers, chunk, width)
+    node_y = (own_rhs.astype(jnp.float32) - node_sum).astype(jnp.bfloat16)
     node_solved = piece_block(row_inverse, node_y).astype(jnp.bfloat16)
     middle_sum = slot_sums(middle_target, middle_count, piece_block(row_link, node_solved))
     middle_piece = lax.dynamic_slice_in_dim(middle_rhs, start, chunk, 2).transpose(0, 2, 1)
     middle_y = (middle_piece.astype(jnp.float32) - middle_sum).astype(jnp.bfloat16)
     middle_solved = piece_block(middle_inverse, middle_y).astype(jnp.bfloat16)
     top_term = slot_sums(middle_parent, top_count, piece_block(middle_link, middle_solved))
-    top_sum = lax.psum(top_term, "row")
+    top_sum = top_term
+    rows = lax.axis_size(ROW)
+    step = 1
+    while step < rows:
+        top_sum = top_sum + lax.ppermute(top_sum, ROW, [(i, i ^ step) for i in range(rows)])
+        step *= 2
     top_piece = lax.dynamic_slice_in_dim(top_rhs, start, chunk, 2).transpose(0, 2, 1)
     top_y = (top_piece.astype(jnp.float32) - top_sum).astype(jnp.bfloat16)
     top_solved = piece_block(top_inverse, top_y).astype(jnp.bfloat16)
@@ -87,7 +102,7 @@
     node_part = piece_transposed(row_inverse, node_w).astype(jnp.bfloat16)
 
     parts = jnp.concatenate([node_part, middle_part, top_part], axis=0)
-    gathered = lax.all_gather(parts, "col", axis=0, tiled=False)
+    gathered = lax.all_gather(parts, COL, axis=0, tiled=False)
     whole = gathered.transpose(1, 3, 0, 2).reshape(parts.shape[0], width, columns)
     row_result = whole[:peers]
     middle_result = whole[peers : peers + middle_count]
@@ -102,30 +117,34 @@
 
 
 def solution(mesh):
+    cores = len({d.core_on_chip for d in mesh.devices[:, 0]})
+    y_size = len({d.coords[1] for d in mesh.devices[0]})
+    grid = mesh.devices.reshape(mesh.shape["row"] // cores, cores, -1, y_size)
+    view = Mesh(grid, ("x", "core", "z", "y"))
     placed = (
-        P(("row", "col"), None, None),
-        P(("row", "col"), None, None),
-        P(("row", "col"), None, None),
-        P(("row", "col")),
-        P(("row", "col"), None, None),
-        P(("row", "col"), None, None),
-        P(("row", "col"), None, None),
-        P("row"),
-        P("row", None, None),
-        P("row", None, None),
-        P("row", None, None),
-        P("row"),
+        P((*ROW, *COL), None, None),
+        P((*ROW, *COL), None, None),
+        P((*ROW, *COL), None, None),
+        P((*ROW, *COL)),
+        P((*ROW, *COL), None, None),
+        P((*ROW, *COL), None, None),
+        P((*ROW, *COL), None, None),
+        P(ROW),
+        P(ROW, None, None),
+        P(ROW, None, None),
+        P(ROW, None, None),
+        P(ROW),
         P(),
         P(),
     )
     return jax.shard_map(
         local,
-        mesh=mesh,
+        mesh=view,
         in_specs=placed,
         out_specs=(
-            P(("row", "col"), None, None),
-            P(("row", "col"), None, None),
-            P("row", None, None),
+            P((*ROW, *COL), None, None),
+            P((*ROW, *COL), None, None),
+            P(ROW, None, None),
             P(),
         ),
         check_vma=False,

time: 308 us -> 284 us (0.922)
  blocking collectives: 23.8 us -> 0 us
  waiting for transfers between devices: 189 us -> 176 us
  starting transfers between devices: 12.4 us -> 21.4 us
    psum x1 -> x0, blocking collectives: 23.8 us -> none  [local(): top_sum = lax.psum(top_term, 'row')]
    all_to_all x1 -> x2, waiting for transfers between devices: 104 us -> 87.1 us  [the longest x1 48.8 us: local(): first = lax.all_to_all(outgoing, 'y', 1, 1, tiled=True)]
    ppermute x0 -> x3, starting transfers between devices: none -> 6.16 us  [local(): lax.ppermute(top_sum, ROW, [(i, i ^ step) for i in range(rows)])]
    all_to_all x1 -> x2, starting transfers between devices: 12.3 us -> 15.2 us  [the longest x1 10.1 us: local(): incoming = lax.all_to_all(second, 'z', 0, 0, tiled=True)]
  transfers between devices with their start and end apart: 3 -> 7, of which waited for: 2 -> 6; matrix products, arithmetic and copies ran while one was open for 2% -> 3% of each run, Pallas kernels for 0% -> 0%
where the time goes in v3:
time: 284 us; the launch traced here: 282 us
  waiting for transfers between devices  176 us (62%)
  local copies, waits for them, and re-layouts  36.9 us (13%)
  matrix products  26 us (9%)
  starting transfers between devices  21.4 us (8%)
  between operations  14.3 us (5%)
  other arithmetic  7.55 us (3%)
    all_gather x1, waiting for transfers between devices, local(): gathered = lax.all_gather(parts, COL, axis=0, tiled=False)  85.9 us
    all_to_all x1, waiting for transfers between devices, local(): first = lax.all_to_all(outgoing, 'y', 1, 1, tiled=True)  48.8 us
    all_to_all x1, waiting for transfers between devices, local(): incoming = lax.all_to_all(second, 'z', 0, 0, tiled=True)  38.2 us
    slice x2, local copies, waits for them, and re-layouts, local(): row_result = whole[:peers]  10.7 us
    dot_general x3, matrix products, slot_sums(): jnp.einsum('sk,k...->s...', select, values, precision=lax.Precision.HIGHEST)  10.3 us
    all_to_all x1, starting transfers between devices, local(): incoming = lax.all_to_all(second, 'z', 0, 0, tiled=True)  10.1 us
    unnamed x31, local copies, waits for them, and re-layouts  9.82 us
    dot_general x1, matrix products, apply_transposed(): jnp.einsum('nij,nir->njr', matrix, vectors, preferred_element_type=jnp.fl...  6.88 us
  transfers between devices with their start and end apart: 7, of which 6 were waited for; matrix products, arithmetic and copies ran while one was open for 3% of the time, Pallas kernels for 0%

profile of v3, /device:TPU:1, one launch (start us, length us, event | category | flops | bytes accessed | tf_op | source)
XLA Modules:
  0.0 282.4 jit_solution(4434043470847596211)
XLA Ops:
  8.0 1.2 copy.85
  9.2 2.2 convolution_convert_fusion
  11.4 1.0 fusion.38
  13.1 9.9 %fusion.5 = bf16[32,512,128]{2,0,1:T(8,128)(2,1)S(1)} fusion(f32[24,512,128]{2,1,0:T(8,128)S(1)} %fusion.38, s32[24]{0:T(128)S(1)} %get-tuple-element.25), kind=kOutput, calls=%fused_computation.12 | convolution fusion | flops 606077696 | bytes 10485856 | tf_op jit(solution)/shard_map/sk,k...->s.../dot_general | solution.py:30
  22.9 1.1 pad_maximum_fusion
  24.1 3.2 %copy.133 = bf16[33,8,4,16,128]{4,3,1,0,2:T(8,128)(2,1)} copy(bf16[33,8,4,16,128]{4,0,3,2,1:T(8,128)(2,1)S(1)} %bitcast.71) | data formatting | bytes 8650752 | tf_op jit(solution)/shard_map/reshape | solution.py:71
  27.3 5.1 %all-to-all-start = ((bf16[8,4,33,16,128]{4,3,0,2,1:T(8,128)(2,1)}), bf16[8,4,33,16,128]{4,3,0,2,1:T(8,128)(2,1)}, u32[]{:S(2)}, u32[]{:S(2)}) async-start(bf16[8,4,33,16,128]{4,3,0,2,1:T(8,128)(2,1)} %bitcast.72), calls=%async_computation | async-start | bytes 8650752 | tf_op jit(solution)/shard_map/all_to_all | solution.py:72
  33.2 48.8 %all-to-all-done = bf16[8,4,33,16,128]{4,3,0,2,1:T(8,128)(2,1)} async-done(((bf16[8,4,33,16,128]{4,3,0,2,1:T(8,128)(2,1)}), bf16[8,4,33,16,128]{4,3,0,2,1:T(8,128)(2,1)}, u32[]{:S(2)}, u32[]{:S(2)}) %all-to-all-start) | async-done | bytes 4325408 | tf_op jit(solution)/shard_map/all_to_all | solution.py:72
  82.0 0.9 slice_bitcast_fusion.7
  82.9 3.0 %slice_reduce_fusion = bf16[8,32,16,128]{3,2,0,1:T(8,128)(2,1)S(1)} fusion(bf16[8,4,33,16,128]{4,3,0,2,1:T(8,128)(2,1)} %all-to-all-done), kind=kLoop, calls=%fused_computation.9 | loop fusion | flops 1572864 | bytes 5242880 | tf_op jit(solution)/shard_map/reduce_sum | solution.py:73
  86.0 1.3 copy.90
  87.3 10.1 %all-to-all-start.1 = ((bf16[8,36,16,128]{3,2,1,0:T(8,128)(2,1)}), bf16[8,36,16,128]{3,2,1,0:T(8,128)(2,1)S(1)}, u32[]{:S(2)}, u32[]{:S(2)}) async-start(bf16[8,36,16,128]{3,2,1,0:T(8,128)(2,1)} %copy.90), calls=%async_computation.1 | async-start | bytes 2359296 | tf_op jit(solution)/shard_map/all_to_all | solution.py:75
  97.4 1.1 constant_dynamic-slice_fusion.1
  98.7 38.2 %all-to-all-done.1 = bf16[8,36,16,128]{3,2,1,0:T(8,128)(2,1)S(1)} async-done(((bf16[8,36,16,128]{3,2,1,0:T(8,128)(2,1)}), bf16[8,36,16,128]{3,2,1,0:T(8,128)(2,1)S(1)}, u32[]{:S(2)}, u32[]{:S(2)}) %all-to-all-start.1) | async-done | bytes 1179680 | tf_op jit(solution)/shard_map/all_to_all | solution.py:75
  137.4 2.0 convolution_convert_fusion.2
  139.4 1.9 fusion.15
  142.3 1.9 collective-permute-start
  144.2 1.0 dynamic-slice_convert_fusion
  145.2 1.3 collective-permute-start.1
  146.5 1.5 collective-permute-done.1
  148.1 3.0 %collective-permute-start.2 = (f32[4,16,128]{2,0,1:T(4,128)S(1)}, f32[4,16,128]{2,0,1:T(4,128)S(1)}, u32[]{:S(2)}, u32[]{:S(2)}) collective-permute-start(f32[4,16,128]{2,0,1:T(4,128)S(1)} %add.46), channel_id=1, source_target_pairs={{0,128},{32,160},{64,192},{96,224},{128,0},{160,32},{192,64},{224,... | collective-permute-start | bytes 98312 | tf_op jit(solution)/shard_map/ppermute | solution.py:89
  151.1 1.3 collective-permute-done.2
  155.6 85.9 %all-gather.7.cloned.1.call-done = bf16[1408,16,128]{2,1,0:T(8,128)(2,1)} async-done(((bf16[44,16,128]{2,1,0:T(8,128)(2,1)}), bf16[1408,16,128]{2,1,0:T(8,128)(2,1)}) %all-gather.7.cloned.1.call-update) | async-done | bytes 5767184 | tf_op jit(solution)/shard_map/all_gather | solution.py:105
  241.5 1.1 slice.62
  242.6 1.5 slice.61
  244.1 5.4 %slice.60 = bf16[32,128,32,16]{1,3,0,2:T(8,128)(2,1)} slice(bf16[44,128,32,16]{1,3,0,2:T(8,128)(2,1)} %bitcast.80), slice={[0:32], [0:128], [0:32], [0:16]} | slice | bytes 8388608 | tf_op jit(solution)/shard_map/slice | solution.py:107
  249.5 1.0 copy.107
  250.6 5.3 %copy.99 = bf16[32,128,32,16]{1,3,2,0:T(8,128)(2,1)} copy(bf16[32,128,32,16]{1,3,0,2:T(8,128)(2,1)} %slice.60) | data formatting | bytes 8388608 | tf_op jit(solution)/shard_map/slice | solution.py:107
  256.1 1.3 copy.106
  258.3 4.9 %gather_fusion.2 = bf16[24,128,512]{1,2,0:T(8,128)(2,1)} fusion(bf16[32,128,512]{1,2,0:T(8,128)(2,1)} %bitcast.74, s32[1024]{0:T(1024)S(1)} %pad_clamp_fusion), kind=kCustom, calls=%fused_computation.2 | custom fusion | bytes 6291552 | tf_op jit(solution)/shard_map/gather | solution.py:113
  263.2 6.9 %convert_bitcast_fusion = bf16[24,128,512]{1,2,0:T(8,128)(2,1)} fusion(bf16[24,128,128]{2,1,0:T(8,128)(2,1)} %param.15, bf16[24,128,512]{2,1,0:T(8,128)(2,1)} %copy-done.2, bf16[24,128,512]{1,2,0:T(8,128)(2,1)} %gather_fusion.2, bf16[24,128,128]{2,1,0:T(8,128)(2,1)} %param.16), kind=kOutput, calls=%fused_computation.11 | convolution fusion | flops 811597824 | bytes 11010048 | tf_op jit(solution)/shard_map/nij,nir->njr/dot_general | solution.py:16
  270.1 4.6 %copy.104 = bf16[24,128,512]{2,1,0:T(8,128)(2,1)} copy(bf16[24,128,512]{1,2,0:T(8,128)(2,1)} %convert_bitcast_fusion) | data formatting | bytes 6291456
  (59 shorter events, 9.1 us)
Async XLA Ops:
  7.2 2.0 copy-start
  9.2 2.2 copy-start.4
  11.4 1.7 copy-start.2
  27.3 5.2 %copy-start.8 = (bf16[1,128,128]{2,1,0:T(8,128)(2,1)S(1)}, bf16[1,128,128]{2,1,0:T(8,128)(2,1)}, u32[]{:S(2)}) copy-start(bf16[1,128,128]{2,1,0:T(8,128)(2,1)} %param.20) | copy-start | bytes 98308
  27.3 5.2 %copy-start.9 = (bf16[1,128,128]{2,1,0:T(8,128)(2,1)S(1)}, bf16[1,128,128]{2,1,0:T(8,128)(2,1)}, u32[]{:S(2)}) copy-start(bf16[1,128,128]{2,1,0:T(8,128)(2,1)} %param.19) | copy-start | bytes 98308
  27.3 54.7 %all-to-all-start = ((bf16[8,4,33,16,128]{4,3,0,2,1:T(8,128)(2,1)}), bf16[8,4,33,16,128]{4,3,0,2,1:T(8,128)(2,1)}, u32[]{:S(2)}, u32[]{:S(2)}) async-start(bf16[8,4,33,16,128]{4,3,0,2,1:T(8,128)(2,1)} %bitcast.72), calls=%async_computation | async-start | bytes 8650752 | tf_op jit(solution)/shard_map/all_to_all | solution.py:72
  32.4 104.9 %all-gather.5.cloned.1.call-start = ((), (), s32[]{:S(2)}) async-start(), calls=%async_computation.2 | async-start | bytes 2162688 | tf_op jit(solution)/shard_map/all_gather | solution.py:62
  86.0 12.7 %copy-start.10 = (s32[8]{0:T(128)S(1)}, s32[8]{0:T(128)}, u32[]{:S(2)}) copy-start(s32[8]{0:T(128)} %param.25) | copy-start | bytes 100
  86.0 12.7 %copy-start.11 = (s32[32]{0:T(128)S(1)}, s32[32]{0:T(128)}, u32[]{:S(2)}) copy-start(s32[32]{0:T(128)} %param.21) | copy-start | bytes 388
  87.3 49.7 %all-to-all-start.1 = ((bf16[8,36,16,128]{3,2,1,0:T(8,128)(2,1)}), bf16[8,36,16,128]{3,2,1,0:T(8,128)(2,1)S(1)}, u32[]{:S(2)}, u32[]{:S(2)}) async-start(bf16[8,36,16,128]{3,2,1,0:T(8,128)(2,1)} %copy.90), calls=%async_computation.1 | async-start | bytes 2359296 | tf_op jit(solution)/shard_map/all_to_all | solution.py:75
  97.3 44.3 %copy-start.5 = (bf16[8,128,128]{2,1,0:T(8,128)(2,1)S(1)}, bf16[8,128,128]{2,1,0:T(8,128)(2,1)}, u32[]{:S(2)}) copy-start(bf16[8,128,128]{2,1,0:T(8,128)(2,1)} %param.23) | copy-start | bytes 786436
  97.3 44.5 %copy-start.6 = (bf16[8,128,128]{2,1,0:T(8,128)(2,1)S(1)}, bf16[8,128,128]{2,1,0:T(8,128)(2,1)}, u32[]{:S(2)}) copy-start(bf16[8,128,128]{2,1,0:T(8,128)(2,1)} %param.24) | copy-start | bytes 786436
  97.4 144.2 %all-gather.7.cloned.1.call-start = ((), (), s32[]{:S(2)}) async-start(), calls=%async_computation.3 | async-start | bytes 5947392 | tf_op jit(solution)/shard_map/all_gather | solution.py:105
  137.0 15.5 %copy-start.7 = (bf16[4,128,128]{2,1,0:T(8,128)(2,1)S(1)}, bf16[4,128,128]{2,1,0:T(8,128)(2,1)}, u32[]{:S(2)}) copy-start(bf16[4,128,128]{2,1,0:T(8,128)(2,1)} %param.27) | copy-start | bytes 393220
  137.4 16.8 %copy-start.3 = (bf16[64,128,128]{2,1,0:T(8,128)(2,1)S(1)}, bf16[64,128,128]{2,1,0:T(8,128)(2,1)}, u32[]{:S(2)}) copy-start(bf16[64,128,128]{2,1,0:T(8,128)(2,1)} %all-gather.5.cloned.1.call-done) | copy-start | bytes 6291460
  142.3 2.9 %collective-permute-start = (f32[4,16,128]{2,0,1:T(4,128)S(1)}, f32[4,16,128]{2,0,1:T(4,128)S(1)}, u32[]{:S(2)}, u32[]{:S(2)}) collective-permute-start(f32[4,16,128]{2,0,1:T(4,128)S(1)} %fusion.20), channel_id=1, source_target_pairs={{0,32},{32,0},{64,96},{96,64},{128,160},{160,128},{192,224},{224,1... | collective-permute-start | bytes 98312 | tf_op jit(solution)/shard_map/ppermute | solution.py:89
  145.2 2.9 %collective-permute-start.1 = (f32[4,16,128]{2,0,1:T(4,128)S(1)}, f32[4,16,128]{2,0,1:T(4,128)S(1)}, u32[]{:S(2)}, u32[]{:S(2)}) collective-permute-start(f32[4,16,128]{2,0,1:T(4,128)S(1)} %add.45), channel_id=1, source_target_pairs={{0,64},{32,96},{64,0},{96,32},{128,192},{160,224},{192,128},{224,1... | collective-permute-start | bytes 98312 | tf_op jit(solution)/shard_map/ppermute | solution.py:89
  148.1 4.4 %collective-permute-start.2 = (f32[4,16,128]{2,0,1:T(4,128)S(1)}, f32[4,16,128]{2,0,1:T(4,128)S(1)}, u32[]{:S(2)}, u32[]{:S(2)}) collective-permute-start(f32[4,16,128]{2,0,1:T(4,128)S(1)} %add.46), channel_id=1, source_target_pairs={{0,128},{32,160},{64,192},{96,224},{128,0},{160,32},{192,64},{224,... | collective-permute-start | bytes 98312 | tf_op jit(solution)/shard_map/ppermute | solution.py:89
  263.2 12.3 %copy-start.1 = (bf16[24,128,512]{2,1,0:T(8,128)(2,1)S(1)}, bf16[24,128,512]{2,1,0:T(8,128)(2,1)}, u32[]{:S(2)}) copy-start(bf16[24,128,512]{2,1,0:T(8,128)(2,1)} %param.14) | copy-start | bytes 9437188
Sparse Core Ops, SparseCore 0:
  36.4 100.9 all-gather.4
  155.7 85.7 all-gather.6

commit v4 on v3

--- a/solution.py
+++ b/solution.py
@@ -102,16 +102,15 @@
     node_part = piece_transposed(row_inverse, node_w).astype(jnp.bfloat16)
 
     parts = jnp.concatenate([node_part, middle_part, top_part], axis=0)
-    gathered = lax.all_gather(parts, COL, axis=0, tiled=False)
-    whole = gathered.transpose(1, 3, 0, 2).reshape(parts.shape[0], width, columns)
-    row_result = whole[:peers]
-    middle_result = whole[peers : peers + middle_count]
-    top_result = whole[peers + middle_count :]
-    node_result = lax.dynamic_slice_in_dim(row_result, col_index, 1)
+    gathered = lax.all_gather(lax.all_gather(parts, "y", axis=0, tiled=False), "z", axis=0, tiled=True)
+    upper = gathered[:, peers:].transpose(1, 3, 0, 2).reshape(middle_count + top_count, width, columns)
+    middle_result = upper[:middle_count]
+    top_result = upper[middle_count:]
+    node_result = lax.dynamic_index_in_dim(gathered, col_index, 1).transpose(1, 3, 0, 2).reshape(1, width, columns)
 
-    leaf_w = (
-        leaf_solved.astype(jnp.float32) - apply_transposed(leaf_link, row_result[leaf_target])
-    ).astype(jnp.bfloat16)
+    parent_t = gathered[:, leaf_target].transpose(1, 0, 2, 3).reshape(leaf_target.shape[0], columns, width)
+    correction = jnp.einsum("kij,kci->kjc", leaf_link, parent_t, preferred_element_type=jnp.float32)
+    leaf_w = (leaf_solved.astype(jnp.float32) - correction).astype(jnp.bfloat16)
     leaf_result = apply_transposed(leaf_inverse, leaf_w).astype(jnp.bfloat16)
     return (leaf_result, node_result, middle_result, top_result)
 

time: 284 us -> 282 us (level)
  waiting for transfers between devices: 176 us -> 158 us
  blocking collectives: 0 us -> 12 us
  matrix products: 26 us -> 30.9 us
  other arithmetic: 7.55 us -> 12.3 us
  local copies, waits for them, and re-layouts: 36.9 us -> 32.7 us
    all_gather x1, waiting for transfers between devices: 85.9 us -> 69.6 us  [local(): lax.all_gather(lax.all_gather(parts, 'y', axis=0, tiled=False), 'z', axis...]
    all_gather x0 -> x1, blocking collectives: none -> 12 us  [local(): lax.all_gather(parts, 'y', axis=0, tiled=False)]
    slice x6 -> x2, local copies, waits for them, and re-layouts: 13.5 us -> 2.06 us  [the longest x1 1.22 us: local(): middle_result = upper[:middle_count]]
    dot_general x3, matrix products: 1.22 us -> 5.47 us  [piece_transposed(): jnp.einsum('nij,nci->ncj', matrix, pieces, preferred_element_type=jnp.flo...]
    unnamed x31 -> x27, local copies, waits for them, and re-layouts: 9.82 us -> 13.2 us
  transfers between devices with their start and end apart: 7 -> 7, of which waited for: 6 -> 5; matrix products, arithmetic and copies ran while one was open for 3% -> 5% of each run, Pallas kernels for 0% -> 0%
where the time goes in v4:
time: 282 us; the launch traced here: 281 us
  waiting for transfers between devices  158 us (56%)
  local copies, waits for them, and re-layouts  32.7 us (12%)
  matrix products  30.9 us (11%)
  starting transfers between devices  20.7 us (7%)
  between operations  14.3 us (5%)
  other arithmetic  12.3 us (4%)
  blocking collectives  12 us (4%)
    all_gather x1, waiting for transfers between devices, local(): lax.all_gather(lax.all_gather(parts, 'y', axis=0, tiled=False), 'z', axis...  69.6 us
    all_to_all x1, waiting for transfers between devices, local(): first = lax.all_to_all(outgoing, 'y', 1, 1, tiled=True)  48.8 us
    all_to_all x1, waiting for transfers between devices, local(): incoming = lax.all_to_all(second, 'z', 0, 0, tiled=True)  36.7 us
    unnamed x27, local copies, waits for them, and re-layouts  13.2 us
    all_gather x1, blocking collectives, local(): lax.all_gather(parts, 'y', axis=0, tiled=False)  12 us
    dot_general x3, matrix products, slot_sums(): jnp.einsum('sk,k...->s...', select, values, precision=lax.Precision.HIGHEST)  11.1 us
    all_to_all x1, starting transfers between devices, local(): incoming = lax.all_to_all(second, 'z', 0, 0, tiled=True)  10.1 us
    dot_general x1, matrix products, apply_transposed(): jnp.einsum('nij,nir->njr', matrix, vectors, preferred_element_type=jnp.fl...  6.69 us
  transfers between devices with their start and end apart: 7, of which 5 were waited for; matrix products, arithmetic and copies ran while one was open for 5% of the time, Pallas kernels for 0%

profile of v4, /device:TPU:1, one launch (start us, length us, event | category | flops | bytes accessed | tf_op | source)
XLA Modules:
  0.0 280.8 jit_solution(7124551260867050995)
XLA Ops:
  8.0 1.2 copy.84
  9.2 2.2 convolution_convert_fusion
  13.1 9.9 %fusion.5 = bf16[32,512,128]{2,0,1:T(8,128)(2,1)S(1)} fusion(f32[24,512,128]{2,1,0:T(8,128)S(1)} %fusion.38, s32[24]{0:T(128)S(1)} %get-tuple-element.25), kind=kOutput, calls=%fused_computation.12 | convolution fusion | flops 606077696 | bytes 10485856 | tf_op jit(solution)/shard_map/sk,k...->s.../dot_general | solution.py:30
  22.9 1.1 pad_maximum_fusion
  24.1 3.2 %copy.134 = bf16[33,8,4,16,128]{4,3,1,0,2:T(8,128)(2,1)} copy(bf16[33,8,4,16,128]{4,0,3,2,1:T(8,128)(2,1)S(1)} %bitcast.76) | data formatting | bytes 8650752 | tf_op jit(solution)/shard_map/reshape | solution.py:71
  27.3 5.1 %all-to-all-start = ((bf16[8,4,33,16,128]{4,3,0,2,1:T(8,128)(2,1)}), bf16[8,4,33,16,128]{4,3,0,2,1:T(8,128)(2,1)}, u32[]{:S(2)}, u32[]{:S(2)}) async-start(bf16[8,4,33,16,128]{4,3,0,2,1:T(8,128)(2,1)} %bitcast.77), calls=%async_computation | async-start | bytes 8650752 | tf_op jit(solution)/shard_map/all_to_all | solution.py:72
  33.2 48.8 %all-to-all-done = bf16[8,4,33,16,128]{4,3,0,2,1:T(8,128)(2,1)} async-done(((bf16[8,4,33,16,128]{4,3,0,2,1:T(8,128)(2,1)}), bf16[8,4,33,16,128]{4,3,0,2,1:T(8,128)(2,1)}, u32[]{:S(2)}, u32[]{:S(2)}) %all-to-all-start) | async-done | bytes 4325408 | tf_op jit(solution)/shard_map/all_to_all | solution.py:72
  82.9 3.0 %slice_reduce_fusion = bf16[8,32,16,128]{3,2,0,1:T(8,128)(2,1)S(1)} fusion(bf16[8,4,33,16,128]{4,3,0,2,1:T(8,128)(2,1)} %all-to-all-done), kind=kLoop, calls=%fused_computation.9 | loop fusion | flops 1572864 | bytes 5242880 | tf_op jit(solution)/shard_map/reduce_sum | solution.py:73
  86.0 1.2 copy.89
  87.2 10.1 %all-to-all-start.1 = ((bf16[8,36,16,128]{3,2,1,0:T(8,128)(2,1)}), bf16[8,36,16,128]{3,2,1,0:T(8,128)(2,1)}, u32[]{:S(2)}, u32[]{:S(2)}) async-start(bf16[8,36,16,128]{3,2,1,0:T(8,128)(2,1)} %copy.89), calls=%async_computation.1 | async-start | bytes 2359296 | tf_op jit(solution)/shard_map/all_to_all | solution.py:75
  100.4 36.7 %all-to-all-done.1 = bf16[8,36,16,128]{3,2,1,0:T(8,128)(2,1)} async-done(((bf16[8,36,16,128]{3,2,1,0:T(8,128)(2,1)}), bf16[8,36,16,128]{3,2,1,0:T(8,128)(2,1)}, u32[]{:S(2)}, u32[]{:S(2)}) %all-to-all-start.1) | async-done | bytes 1179680 | tf_op jit(solution)/shard_map/all_to_all | solution.py:75
  137.1 1.6 slice.52
  138.7 2.1 convert_reduce_fusion
  140.8 2.0 convolution_convert_fusion.2
  142.8 1.9 fusion.15
  146.7 1.4 collective-permute-start
  149.1 1.3 collective-permute-start.1
  150.4 1.6 collective-permute-done.1
  152.6 2.7 collective-permute-start.2
  156.1 1.1 collective-permute-done.2
  158.0 1.3 convolution_convert_fusion.5
  159.9 1.3 convolution_convert_fusion.3
  161.8 2.9 %convolution_convert_fusion.1 = bf16[32,16,128]{2,1,0:T(8,128)(2,1)} fusion(bf16[32,16,128]{2,1,0:T(8,128)(2,1)S(1)} %gather_fusion.1, bf16[32,2,128,128]{3,2,1,0:T(8,128)(2,1)} %bitcast.81, bf16[32,16,128]{2,1,0:T(8,128)(2,1)S(1)} %convolution_convert_fusion.2), kind=kOutput, calls=%fused_computation.19 | convolution fusion | flops 33816576 | bytes 2490368 | tf_op jit(solution)/shard_map/nij,nci->ncj/dot_general | solution.py:24
  165.6 12.0 %all-gather.1 = bf16[176,16,128]{2,1,0:T(8,128)(2,1)} all-gather(bf16[44,16,128]{2,1,0:T(8,128)(2,1)S(1)} %pad_maximum_fusion.2), channel_id=3, replica_groups=mesh['x'=4,'core'=2,'z'=8,'y'=4] {'y'}, dimensions={0}, use_global_device_ids=true | all-gather | bytes 901120 | tf_op jit(solution)/shard_map/all_gather | solution.py:105
  177.6 69.6 %all-gather.5.cloned.1.call-done = bf16[32,44,16,128]{3,2,1,0:T(8,128)(2,1)} async-done(((bf16[4,44,16,128]{3,2,1,0:T(8,128)(2,1)}), bf16[32,44,16,128]{3,2,1,0:T(8,128)(2,1)}) %all-gather.5.cloned.1.call-update) | async-done | bytes 5767184 | tf_op jit(solution)/shard_map/all_gather | solution.py:105
  247.2 1.8 copy_bitcast_fusion.1
  249.0 1.2 slice.57
  251.0 5.6 %gather_fusion.2 = bf16[24,32,16,128]{3,2,1,0:T(8,128)(2,1)} fusion(bf16[32,44,16,128]{3,2,1,0:T(8,128)(2,1)} %all-gather.5.cloned.1.call-done, s32[1024]{0:T(1024)S(1)} %pad_clamp_fusion), kind=kCustom, calls=%fused_computation.2 | custom fusion | bytes 6291552 | tf_op jit(solution)/shard_map/gather | solution.py:111
  256.6 6.7 %convert_bitcast_fusion = bf16[24,128,512]{1,2,0:T(8,128)(2,1)} fusion(bf16[24,128,128]{2,1,0:T(8,128)(2,1)} %param.15, bf16[24,128,512]{2,1,0:T(8,128)(2,1)} %copy-done.1, bf16[24,512,128]{2,1,0:T(8,128)(2,1)} %bitcast.78, bf16[24,128,128]{2,1,0:T(8,128)(2,1)} %param.16), kind=kOutput, calls=%fused_computation.11 | convolution fusion | flops 811597824 | bytes 11010048 | tf_op jit(solution)/shard_map/nij,nir->njr/dot_general | solution.py:16
  263.3 4.6 %copy.102 = bf16[24,128,512]{2,1,0:T(8,128)(2,1)} copy(bf16[24,128,512]{1,2,0:T(8,128)(2,1)} %convert_bitcast_fusion) | data formatting | bytes 6291456
  267.9 2.3 copy.104
  270.2 2.0 copy.105
  (53 shorter events, 17.1 us)
Async XLA Ops:
  7.2 2.0 copy-start
  9.2 2.2 copy-start.2
  11.4 1.7 copy-start.1
  27.3 5.2 %copy-start.6 = (bf16[1,128,128]{2,1,0:T(8,128)(2,1)S(1)}, bf16[1,128,128]{2,1,0:T(8,128)(2,1)}, u32[]{:S(2)}) copy-start(bf16[1,128,128]{2,1,0:T(8,128)(2,1)} %param.20) | copy-start | bytes 98308
  27.3 5.2 %copy-start.7 = (bf16[1,128,128]{2,1,0:T(8,128)(2,1)S(1)}, bf16[1,128,128]{2,1,0:T(8,128)(2,1)}, u32[]{:S(2)}) copy-start(bf16[1,128,128]{2,1,0:T(8,128)(2,1)} %param.19) | copy-start | bytes 98308
  27.3 54.7 %all-to-all-start = ((bf16[8,4,33,16,128]{4,3,0,2,1:T(8,128)(2,1)}), bf16[8,4,33,16,128]{4,3,0,2,1:T(8,128)(2,1)}, u32[]{:S(2)}, u32[]{:S(2)}) async-start(bf16[8,4,33,16,128]{4,3,0,2,1:T(8,128)(2,1)} %bitcast.77), calls=%async_computation | async-start | bytes 8650752 | tf_op jit(solution)/shard_map/all_to_all | solution.py:72
  32.4 108.3 %all-gather.7.cloned.1.call-start = ((), (), s32[]{:S(2)}) async-start(), calls=%async_computation.3 | async-start | bytes 2162688 | tf_op jit(solution)/shard_map/all_gather | solution.py:62
  86.0 13.2 %copy-start.8 = (s32[8]{0:T(128)S(1)}, s32[8]{0:T(128)}, u32[]{:S(2)}) copy-start(s32[8]{0:T(128)} %param.25) | copy-start | bytes 100
  87.2 49.9 %all-to-all-start.1 = ((bf16[8,36,16,128]{3,2,1,0:T(8,128)(2,1)}), bf16[8,36,16,128]{3,2,1,0:T(8,128)(2,1)}, u32[]{:S(2)}, u32[]{:S(2)}) async-start(bf16[8,36,16,128]{3,2,1,0:T(8,128)(2,1)} %copy.89), calls=%async_computation.1 | async-start | bytes 2359296 | tf_op jit(solution)/shard_map/all_to_all | solution.py:75
  97.3 149.9 %all-gather.5.cloned.1.call-start = ((), (), s32[]{:S(2)}) async-start(), calls=%async_computation.2 | async-start | bytes 6488064 | tf_op jit(solution)/shard_map/all_gather | solution.py:105
  99.1 46.6 %copy-start.3 = (bf16[8,128,128]{2,1,0:T(8,128)(2,1)S(1)}, bf16[8,128,128]{2,1,0:T(8,128)(2,1)}, u32[]{:S(2)}) copy-start(bf16[8,128,128]{2,1,0:T(8,128)(2,1)} %param.23) | copy-start | bytes 786436
  140.8 5.2 %copy-start.4 = (bf16[8,128,128]{2,1,0:T(8,128)(2,1)S(1)}, bf16[8,128,128]{2,1,0:T(8,128)(2,1)}, u32[]{:S(2)}) copy-start(bf16[8,128,128]{2,1,0:T(8,128)(2,1)} %param.24) | copy-start | bytes 786436
  140.8 9.6 %copy-start.9 = (s32[8]{0:T(128)S(1)}, s32[8]{0:T(128)}, u32[]{:S(2)}) copy-start(s32[8]{0:T(128)} %compare_select_fusion.2) | copy-start | bytes 100
  146.0 0.6 copy-start.5
  146.7 2.5 collective-permute-start
  149.1 2.9 %collective-permute-start.1 = (f32[4,16,128]{2,0,1:T(4,128)S(1)}, f32[4,16,128]{2,0,1:T(4,128)S(1)}, u32[]{:S(2)}, u32[]{:S(2)}) collective-permute-start(f32[4,16,128]{2,0,1:T(4,128)S(1)} %add.46), channel_id=1, source_target_pairs={{0,64},{32,96},{64,0},{96,32},{128,192},{160,224},{192,128},{224,1... | collective-permute-start | bytes 98312 | tf_op jit(solution)/shard_map/ppermute | solution.py:89
  152.6 4.6 %collective-permute-start.2 = (f32[4,16,128]{2,0,1:T(4,128)}, f32[4,16,128]{2,0,1:T(4,128)}, u32[]{:S(2)}, u32[]{:S(2)}) collective-permute-start(f32[4,16,128]{2,0,1:T(4,128)} %add.47), channel_id=1, source_target_pairs={{0,128},{32,160},{64,192},{96,224},{128,0},{160,32},{192,64},{224,... | collective-permute-start | bytes 98312 | tf_op jit(solution)/shard_map/ppermute | solution.py:89
Sparse Core Ops, SparseCore 0:
  36.4 100.9 all-gather.6
  177.7 69.4 all-gather.4

commit v5 on v4

--- a/solution.py
+++ b/solution.py
@@ -28,6 +28,15 @@
     slots = lax.iota(jnp.int32, count)
     select = (slots[:, None] == targets[None, :]).astype(jnp.float32)
     return jnp.einsum("sk,k...->s...", select, values, precision=lax.Precision.HIGHEST)
+
+
+def split_slot_sums(targets, count, values):
+    slots = lax.iota(jnp.int32, count)
+    select = (slots[:, None] == targets[None, :]).astype(jnp.bfloat16)
+    high = values.astype(jnp.bfloat16)
+    low = (values - high.astype(jnp.float32)).astype(jnp.bfloat16)
+    total = jnp.einsum("sk,k...->s...", select, high, preferred_element_type=jnp.float32)
+    return total + jnp.einsum("sk,k...->s...", select, low, preferred_element_type=jnp.float32)
 
 
 def local(
@@ -65,16 +74,30 @@
 
     leaf_solved = apply_block(leaf_inverse, leaf_rhs).astype(jnp.bfloat16)
     leaf_update = jnp.einsum("kij,kjr->kri", leaf_link, leaf_solved, preferred_element_type=jnp.float32)
-    outgoing = jnp.concatenate(
-        [slot_sums(leaf_target, peers, leaf_update).astype(jnp.bfloat16), node_rhs.transpose(0, 2, 1)], axis=0
-    )
-    outgoing = outgoing.reshape(peers + 1, z_size, y_size, chunk, width).transpose(1, 2, 0, 3, 4)
-    first = lax.all_to_all(outgoing, "y", 1, 1, tiled=True)
-    partial = jnp.sum(first[:, :, :peers].astype(jnp.float32), axis=1).astype(jnp.bfloat16)
-    second = jnp.concatenate([partial, first[:, :, peers]], axis=1)
-    incoming = lax.all_to_all(second, "z", 0, 0, tiled=True)
-    node_sum = jnp.sum(incoming[:, :peers].astype(jnp.float32), axis=0)
-    own_rhs = incoming[:, peers:].reshape(peers, chunk, width)
+    half = peers // 2
+    y_index = lax.axis_index("y")
+    rhs_t = node_rhs.transpose(0, 2, 1)
+    sums = []
+    for group in range(2):
+        targets = leaf_target - group * half
+        entries = split_slot_sums(targets, half, leaf_update).astype(jnp.bfloat16)
+        if group == 1:
+            entries = jnp.concatenate([entries, rhs_t], axis=0)
+        count = entries.shape[0]
+        entries = entries.reshape(count, z_size, y_size, chunk, width).transpose(2, 1, 0, 3, 4)
+        arrivals = [lax.dynamic_index_in_dim(entries, y_index, 0, keepdims=False)]
+        for shift in range(1, y_size):
+            outbound = lax.dynamic_index_in_dim(entries, (y_index + shift) % y_size, 0, keepdims=False)
+            pairs = [(i, (i + shift) % y_size) for i in range(y_size)]
+            arrivals.append(lax.ppermute(outbound, "y", pairs))
+        partial = sum(a[:, :half].astype(jnp.float32) for a in arrivals).astype(jnp.bfloat16)
+        if group == 1:
+            partial = jnp.concatenate([partial, jnp.stack([a[:, half] for a in arrivals], axis=1)], axis=1)
+        incoming = lax.all_to_all(partial, "z", 0, 0, tiled=True)
+        sums.append(jnp.sum(incoming[:, :half].astype(jnp.float32), axis=0))
+    node_sum = jnp.concatenate(sums, axis=0)
+    offsets = (y_index - lax.iota(jnp.int32, y_size)) % y_size
+    own_rhs = jnp.take(incoming[:, half:], offsets, axis=1).reshape(peers, chunk, width)
     node_y = (own_rhs.astype(jnp.float32) - node_sum).astype(jnp.bfloat16)
     node_solved = piece_block(row_inverse, node_y).astype(jnp.bfloat16)
     middle_sum = slot_sums(middle_target, middle_count, piece_block(row_link, node_solved))

time: 282 us -> 255 us (0.904)
  waiting for transfers between devices: 158 us -> 127 us
  starting transfers between devices: 20.7 us -> 30.5 us
  other arithmetic: 12.3 us -> 8.85 us
    all_to_all x2, waiting for transfers between devices: 85.6 us -> 22.9 us  [local(): incoming = lax.all_to_all(partial, 'z', 0, 0, tiled=True)]
    ppermute x0 -> x6, waiting for transfers between devices: none -> 20.5 us  [local(): arrivals.append(lax.ppermute(outbound, 'y', pairs))]
    dot_general x0 -> x4, matrix products: none -> 12.7 us  [the longest x2 6.42 us: split_slot_sums(): jnp.einsum('sk,k...->s...', select, low, preferred_element_type=jnp.float32)]
    dot_general x3 -> x2, matrix products: 11.1 us -> 0.48 us  [slot_sums(): jnp.einsum('sk,k...->s...', select, values, precision=lax.Precision.HIGHEST)]
    ppermute x0 -> x6, starting transfers between devices: none -> 8.61 us  [local(): arrivals.append(lax.ppermute(outbound, 'y', pairs))]
    all_gather x1, waiting for transfers between devices: 0.01 us -> 7.51 us  [local(): lax.all_gather(jnp.concatenate([node_inverse, node_link], axis=0), COL, a...]
    reduce_sum x2, other arithmetic: 5.04 us -> 0.14 us  [local(): sums.append(jnp.sum(incoming[:, :half].astype(jnp.float32), axis=0))]
    dot_general x3, matrix products: 5.47 us -> 1.22 us  [piece_transposed(): jnp.einsum('nij,nci->ncj', matrix, pieces, preferred_element_type=jnp.flo...]
  transfers between devices with their start and end apart: 7 -> 13, of which waited for: 5 -> 9; matrix products, arithmetic and copies ran while one was open for 5% -> 9% of each run, Pallas kernels for 0% -> 0%
where the time goes in v5:
time: 255 us; the launch traced here: 254 us
  waiting for transfers between devices  127 us (50%)
  local copies, waits for them, and re-layouts  33.2 us (13%)
  starting transfers between devices  30.5 us (12%)
  matrix products  28.2 us (11%)
  between operations  14.4 us (6%)
  blocking collectives  11.5 us (5%)
  other arithmetic  8.85 us (3%)
    all_gather x1, waiting for transfers between devices, local(): lax.all_gather(lax.all_gather(parts, 'y', axis=0, tiled=False), 'z', axis...  73.6 us
    all_to_all x2, waiting for transfers between devices, local(): incoming = lax.all_to_all(partial, 'z', 0, 0, tiled=True)  22.9 us
    ppermute x6, waiting for transfers between devices, local(): arrivals.append(lax.ppermute(outbound, 'y', pairs))  20.5 us
    unnamed x46, local copies, waits for them, and re-layouts  17.4 us
    all_to_all x2, starting transfers between devices, local(): incoming = lax.all_to_all(partial, 'z', 0, 0, tiled=True)  14.5 us
    all_gather x1, blocking collectives, local(): lax.all_gather(parts, 'y', axis=0, tiled=False)  11.5 us
    ppermute x6, starting transfers between devices, local(): arrivals.append(lax.ppermute(outbound, 'y', pairs))  8.61 us
    all_gather x1, waiting for transfers between devices, local(): lax.all_gather(jnp.concatenate([node_inverse, node_link], axis=0), COL, a...  7.51 us
  transfers between devices with their start and end apart: 13, of which 9 were waited for; matrix products, arithmetic and copies ran while one was open for 9% of the time, Pallas kernels for 0%

profile of v5, /device:TPU:1, one launch (start us, length us, event | category | flops | bytes accessed | tf_op | source)
XLA Modules:
  0.0 253.9 jit_solution(7839906228729198224)
XLA Ops:
  9.1 2.2 convolution_convert_fusion
  12.9 2.3 fusion.3
  15.2 2.5 add_convert_fusion
  20.1 2.1 collective-permute-start.3
  22.3 2.6 %collective-permute-start.4 = (bf16[8,16,16,128]{3,1,2,0:T(8,128)(2,1)}, bf16[8,16,16,128]{3,1,2,0:T(8,128)(2,1)}, u32[]{:S(2)}, u32[]{:S(2)}) collective-permute-start(bf16[8,16,16,128]{3,1,2,0:T(8,128)(2,1)} %get-tuple-element.39), channel_id=1, source_target_pairs={{0,2},{1,3},{2,0},{3,1},{4,6},{5,7},{6,4},{7,5},{8,10},{9,11},{10,... | collective-permute-start | bytes 1572872 | tf_op jit(solution)/shard_map/ppermute | solution.py:92
  26.6 4.2 %fusion.5 = f32[16,512,128]{2,0,1:T(8,128)S(1)} fusion(bf16[24,512,128]{2,1,0:T(8,128)(2,1)} %copy-done.4, s32[24]{0:T(128)S(1)} %broadcast_add_fusion), kind=kOutput, calls=%fused_computation.14 | convolution fusion | flops 50332032 | bytes 7340128 | tf_op jit(solution)/shard_map/sk,k...->s.../dot_general | solution.py:39
  30.8 3.8 %add_convert_fusion.1 = bf16[16,512,128]{2,0,1:T(8,128)(2,1)} fusion(f32[16,512,128]{2,0,1:T(8,128)S(1)} %fusion.5, bf16[24,512,128]{2,1,0:T(8,128)(2,1)S(1)} %get-tuple-element.32, s32[24]{0:T(128)S(1)} %broadcast_add_fusion), kind=kOutput, calls=%fused_computation.8 | convolution fusion | flops 52429184 | bytes 9437280 | tf_op jit(solution)/shard_map/sk,k...->s.../dot_general | solution.py:38
  34.8 2.3 pad_maximum_fusion
  41.5 1.6 collective-permute-start.2
  43.2 5.0 %collective-permute-done.4 = bf16[8,16,16,128]{3,1,2,0:T(8,128)(2,1)} collective-permute-done((bf16[8,16,16,128]{3,1,2,0:T(8,128)(2,1)}, bf16[8,16,16,128]{3,1,2,0:T(8,128)(2,1)}, u32[]{:S(2)}, u32[]{:S(2)}) %collective-permute-start.4) | collective-permute-done | bytes 524320 | tf_op jit(solution)/shard_map/ppermute | solution.py:92
  48.2 2.1 collective-permute-done.5
  50.3 2.6 %fusion.24 = bf16[8,16,16,128]{3,1,2,0:T(8,128)(2,1)} fusion(bf16[8,16,16,128]{3,1,2,0:T(8,128)(2,1)} %collective-permute-done.5, bf16[8,16,16,128]{3,1,2,0:T(8,128)(2,1)} %collective-permute-done.4, bf16[8,16,16,128]{3,1,2,0:T(8,128)(2,1)} %collective-permute-done.3, bf16[16,8,4,16,128]{4,0,3,2,1:T(8,128)(2,1)} %bitcast.131, s32[]{:T(128)S(6)} %select_n.109), kind=kLoop, calls=%fused_computation.40 | loop fusion | flops 2097152 | bytes 2621444 | tf_op jit(solution)/shard_map/convert_element_type | solution.py:93
  52.9 6.3 %all-to-all-start.1 = ((bf16[8,16,16,128]{3,1,2,0:T(8,128)(2,1)}), bf16[8,16,16,128]{3,1,2,0:T(8,128)(2,1)S(1)}, u32[]{:S(2)}, u32[]{:S(2)}) async-start(bf16[8,16,16,128]{3,1,2,0:T(8,128)(2,1)} %fusion.24), calls=%async_computation.1 | async-start | bytes 1048576 | tf_op jit(solution)/shard_map/all_to_all | solution.py:96
  59.2 3.5 %collective-permute-done = bf16[8,17,16,128]{3,2,1,0:T(8,128)(2,1)S(1)} collective-permute-done((bf16[8,17,16,128]{3,2,1,0:T(8,128)(2,1)}, bf16[8,17,16,128]{3,2,1,0:T(8,128)(2,1)S(1)}, u32[]{:S(2)}, u32[]{:S(2)}) %collective-permute-start) | collective-permute-done | bytes 557088 | tf_op jit(solution)/shard_map/ppermute | solution.py:92
  62.7 9.9 %collective-permute-done.1 = bf16[8,17,16,128]{3,2,1,0:T(8,128)(2,1)S(1)} collective-permute-done((bf16[8,17,16,128]{3,2,1,0:T(8,128)(2,1)}, bf16[8,17,16,128]{3,2,1,0:T(8,128)(2,1)S(1)}, u32[]{:S(2)}, u32[]{:S(2)}) %collective-permute-start.1) | collective-permute-done | bytes 557088 | tf_op jit(solution)/shard_map/ppermute | solution.py:92
  76.2 8.2 %all-to-all-start = ((bf16[8,20,16,128]{3,2,1,0:T(8,128)(2,1)}), bf16[8,20,16,128]{3,2,1,0:T(8,128)(2,1)S(1)}, u32[]{:S(2)}, u32[]{:S(2)}) async-start(bf16[8,20,16,128]{3,2,1,0:T(8,128)(2,1)} %slice_dynamic-update-slice_fusion), calls=%async_computation | async-start | bytes 1310720 | tf_op jit(solution)/shard_map/all_to_all | solution.py:96
  85.9 22.9 %all-to-all-done = bf16[8,20,16,128]{3,2,1,0:T(8,128)(2,1)S(1)} async-done(((bf16[8,20,16,128]{3,2,1,0:T(8,128)(2,1)}), bf16[8,20,16,128]{3,2,1,0:T(8,128)(2,1)S(1)}, u32[]{:S(2)}, u32[]{:S(2)}) %all-to-all-start) | async-done | bytes 655392 | tf_op jit(solution)/shard_map/all_to_all | solution.py:96
  109.6 7.5 %all-gather.7.cloned.1.call-done = bf16[64,128,128]{2,1,0:T(8,128)(2,1)} async-done(((bf16[2,128,128]{2,1,0:T(8,128)(2,1)}), bf16[64,128,128]{2,1,0:T(8,128)(2,1)}) %all-gather.7.cloned.1.call-update) | async-done | bytes 2097168 | tf_op jit(solution)/shard_map/all_gather | solution.py:71
  117.2 2.0 convolution_convert_fusion.2
  119.2 1.9 fusion.25
  122.0 2.7 %collective-permute-start.6 = (f32[4,16,128]{2,0,1:T(4,128)S(1)}, f32[4,16,128]{2,0,1:T(4,128)S(1)}, u32[]{:S(2)}, u32[]{:S(2)}) collective-permute-start(f32[4,16,128]{2,0,1:T(4,128)S(1)} %fusion.31), channel_id=1, source_target_pairs={{0,32},{32,0},{64,96},{96,64},{128,160},{160,128},{192,224},{224,1... | collective-permute-start | bytes 98312 | tf_op jit(solution)/shard_map/ppermute | solution.py:112
  125.8 1.6 collective-permute-start.7
  127.4 1.5 collective-permute-done.7
  128.9 3.0 %collective-permute-start.8 = (f32[4,16,128]{2,0,1:T(4,128)S(1)}, f32[4,16,128]{2,0,1:T(4,128)S(1)}, u32[]{:S(2)}, u32[]{:S(2)}) collective-permute-start(f32[4,16,128]{2,0,1:T(4,128)S(1)} %add.169), channel_id=1, source_target_pairs={{0,128},{32,160},{64,192},{96,224},{128,0},{160,32},{192,64},{224,... | collective-permute-start | bytes 98312 | tf_op jit(solution)/shard_map/ppermute | solution.py:112
  135.8 11.5 %all-gather.1 = bf16[176,16,128]{2,1,0:T(8,128)(2,1)} all-gather(bf16[44,16,128]{2,1,0:T(8,128)(2,1)S(1)} %pad_maximum_fusion.1), channel_id=3, replica_groups=mesh['x'=4,'core'=2,'z'=8,'y'=4] {'y'}, dimensions={0}, use_global_device_ids=true | all-gather | bytes 901120 | tf_op jit(solution)/shard_map/all_gather | solution.py:128
  147.3 73.6 %all-gather.5.cloned.1.call-done = bf16[32,44,16,128]{3,2,1,0:T(8,128)(2,1)} async-done(((bf16[4,44,16,128]{3,2,1,0:T(8,128)(2,1)}), bf16[32,44,16,128]{3,2,1,0:T(8,128)(2,1)}) %all-gather.5.cloned.1.call-update) | async-done | bytes 5767184 | tf_op jit(solution)/shard_map/all_gather | solution.py:128
  220.9 1.8 copy_bitcast_fusion
  224.7 5.7 %gather_fusion.3 = bf16[24,32,16,128]{3,2,1,0:T(8,128)(2,1)} fusion(bf16[32,44,16,128]{3,2,1,0:T(8,128)(2,1)} %all-gather.5.cloned.1.call-done, s32[1024]{0:T(1024)S(1)} %pad_clamp_fusion), kind=kCustom, calls=%fused_computation.3 | custom fusion | bytes 6291552 | tf_op jit(solution)/shard_map/gather | solution.py:134
  230.5 5.8 %convert_bitcast_fusion = bf16[24,128,512]{1,2,0:T(8,128)(2,1)} fusion(bf16[24,128,128]{2,1,0:T(8,128)(2,1)} %param.15, bf16[24,128,512]{2,1,0:T(8,128)(2,1)S(1)} %copy-done.3, bf16[24,512,128]{2,1,0:T(8,128)(2,1)} %bitcast.129, bf16[24,128,128]{2,1,0:T(8,128)(2,1)} %param.16), kind=kOutput, calls=%fused_computation.11 | convolution fusion | flops 811597824 | bytes 11010048 | tf_op jit(solution)/shard_map/nij,nir->njr/dot_general | solution.py:16
  236.3 4.8 %copy.183 = bf16[24,128,512]{2,1,0:T(8,128)(2,1)} copy(bf16[24,128,512]{1,2,0:T(8,128)(2,1)} %convert_bitcast_fusion) | data formatting | bytes 6291456
  241.0 2.3 copy.185
  243.3 2.0 copy.186
  (98 shorter events, 27.8 us)
Async XLA Ops:
  7.2 1.9 copy-start
  7.2 110.0 %all-gather.7.cloned.1.call-start = ((), (), s32[]{:S(2)}) async-start(), calls=%async_computation.3 | async-start | bytes 2162688 | tf_op jit(solution)/shard_map/all_gather | solution.py:71
  9.1 2.2 copy-start.7
  11.3 1.7 copy-start.2
  12.9 2.3 copy-start.4
  17.6 1.3 copy-start.5
  17.7 8.3 %copy-start.12 = (bf16[1,128,128]{2,1,0:T(8,128)(2,1)S(1)}, bf16[1,128,128]{2,1,0:T(8,128)(2,1)}, u32[]{:S(2)}) copy-start(bf16[1,128,128]{2,1,0:T(8,128)(2,1)} %param.20) | copy-start | bytes 98308
  17.7 8.3 %copy-start.13 = (bf16[1,128,128]{2,1,0:T(8,128)(2,1)S(1)}, bf16[1,128,128]{2,1,0:T(8,128)(2,1)}, u32[]{:S(2)}) copy-start(bf16[1,128,128]{2,1,0:T(8,128)(2,1)} %param.19) | copy-start | bytes 98308
  20.1 21.4 %collective-permute-start.3 = (bf16[8,16,16,128]{3,1,2,0:T(8,128)(2,1)}, bf16[8,16,16,128]{3,1,2,0:T(8,128)(2,1)}, u32[]{:S(2)}, u32[]{:S(2)}) collective-permute-start(bf16[8,16,16,128]{3,1,2,0:T(8,128)(2,1)} %get-tuple-element.38), channel_id=1, source_target_pairs={{0,1},{1,2},{2,3},{3,0},{4,5},{5,6},{6,7},{7,4},{8,9},{9,10},{10,1... | collective-permute-start | bytes 1572872 | tf_op jit(solution)/shard_map/ppermute | solution.py:92
  22.3 25.9 %collective-permute-start.4 = (bf16[8,16,16,128]{3,1,2,0:T(8,128)(2,1)}, bf16[8,16,16,128]{3,1,2,0:T(8,128)(2,1)}, u32[]{:S(2)}, u32[]{:S(2)}) collective-permute-start(bf16[8,16,16,128]{3,1,2,0:T(8,128)(2,1)} %get-tuple-element.39), channel_id=1, source_target_pairs={{0,2},{1,3},{2,0},{3,1},{4,6},{5,7},{6,4},{7,5},{8,10},{9,11},{10,... | collective-permute-start | bytes 1572872 | tf_op jit(solution)/shard_map/ppermute | solution.py:92
  24.9 25.4 %collective-permute-start.5 = (bf16[8,16,16,128]{3,1,2,0:T(8,128)(2,1)}, bf16[8,16,16,128]{3,1,2,0:T(8,128)(2,1)}, u32[]{:S(2)}, u32[]{:S(2)}) collective-permute-start(bf16[8,16,16,128]{3,1,2,0:T(8,128)(2,1)} %get-tuple-element.40), channel_id=1, source_target_pairs={{0,3},{1,0},{2,1},{3,2},{4,7},{5,4},{6,5},{7,6},{8,11},{9,8},{10,9... | collective-permute-start | bytes 1572872 | tf_op jit(solution)/shard_map/ppermute | solution.py:92
  30.8 3.8 %copy-start.11 = (bf16[1,128,512]{2,1,0:T(8,128)(2,1)S(1)}, bf16[1,128,512]{2,1,0:T(8,128)(2,1)}, u32[]{:S(2)}) copy-start(bf16[1,128,512]{2,1,0:T(8,128)(2,1)} %param.18) | copy-start | bytes 393220
  38.6 24.1 %collective-permute-start = (bf16[8,17,16,128]{3,2,1,0:T(8,128)(2,1)}, bf16[8,17,16,128]{3,2,1,0:T(8,128)(2,1)S(1)}, u32[]{:S(2)}, u32[]{:S(2)}) collective-permute-start(bf16[8,17,16,128]{3,2,1,0:T(8,128)(2,1)} %bitcast.126), channel_id=1, source_target_pairs={{0,1},{1,2},{2,3},{3,0},{4,5},{5,6},{6,7},{7,4},{8,9},{9,10},{10,1... | collective-permute-start | bytes 1671176 | tf_op jit(solution)/shard_map/ppermute | solution.py:92
  39.9 32.8 %collective-permute-start.1 = (bf16[8,17,16,128]{3,2,1,0:T(8,128)(2,1)}, bf16[8,17,16,128]{3,2,1,0:T(8,128)(2,1)S(1)}, u32[]{:S(2)}, u32[]{:S(2)}) collective-permute-start(bf16[8,17,16,128]{3,2,1,0:T(8,128)(2,1)} %bitcast.125), channel_id=1, source_target_pairs={{0,2},{1,3},{2,0},{3,1},{4,6},{5,7},{6,4},{7,5},{8,10},{9,11},{10,... | collective-permute-start | bytes 1671176 | tf_op jit(solution)/shard_map/ppermute | solution.py:92
  41.5 31.1 %collective-permute-start.2 = (bf16[8,17,16,128]{3,2,1,0:T(8,128)(2,1)}, bf16[8,17,16,128]{3,2,1,0:T(8,128)(2,1)S(1)}, u32[]{:S(2)}, u32[]{:S(2)}) collective-permute-start(bf16[8,17,16,128]{3,2,1,0:T(8,128)(2,1)} %bitcast.124), channel_id=1, source_target_pairs={{0,3},{1,0},{2,1},{3,2},{4,7},{5,4},{6,5},{7,6},{8,11},{9,8},{10,9... | collective-permute-start | bytes 1671176 | tf_op jit(solution)/shard_map/ppermute | solution.py:92
  52.9 32.9 %copy-start.14 = (s32[8]{0:T(128)S(1)}, s32[8]{0:T(128)}, u32[]{:S(2)}) copy-start(s32[8]{0:T(128)} %param.25) | copy-start | bytes 100
  52.9 32.9 %copy-start.15 = (s32[32]{0:T(128)S(1)}, s32[32]{0:T(128)}, u32[]{:S(2)}) copy-start(s32[32]{0:T(128)} %param.21) | copy-start | bytes 388
  52.9 23.3 %all-to-all-start.1 = ((bf16[8,16,16,128]{3,1,2,0:T(8,128)(2,1)}), bf16[8,16,16,128]{3,1,2,0:T(8,128)(2,1)S(1)}, u32[]{:S(2)}, u32[]{:S(2)}) async-start(bf16[8,16,16,128]{3,1,2,0:T(8,128)(2,1)} %fusion.24), calls=%async_computation.1 | async-start | bytes 1048576 | tf_op jit(solution)/shard_map/all_to_all | solution.py:96
  76.2 32.6 %all-to-all-start = ((bf16[8,20,16,128]{3,2,1,0:T(8,128)(2,1)}), bf16[8,20,16,128]{3,2,1,0:T(8,128)(2,1)S(1)}, u32[]{:S(2)}, u32[]{:S(2)}) async-start(bf16[8,20,16,128]{3,2,1,0:T(8,128)(2,1)} %slice_dynamic-update-slice_fusion), calls=%async_computation | async-start | bytes 1310720 | tf_op jit(solution)/shard_map/all_to_all | solution.py:96
  84.3 136.6 %all-gather.5.cloned.1.call-start = ((), (), s32[]{:S(2)}) async-start(), calls=%async_computation.2 | async-start | bytes 6488064 | tf_op jit(solution)/shard_map/all_gather | solution.py:128
  85.6 35.8 %copy-start.8 = (bf16[8,128,128]{2,1,0:T(8,128)(2,1)S(1)}, bf16[8,128,128]{2,1,0:T(8,128)(2,1)}, u32[]{:S(2)}) copy-start(bf16[8,128,128]{2,1,0:T(8,128)(2,1)} %param.23) | copy-start | bytes 786436
  85.8 35.8 %copy-start.9 = (bf16[8,128,128]{2,1,0:T(8,128)(2,1)S(1)}, bf16[8,128,128]{2,1,0:T(8,128)(2,1)}, u32[]{:S(2)}) copy-start(bf16[8,128,128]{2,1,0:T(8,128)(2,1)} %param.24) | copy-start | bytes 786436
  109.4 23.9 %copy-start.10 = (bf16[4,128,128]{2,1,0:T(8,128)(2,1)S(1)}, bf16[4,128,128]{2,1,0:T(8,128)(2,1)}, u32[]{:S(2)}) copy-start(bf16[4,128,128]{2,1,0:T(8,128)(2,1)} %param.27) | copy-start | bytes 393220
  117.2 17.9 %copy-start.6 = (bf16[64,128,128]{2,1,0:T(8,128)(2,1)S(1)}, bf16[64,128,128]{2,1,0:T(8,128)(2,1)}, u32[]{:S(2)}) copy-start(bf16[64,128,128]{2,1,0:T(8,128)(2,1)} %all-gather.7.cloned.1.call-done) | copy-start | bytes 6291460
  122.0 3.8 %collective-permute-start.6 = (f32[4,16,128]{2,0,1:T(4,128)S(1)}, f32[4,16,128]{2,0,1:T(4,128)S(1)}, u32[]{:S(2)}, u32[]{:S(2)}) collective-permute-start(f32[4,16,128]{2,0,1:T(4,128)S(1)} %fusion.31), channel_id=1, source_target_pairs={{0,32},{32,0},{64,96},{96,64},{128,160},{160,128},{192,224},{224,1... | collective-permute-start | bytes 98312 | tf_op jit(solution)/shard_map/ppermute | solution.py:112
  125.8 3.1 %collective-permute-start.7 = (f32[4,16,128]{2,0,1:T(4,128)S(1)}, f32[4,16,128]{2,0,1:T(4,128)S(1)}, u32[]{:S(2)}, u32[]{:S(2)}) collective-permute-start(f32[4,16,128]{2,0,1:T(4,128)S(1)} %add.168), channel_id=1, source_target_pairs={{0,64},{32,96},{64,0},{96,32},{128,192},{160,224},{192,128},{224,1... | collective-permute-start | bytes 98312 | tf_op jit(solution)/shard_map/ppermute | solution.py:112
  128.9 4.4 %collective-permute-start.8 = (f32[4,16,128]{2,0,1:T(4,128)S(1)}, f32[4,16,128]{2,0,1:T(4,128)S(1)}, u32[]{:S(2)}, u32[]{:S(2)}) collective-permute-start(f32[4,16,128]{2,0,1:T(4,128)S(1)} %add.169), channel_id=1, source_target_pairs={{0,128},{32,160},{64,192},{96,224},{128,0},{160,32},{192,64},{224,... | collective-permute-start | bytes 98312 | tf_op jit(solution)/shard_map/ppermute | solution.py:112
  224.7 5.7 %copy-start.3 = (bf16[24,128,512]{2,1,0:T(8,128)(2,1)S(1)}, bf16[24,128,512]{2,1,0:T(8,128)(2,1)}, u32[]{:S(2)}) copy-start(bf16[24,128,512]{2,1,0:T(8,128)(2,1)} %copy-done.2) | copy-start | bytes 9437188
  236.3 10.8 %copy-start.1 = (bf16[24,128,512]{2,1,0:T(8,128)(2,1)S(1)}, bf16[24,128,512]{2,1,0:T(8,128)(2,1)}, u32[]{:S(2)}) copy-start(bf16[24,128,512]{2,1,0:T(8,128)(2,1)} %param.14) | copy-start | bytes 9437188
Sparse Core Ops, SparseCore 0:
  26.7 90.3 all-gather.6
  147.4 73.4 all-gather.4

commit v6 on v5

--- a/solution.py
+++ b/solution.py
@@ -1,6 +1,8 @@
 import jax
 import jax.numpy as jnp
 from jax import lax
+from jax.experimental import pallas as pl
+from jax.experimental.pallas import tpu as pltpu
 from jax.sharding import Mesh
 from jax.sharding import PartitionSpec as P
 
@@ -37,6 +39,52 @@
     low = (values - high.astype(jnp.float32)).astype(jnp.bfloat16)
     total = jnp.einsum("sk,k...->s...", select, high, preferred_element_type=jnp.float32)
     return total + jnp.einsum("sk,k...->s...", select, low, preferred_element_type=jnp.float32)
+
+
+def leaf_backward_kernel(parent_ref, pieces_ref, solved_ref, link_t_ref, inverse_t_ref, out_ref):
+    pieces = pieces_ref[...]
+    parent_t = pieces.reshape(pieces.shape[0] * pieces.shape[1], pieces.shape[2])
+    correction = lax.dot_general(
+        link_t_ref[...], parent_t, (((1,), (1,)), ((), ())), preferred_element_type=jnp.float32
+    )
+    w = (solved_ref[...].astype(jnp.float32) - correction).astype(jnp.bfloat16)
+    out_ref[...] = jnp.dot(inverse_t_ref[...], w, preferred_element_type=jnp.float32).astype(out_ref.dtype)
+
+
+def leaf_backward(targets, gathered, leaf_solved, leaf_link, leaf_inverse):
+    count, width, columns = leaf_solved.shape
+    peers, _, chunk, _ = gathered.shape
+    link_t = leaf_link.transpose(0, 2, 1)
+    inverse_t = leaf_inverse.transpose(0, 2, 1)
+
+    def own(k, parent):
+        return (k, 0, 0)
+
+    def parent_pieces(k, parent):
+        return (0, parent[k], 0, 0)
+
+    grid_spec = pltpu.PrefetchScalarGridSpec(
+        num_scalar_prefetch=1,
+        grid=(count,),
+        in_specs=[
+            pl.BlockSpec((peers, None, chunk, width), parent_pieces),
+            pl.BlockSpec((None, width, columns), own),
+            pl.BlockSpec((None, width, width), own),
+            pl.BlockSpec((None, width, width), own),
+        ],
+        out_specs=pl.BlockSpec((None, width, columns), own),
+    )
+    cost = pl.CostEstimate(
+        flops=4 * count * width * width * columns,
+        transcendentals=0,
+        bytes_accessed=2 * count * (3 * width * columns + 2 * width * width),
+    )
+    return pl.pallas_call(
+        leaf_backward_kernel,
+        grid_spec=grid_spec,
+        out_shape=jax.ShapeDtypeStruct(leaf_solved.shape, jnp.bfloat16),
+        cost_estimate=cost,
+    )(targets, gathered, leaf_solved, link_t, inverse_t)
 
 
 def local(
@@ -131,10 +179,7 @@
     top_result = upper[middle_count:]
     node_result = lax.dynamic_index_in_dim(gathered, col_index, 1).transpose(1, 3, 0, 2).reshape(1, width, columns)
 
-    parent_t = gathered[:, leaf_target].transpose(1, 0, 2, 3).reshape(leaf_target.shape[0], columns, width)
-    correction = jnp.einsum("kij,kci->kjc", leaf_link, parent_t, preferred_element_type=jnp.float32)
-    leaf_w = (leaf_solved.astype(jnp.float32) - correction).astype(jnp.bfloat16)
-    leaf_result = apply_transposed(leaf_inverse, leaf_w).astype(jnp.bfloat16)
+    leaf_result = leaf_backward(leaf_target, gathered, leaf_solved, leaf_link, leaf_inverse)
     return (leaf_result, node_result, middle_result, top_result)
 
 

time: 255 us -> 266 us (1.043)
  waiting for transfers between devices: 127 us -> 101 us
  Pallas kernels: 0 us -> 18.9 us
  other arithmetic: 8.85 us -> 20.1 us
  local copies, waits for them, and re-layouts: 33.2 us -> 38.9 us
    pallas_call x0 -> x1, Pallas kernels: none -> 18.9 us  [leaf_backward(): pl.pallas_call(leaf_backward_kernel, grid_spec=grid_spec, out_shape=jax.S...]
    all_gather x1, waiting for transfers between devices: 73.6 us -> 64.5 us  [local(): lax.all_gather(lax.all_gather(parts, 'y', axis=0, tiled=False), 'z', axis...]
    all_gather x1, waiting for transfers between devices: 7.51 us -> 0.01 us  [local(): lax.all_gather(jnp.concatenate([node_inverse, node_link], axis=0), COL, a...]
    ppermute x6, waiting for transfers between devices: 20.5 us -> 13.8 us  [local(): arrivals.append(lax.ppermute(outbound, 'y', pairs))]
    dot_general x1 -> x0, matrix products: 5.81 us -> none  [apply_transposed(): jnp.einsum('nij,nir->njr', matrix, vectors, preferred_element_type=jnp.fl...]
    gather x1 -> x0, local copies, waits for them, and re-layouts: 5.73 us -> none  [local(): gathered[:, leaf_target].transpose(1, 0, 2, 3)]
    unnamed x46 -> x45, local copies, waits for them, and re-layouts: 17.4 us -> 22.1 us
    dot_general x3, matrix products: 1.22 us -> 5.47 us  [piece_transposed(): jnp.einsum('nij,nci->ncj', matrix, pieces, preferred_element_type=jnp.flo...]
  transfers between devices with their start and end apart: 13 -> 13, of which waited for: 9 -> 7; matrix products, arithmetic and copies ran while one was open for 9% -> 18% of each run, Pallas kernels for 0% -> 0%
where the time goes in v6:
time: 266 us; the launch traced here: 265 us
  waiting for transfers between devices  101 us (38%)
  local copies, waits for them, and re-layouts  38.9 us (15%)
  starting transfers between devices  32.3 us (12%)
  matrix products  27.6 us (10%)
  other arithmetic  20.1 us (8%)
  Pallas kernels  18.9 us (7%)
  between operations  14.3 us (5%)
  blocking collectives  12 us (5%)
    all_gather x1, waiting for transfers between devices, local(): lax.all_gather(lax.all_gather(parts, 'y', axis=0, tiled=False), 'z', axis...  64.5 us
    unnamed x45, local copies, waits for them, and re-layouts  22.1 us
    all_to_all x2, waiting for transfers between devices, local(): incoming = lax.all_to_all(partial, 'z', 0, 0, tiled=True)  20.9 us
    pallas_call x1, Pallas kernels, leaf_backward(): pl.pallas_call(leaf_backward_kernel, grid_spec=grid_spec, out_shape=jax.S...  18.9 us
    all_to_all x2, starting transfers between devices, local(): incoming = lax.all_to_all(partial, 'z', 0, 0, tiled=True)  16.8 us
    ppermute x6, waiting for transfers between devices, local(): arrivals.append(lax.ppermute(outbound, 'y', pairs))  13.8 us
    all_gather x1, blocking collectives, local(): lax.all_gather(parts, 'y', axis=0, tiled=False)  12 us
    ppermute x6, starting transfers between devices, local(): arrivals.append(lax.ppermute(outbound, 'y', pairs))  8.58 us
  transfers between devices with their start and end apart: 13, of which 7 were waited for; matrix products, arithmetic and copies ran while one was open for 18% of the time, Pallas kernels for 0%

profile of v6, /device:TPU:1, one launch (start us, length us, event | category | flops | bytes accessed | tf_op | source)
XLA Modules:
  0.0 264.6 jit_solution(17495535974773809575)
XLA Ops:
  9.1 2.2 convolution_convert_fusion.solved_ref
  13.0 2.3 fusion
  15.6 2.5 add_convert_fusion
  20.7 2.1 collective-permute-start.3
  22.8 2.6 collective-permute-start.4
  27.2 4.3 %fusion.2 = f32[16,512,128]{2,0,1:T(8,128)S(1)} fusion(bf16[24,512,128]{2,1,0:T(8,128)(2,1)} %copy-done.4, s32[24]{0:T(128)S(1)} %get-tuple-element.26), kind=kOutput, calls=%fused_computation.9 | convolution fusion | flops 50332032 | bytes 7340128 | tf_op jit(solution)/shard_map/sk,k...->s.../dot_general | solution.py:41
  31.5 3.8 %add_convert_fusion.1 = bf16[16,512,128]{2,0,1:T(8,128)(2,1)} fusion(f32[16,512,128]{2,0,1:T(8,128)S(1)} %fusion.2, bf16[24,512,128]{2,1,0:T(8,128)(2,1)S(1)} %copy-done.3, s32[24]{0:T(128)S(1)} %get-tuple-element.26), kind=kOutput, calls=%fused_computation.5 | convolution fusion | flops 52429184 | bytes 9437280 | tf_op jit(solution)/shard_map/sk,k...->s.../dot_general | solution.py:40
  35.5 4.0 %pad_maximum_fusion = bf16[17,512,128]{2,0,1:T(8,128)(2,1)} fusion(bf16[1,512,128]{2,0,1:T(2,128)(2,1)S(1)} %bitcast.128, bf16[16,512,128]{2,0,1:T(8,128)(2,1)} %add_convert_fusion.1), kind=kLoop, calls=%fused_computation.6 | loop fusion | flops 4456448 | bytes 4456448 | tf_op jit(solution)/shard_map/concatenate | solution.py:133
  39.5 2.4 constant_dynamic-slice_fusion.5
  45.8 1.6 collective-permute-start.2
  48.7 2.6 fusion.17
  51.3 8.6 %all-to-all-start.1 = ((bf16[8,16,16,128]{3,1,2,0:T(8,128)(2,1)}), bf16[8,16,16,128]{3,1,2,0:T(8,128)(2,1)}, u32[]{:S(2)}, u32[]{:S(2)}) async-start(bf16[8,16,16,128]{3,1,2,0:T(8,128)(2,1)} %fusion.17), calls=%async_computation.1 | async-start | bytes 1048576 | tf_op jit(solution)/shard_map/all_to_all | solution.py:144
  59.9 3.4 %collective-permute-done = bf16[8,17,16,128]{3,2,1,0:T(8,128)(2,1)} collective-permute-done((bf16[8,17,16,128]{3,2,1,0:T(8,128)(2,1)}, bf16[8,17,16,128]{3,2,1,0:T(8,128)(2,1)}, u32[]{:S(2)}, u32[]{:S(2)}) %collective-permute-start) | collective-permute-done | bytes 557088 | tf_op jit(solution)/shard_map/ppermute | solution.py:140
  63.4 9.9 %collective-permute-done.1 = bf16[8,17,16,128]{3,2,1,0:T(8,128)(2,1)} collective-permute-done((bf16[8,17,16,128]{3,2,1,0:T(8,128)(2,1)}, bf16[8,17,16,128]{3,2,1,0:T(8,128)(2,1)}, u32[]{:S(2)}, u32[]{:S(2)}) %collective-permute-start.1) | collective-permute-done | bytes 557088 | tf_op jit(solution)/shard_map/ppermute | solution.py:140
  73.3 2.6 fusion.19
  81.4 8.2 %all-to-all-start = ((bf16[8,20,16,128]{3,2,1,0:T(8,128)(2,1)}), bf16[8,20,16,128]{3,2,1,0:T(8,128)(2,1)}, u32[]{:S(2)}, u32[]{:S(2)}) async-start(bf16[8,20,16,128]{3,2,1,0:T(8,128)(2,1)} %slice_dynamic-update-slice_fusion), calls=%async_computation | async-start | bytes 1310720 | tf_op jit(solution)/shard_map/all_to_all | solution.py:144
  94.5 20.9 %all-to-all-done = bf16[8,20,16,128]{3,2,1,0:T(8,128)(2,1)} async-done(((bf16[8,20,16,128]{3,2,1,0:T(8,128)(2,1)}), bf16[8,20,16,128]{3,2,1,0:T(8,128)(2,1)}, u32[]{:S(2)}, u32[]{:S(2)}) %all-to-all-start) | async-done | bytes 655392 | tf_op jit(solution)/shard_map/all_to_all | solution.py:144
  117.0 2.1 gather_fusion
  122.0 2.0 convolution_convert_fusion.2
  124.0 1.9 fusion.18
  127.8 2.4 collective-permute-start.6
  131.3 1.6 collective-permute-start.7
  135.0 2.8 %collective-permute-start.8 = (f32[4,16,128]{2,0,1:T(4,128)}, f32[4,16,128]{2,0,1:T(4,128)}, u32[]{:S(2)}, u32[]{:S(2)}) collective-permute-start(f32[4,16,128]{2,0,1:T(4,128)} %add.166), channel_id=1, source_target_pairs={{0,128},{32,160},{64,192},{96,224},{128,0},{160,32},{192,64},{224,... | collective-permute-start | bytes 98312 | tf_op jit(solution)/shard_map/ppermute | solution.py:160
  144.2 2.9 %convolution_convert_fusion.1 = bf16[32,16,128]{2,1,0:T(8,128)(2,1)} fusion(bf16[32,16,128]{2,1,0:T(8,128)(2,1)S(1)} %gather_fusion.2, bf16[32,2,128,128]{3,2,1,0:T(8,128)(2,1)} %bitcast.120, bf16[32,16,128]{2,1,0:T(8,128)(2,1)S(1)} %convolution_convert_fusion.2), kind=kOutput, calls=%fused_computation.18 | convolution fusion | flops 33816576 | bytes 2490368 | tf_op jit(solution)/shard_map/nij,nci->ncj/dot_general | solution.py:26
  148.0 12.0 %all-gather.1 = bf16[176,16,128]{2,1,0:T(8,128)(2,1)} all-gather(bf16[44,16,128]{2,1,0:T(8,128)(2,1)S(1)} %pad_maximum_fusion.1), channel_id=3, replica_groups=mesh['x'=4,'core'=2,'z'=8,'y'=4] {'y'}, dimensions={0}, use_global_device_ids=true | all-gather | bytes 901120 | tf_op jit(solution)/shard_map/all_gather | solution.py:176
  160.0 2.3 copy.145
  162.3 2.3 copy.146
  164.6 64.5 %all-gather.5.cloned.1.call-done.pieces_ref = bf16[32,44,16,128]{3,2,1,0:T(8,128)(2,1)} async-done(((bf16[4,44,16,128]{3,2,1,0:T(8,128)(2,1)}), bf16[32,44,16,128]{3,2,1,0:T(8,128)(2,1)}) %all-gather.5.cloned.1.call-update) | async-done | bytes 5767184 | tf_op jit(solution)/shard_map/all_gather | solution.py:176
  229.1 1.8 copy_bitcast_fusion
  232.9 2.3 copy.149
  235.2 2.0 copy.150
  238.9 18.9 %shard_map.165 = bf16[24,128,512]{2,1,0:T(8,128)(2,1)} custom-call(s32[24]{0:T(128)} %copy-done.13, bf16[32,44,16,128]{3,2,1,0:T(8,128)(2,1)} %all-gather.5.cloned.1.call-done.pieces_ref, bf16[24,128,512]{2,1,0:T(8,128)(2,1)} %copy-done.1, bf16[24,128,128]{2,1,0:T(8,128)(2,1)} %bitcast.122, bf16[24,128,128]{2,1,0:T(8,128)(2,1)} %bitcast.123), custom_call_target="tpu_custom_call" | custom-call | flops 805306368 | bytes 11010048 | tf_op jit(solution)/shard_map/pallas_call | solution.py:82
  (94 shorter events, 44.4 us)
Async XLA Ops:
  7.2 1.9 copy-start
  7.2 114.8 %all-gather.7.cloned.1.call-start = ((), (), s32[]{:S(2)}) async-start(), calls=%async_computation.3 | async-start | bytes 2162688 | tf_op jit(solution)/shard_map/all_gather | solution.py:119
  8.1 7.1 %copy-start.13 = (s32[24]{0:T(128)}, s32[24]{0:T(128)S(1)}, u32[]{:S(2)}) copy-start(s32[24]{0:T(128)S(1)} %get-tuple-element.27.parent_ref) | copy-start | bytes 292
  9.1 2.2 copy-start.6
  11.3 1.7 copy-start.1
  13.0 2.3 copy-start.4
  13.0 2.7 %copy-start.2 = (bf16[24,512,128]{2,1,0:T(8,128)(2,1)}, bf16[24,512,128]{2,1,0:T(8,128)(2,1)S(1)}, u32[]{:S(2)}) copy-start(bf16[24,512,128]{2,1,0:T(8,128)(2,1)S(1)} %get-tuple-element.28) | copy-start | bytes 9437188
  18.2 1.3 copy-start.5
  18.2 8.4 %copy-start.11 = (bf16[1,128,128]{2,1,0:T(8,128)(2,1)S(1)}, bf16[1,128,128]{2,1,0:T(8,128)(2,1)}, u32[]{:S(2)}) copy-start(bf16[1,128,128]{2,1,0:T(8,128)(2,1)} %param.20) | copy-start | bytes 98308
  18.2 8.3 %copy-start.12 = (bf16[1,128,128]{2,1,0:T(8,128)(2,1)S(1)}, bf16[1,128,128]{2,1,0:T(8,128)(2,1)}, u32[]{:S(2)}) copy-start(bf16[1,128,128]{2,1,0:T(8,128)(2,1)} %param.19) | copy-start | bytes 98308
  20.7 25.1 %collective-permute-start.3 = (bf16[8,16,16,128]{3,1,2,0:T(8,128)(2,1)}, bf16[8,16,16,128]{3,1,2,0:T(8,128)(2,1)}, u32[]{:S(2)}, u32[]{:S(2)}) collective-permute-start(bf16[8,16,16,128]{3,1,2,0:T(8,128)(2,1)} %get-tuple-element.34), channel_id=1, source_target_pairs={{0,1},{1,2},{2,3},{3,0},{4,5},{5,6},{6,7},{7,4},{8,9},{9,10},{10,1... | collective-permute-start | bytes 1572872 | tf_op jit(solution)/shard_map/ppermute | solution.py:140
  22.8 25.9 %collective-permute-start.4 = (bf16[8,16,16,128]{3,1,2,0:T(8,128)(2,1)}, bf16[8,16,16,128]{3,1,2,0:T(8,128)(2,1)}, u32[]{:S(2)}, u32[]{:S(2)}) collective-permute-start(bf16[8,16,16,128]{3,1,2,0:T(8,128)(2,1)} %get-tuple-element.35), channel_id=1, source_target_pairs={{0,2},{1,3},{2,0},{3,1},{4,6},{5,7},{6,4},{7,5},{8,10},{9,11},{10,... | collective-permute-start | bytes 1572872 | tf_op jit(solution)/shard_map/ppermute | solution.py:140
  25.5 23.3 %collective-permute-start.5 = (bf16[8,16,16,128]{3,1,2,0:T(8,128)(2,1)}, bf16[8,16,16,128]{3,1,2,0:T(8,128)(2,1)}, u32[]{:S(2)}, u32[]{:S(2)}) collective-permute-start(bf16[8,16,16,128]{3,1,2,0:T(8,128)(2,1)} %get-tuple-element.36), channel_id=1, source_target_pairs={{0,3},{1,0},{2,1},{3,2},{4,7},{5,4},{6,5},{7,6},{8,11},{9,8},{10,9... | collective-permute-start | bytes 1572872 | tf_op jit(solution)/shard_map/ppermute | solution.py:140
  27.2 4.3 %copy-start.3 = (bf16[24,512,128]{2,1,0:T(8,128)(2,1)S(1)}, bf16[24,512,128]{2,1,0:T(8,128)(2,1)}, u32[]{:S(2)}) copy-start(bf16[24,512,128]{2,1,0:T(8,128)(2,1)} %copy-done.2) | copy-start | bytes 9437188
  31.5 3.8 %copy-start.10 = (bf16[1,128,512]{2,1,0:T(8,128)(2,1)S(1)}, bf16[1,128,512]{2,1,0:T(8,128)(2,1)}, u32[]{:S(2)}) copy-start(bf16[1,128,512]{2,1,0:T(8,128)(2,1)} %param.18) | copy-start | bytes 393220
  42.9 20.5 %collective-permute-start = (bf16[8,17,16,128]{3,2,1,0:T(8,128)(2,1)}, bf16[8,17,16,128]{3,2,1,0:T(8,128)(2,1)}, u32[]{:S(2)}, u32[]{:S(2)}) collective-permute-start(bf16[8,17,16,128]{3,2,1,0:T(8,128)(2,1)} %bitcast.113), channel_id=1, source_target_pairs={{0,1},{1,2},{2,3},{3,0},{4,5},{5,6},{6,7},{7,4},{8,9},{9,10},{10,1... | collective-permute-start | bytes 1671176 | tf_op jit(solution)/shard_map/ppermute | solution.py:140
  44.1 29.2 %collective-permute-start.1 = (bf16[8,17,16,128]{3,2,1,0:T(8,128)(2,1)}, bf16[8,17,16,128]{3,2,1,0:T(8,128)(2,1)}, u32[]{:S(2)}, u32[]{:S(2)}) collective-permute-start(bf16[8,17,16,128]{3,2,1,0:T(8,128)(2,1)} %bitcast.112), channel_id=1, source_target_pairs={{0,2},{1,3},{2,0},{3,1},{4,6},{5,7},{6,4},{7,5},{8,10},{9,11},{10,... | collective-permute-start | bytes 1671176 | tf_op jit(solution)/shard_map/ppermute | solution.py:140
  45.8 27.5 %collective-permute-start.2 = (bf16[8,17,16,128]{3,2,1,0:T(8,128)(2,1)}, bf16[8,17,16,128]{3,2,1,0:T(8,128)(2,1)}, u32[]{:S(2)}, u32[]{:S(2)}) collective-permute-start(bf16[8,17,16,128]{3,2,1,0:T(8,128)(2,1)} %bitcast.111), channel_id=1, source_target_pairs={{0,3},{1,0},{2,1},{3,2},{4,7},{5,4},{6,5},{7,6},{8,11},{9,8},{10,9... | collective-permute-start | bytes 1671176 | tf_op jit(solution)/shard_map/ppermute | solution.py:140
  51.3 40.3 %copy-start.14 = (s32[8]{0:T(128)S(1)}, s32[8]{0:T(128)}, u32[]{:S(2)}) copy-start(s32[8]{0:T(128)} %param.25) | copy-start | bytes 100
  51.3 30.1 %all-to-all-start.1 = ((bf16[8,16,16,128]{3,1,2,0:T(8,128)(2,1)}), bf16[8,16,16,128]{3,1,2,0:T(8,128)(2,1)}, u32[]{:S(2)}, u32[]{:S(2)}) async-start(bf16[8,16,16,128]{3,1,2,0:T(8,128)(2,1)} %fusion.17), calls=%async_computation.1 | async-start | bytes 1048576 | tf_op jit(solution)/shard_map/all_to_all | solution.py:144
  81.4 34.0 %all-to-all-start = ((bf16[8,20,16,128]{3,2,1,0:T(8,128)(2,1)}), bf16[8,20,16,128]{3,2,1,0:T(8,128)(2,1)}, u32[]{:S(2)}, u32[]{:S(2)}) async-start(bf16[8,20,16,128]{3,2,1,0:T(8,128)(2,1)} %slice_dynamic-update-slice_fusion), calls=%async_computation | async-start | bytes 1310720 | tf_op jit(solution)/shard_map/all_to_all | solution.py:144
  89.6 139.6 %all-gather.5.cloned.1.call-start = ((), (), s32[]{:S(2)}) async-start(), calls=%async_computation.2 | async-start | bytes 6488064 | tf_op jit(solution)/shard_map/all_gather | solution.py:176
  91.6 35.3 %copy-start.7 = (bf16[8,128,128]{2,1,0:T(8,128)(2,1)S(1)}, bf16[8,128,128]{2,1,0:T(8,128)(2,1)}, u32[]{:S(2)}) copy-start(bf16[8,128,128]{2,1,0:T(8,128)(2,1)} %param.23) | copy-start | bytes 786436
  122.0 5.2 %copy-start.8 = (bf16[8,128,128]{2,1,0:T(8,128)(2,1)S(1)}, bf16[8,128,128]{2,1,0:T(8,128)(2,1)}, u32[]{:S(2)}) copy-start(bf16[8,128,128]{2,1,0:T(8,128)(2,1)} %param.24) | copy-start | bytes 786436
  127.1 0.6 copy-start.9
  127.8 3.5 %collective-permute-start.6 = (f32[4,16,128]{2,0,1:T(4,128)S(1)}, f32[4,16,128]{2,0,1:T(4,128)S(1)}, u32[]{:S(2)}, u32[]{:S(2)}) collective-permute-start(f32[4,16,128]{2,0,1:T(4,128)S(1)} %fusion.24), channel_id=1, source_target_pairs={{0,32},{32,0},{64,96},{96,64},{128,160},{160,128},{192,224},{224,1... | collective-permute-start | bytes 98312 | tf_op jit(solution)/shard_map/ppermute | solution.py:160
  131.3 3.1 %collective-permute-start.7 = (f32[4,16,128]{2,0,1:T(4,128)S(1)}, f32[4,16,128]{2,0,1:T(4,128)S(1)}, u32[]{:S(2)}, u32[]{:S(2)}) collective-permute-start(f32[4,16,128]{2,0,1:T(4,128)S(1)} %add.165), channel_id=1, source_target_pairs={{0,64},{32,96},{64,0},{96,32},{128,192},{160,224},{192,128},{224,1... | collective-permute-start | bytes 98312 | tf_op jit(solution)/shard_map/ppermute | solution.py:160
  135.0 4.6 %collective-permute-start.8 = (f32[4,16,128]{2,0,1:T(4,128)}, f32[4,16,128]{2,0,1:T(4,128)}, u32[]{:S(2)}, u32[]{:S(2)}) collective-permute-start(f32[4,16,128]{2,0,1:T(4,128)} %add.166), channel_id=1, source_target_pairs={{0,128},{32,160},{64,192},{96,224},{128,0},{160,32},{192,64},{224,... | collective-permute-start | bytes 98312 | tf_op jit(solution)/shard_map/ppermute | solution.py:160
Sparse Core Ops, SparseCore 0:
  27.3 89.0 all-gather.6
  160.1 68.9 all-gather.4

commit v7 on v5

--- a/solution.py
+++ b/solution.py
@@ -125,7 +125,12 @@
     node_part = piece_transposed(row_inverse, node_w).astype(jnp.bfloat16)
 
     parts = jnp.concatenate([node_part, middle_part, top_part], axis=0)
-    gathered = lax.all_gather(lax.all_gather(parts, "y", axis=0, tiled=False), "z", axis=0, tiled=True)
+    arrivals = [parts]
+    for shift in range(1, y_size):
+        pairs = [(i, (i + shift) % y_size) for i in range(y_size)]
+        arrivals.append(lax.ppermute(parts, "y", pairs))
+    by_y = jnp.take(jnp.stack(arrivals), (y_index - lax.iota(jnp.int32, y_size)) % y_size, axis=0)
+    gathered = lax.all_gather(by_y, "z", axis=0, tiled=True)
     upper = gathered[:, peers:].transpose(1, 3, 0, 2).reshape(middle_count + top_count, width, columns)
     middle_result = upper[:middle_count]
     top_result = upper[middle_count:]

time: 255 us -> 252 us (0.988)
  blocking collectives: 11.5 us -> 0 us
  starting transfers between devices: 30.5 us -> 35.4 us
  waiting for transfers between devices: 127 us -> 130 us
    all_gather x1 -> x0, blocking collectives: 11.5 us -> none  [local(): lax.all_gather(parts, 'y', axis=0, tiled=False)]
    ppermute x0 -> x3, waiting for transfers between devices: none -> 5.33 us  [local(): arrivals.append(lax.ppermute(parts, 'y', pairs))]
    ppermute x0 -> x3, starting transfers between devices: none -> 4.68 us  [local(): arrivals.append(lax.ppermute(parts, 'y', pairs))]
  transfers between devices with their start and end apart: 13 -> 16, of which waited for: 9 -> 11; matrix products, arithmetic and copies ran while one was open for 9% -> 10% of each run, Pallas kernels for 0% -> 0%
where the time goes in v7:
time: 252 us
  waiting for transfers between devices  130 us (52%)
  starting transfers between devices  35.4 us (14%)
  local copies, waits for them, and re-layouts  33.9 us (13%)
  matrix products  28.2 us (11%)
  between operations  14.5 us (6%)
  other arithmetic  9.94 us (4%)
    all_gather x1, waiting for transfers between devices, local(): gathered = lax.all_gather(by_y, 'z', axis=0, tiled=True)  71.1 us
    all_to_all x2, waiting for transfers between devices, local(): incoming = lax.all_to_all(partial, 'z', 0, 0, tiled=True)  23 us
    ppermute x6, waiting for transfers between devices, local(): arrivals.append(lax.ppermute(outbound, 'y', pairs))  20.4 us
    unnamed x46, local copies, waits for them, and re-layouts  17.4 us
    all_to_all x2, starting transfers between devices, local(): incoming = lax.all_to_all(partial, 'z', 0, 0, tiled=True)  14.5 us
    ppermute x6, starting transfers between devices, local(): arrivals.append(lax.ppermute(outbound, 'y', pairs))  8.61 us
    ppermute x3, starting transfers between devices, local(): lax.ppermute(top_sum, ROW, [(i, i ^ step) for i in range(rows)])  7.51 us
    all_gather x1, waiting for transfers between devices, local(): lax.all_gather(jnp.concatenate([node_inverse, node_link], axis=0), COL, a...  7.47 us
  transfers between devices with their start and end apart: 16, of which 11 were waited for; matrix products, arithmetic and copies ran while one was open for 10% of the time, Pallas kernels for 0%

profile of v7, /device:TPU:1, one launch (start us, length us, event | category | flops | bytes accessed | tf_op | source)
XLA Modules:
  0.0 251.9 jit_solution(5213313864604630494)
XLA Ops:
  9.1 2.2 convolution_convert_fusion
  12.9 2.3 fusion.3
  15.2 2.5 add_convert_fusion
  20.1 2.1 collective-permute-start.3
  22.3 2.6 %collective-permute-start.4 = (bf16[8,16,16,128]{3,1,2,0:T(8,128)(2,1)}, bf16[8,16,16,128]{3,1,2,0:T(8,128)(2,1)}, u32[]{:S(2)}, u32[]{:S(2)}) collective-permute-start(bf16[8,16,16,128]{3,1,2,0:T(8,128)(2,1)} %get-tuple-element.35), channel_id=1, source_target_pairs={{0,2},{1,3},{2,0},{3,1},{4,6},{5,7},{6,4},{7,5},{8,10},{9,11},{10,... | collective-permute-start | bytes 1572872 | tf_op jit(solution)/shard_map/ppermute | solution.py:92
  26.6 4.2 %fusion.5 = f32[16,512,128]{2,0,1:T(8,128)S(1)} fusion(bf16[24,512,128]{2,1,0:T(8,128)(2,1)} %copy-done.4, s32[24]{0:T(128)S(1)} %broadcast_add_fusion), kind=kOutput, calls=%fused_computation.15 | convolution fusion | flops 50332032 | bytes 7340128 | tf_op jit(solution)/shard_map/sk,k...->s.../dot_general | solution.py:39
  30.8 3.8 %add_convert_fusion.1 = bf16[16,512,128]{2,0,1:T(8,128)(2,1)} fusion(f32[16,512,128]{2,0,1:T(8,128)S(1)} %fusion.5, bf16[24,512,128]{2,1,0:T(8,128)(2,1)S(1)} %get-tuple-element.28, s32[24]{0:T(128)S(1)} %broadcast_add_fusion), kind=kOutput, calls=%fused_computation.9 | convolution fusion | flops 52429184 | bytes 9437280 | tf_op jit(solution)/shard_map/sk,k...->s.../dot_general | solution.py:38
  34.8 2.3 pad_maximum_fusion
  41.6 1.6 collective-permute-start.2
  43.3 4.9 %collective-permute-done.4 = bf16[8,16,16,128]{3,1,2,0:T(8,128)(2,1)} collective-permute-done((bf16[8,16,16,128]{3,1,2,0:T(8,128)(2,1)}, bf16[8,16,16,128]{3,1,2,0:T(8,128)(2,1)}, u32[]{:S(2)}, u32[]{:S(2)}) %collective-permute-start.4) | collective-permute-done | bytes 524320 | tf_op jit(solution)/shard_map/ppermute | solution.py:92
  48.2 2.1 collective-permute-done.5
  50.3 2.6 %fusion.24 = bf16[8,16,16,128]{3,1,2,0:T(8,128)(2,1)} fusion(bf16[8,16,16,128]{3,1,2,0:T(8,128)(2,1)} %collective-permute-done.5, bf16[8,16,16,128]{3,1,2,0:T(8,128)(2,1)} %collective-permute-done.4, bf16[8,16,16,128]{3,1,2,0:T(8,128)(2,1)} %collective-permute-done.3, bf16[16,8,4,16,128]{4,0,3,2,1:T(8,128)(2,1)} %bitcast.133, s32[]{:T(128)S(6)} %select_n.117), kind=kLoop, calls=%fused_computation.41 | loop fusion | flops 2097152 | bytes 2621444 | tf_op jit(solution)/shard_map/convert_element_type | solution.py:93
  52.9 6.3 %all-to-all-start.1 = ((bf16[8,16,16,128]{3,1,2,0:T(8,128)(2,1)}), bf16[8,16,16,128]{3,1,2,0:T(8,128)(2,1)S(1)}, u32[]{:S(2)}, u32[]{:S(2)}) async-start(bf16[8,16,16,128]{3,1,2,0:T(8,128)(2,1)} %fusion.24), calls=%async_computation.1 | async-start | bytes 1048576 | tf_op jit(solution)/shard_map/all_to_all | solution.py:96
  59.2 3.5 %collective-permute-done = bf16[8,17,16,128]{3,2,1,0:T(8,128)(2,1)S(1)} collective-permute-done((bf16[8,17,16,128]{3,2,1,0:T(8,128)(2,1)}, bf16[8,17,16,128]{3,2,1,0:T(8,128)(2,1)S(1)}, u32[]{:S(2)}, u32[]{:S(2)}) %collective-permute-start) | collective-permute-done | bytes 557088 | tf_op jit(solution)/shard_map/ppermute | solution.py:92
  62.7 9.9 %collective-permute-done.1 = bf16[8,17,16,128]{3,2,1,0:T(8,128)(2,1)S(1)} collective-permute-done((bf16[8,17,16,128]{3,2,1,0:T(8,128)(2,1)}, bf16[8,17,16,128]{3,2,1,0:T(8,128)(2,1)S(1)}, u32[]{:S(2)}, u32[]{:S(2)}) %collective-permute-start.1) | collective-permute-done | bytes 557088 | tf_op jit(solution)/shard_map/ppermute | solution.py:92
  76.2 8.2 %all-to-all-start = ((bf16[8,20,16,128]{3,2,1,0:T(8,128)(2,1)}), bf16[8,20,16,128]{3,2,1,0:T(8,128)(2,1)S(1)}, u32[]{:S(2)}, u32[]{:S(2)}) async-start(bf16[8,20,16,128]{3,2,1,0:T(8,128)(2,1)} %slice_dynamic-update-slice_fusion), calls=%async_computation | async-start | bytes 1310720 | tf_op jit(solution)/shard_map/all_to_all | solution.py:96
  85.9 23.0 %all-to-all-done = bf16[8,20,16,128]{3,2,1,0:T(8,128)(2,1)S(1)} async-done(((bf16[8,20,16,128]{3,2,1,0:T(8,128)(2,1)}), bf16[8,20,16,128]{3,2,1,0:T(8,128)(2,1)S(1)}, u32[]{:S(2)}, u32[]{:S(2)}) %all-to-all-start) | async-done | bytes 655392 | tf_op jit(solution)/shard_map/all_to_all | solution.py:96
  109.8 7.5 %all-gather.6.cloned.1.call-done = bf16[64,128,128]{2,1,0:T(8,128)(2,1)} async-done(((bf16[2,128,128]{2,1,0:T(8,128)(2,1)}), bf16[64,128,128]{2,1,0:T(8,128)(2,1)}) %all-gather.6.cloned.1.call-update) | async-done | bytes 2097168 | tf_op jit(solution)/shard_map/all_gather | solution.py:71
  117.2 2.0 convolution_convert_fusion.2
  119.3 1.9 fusion.25
  122.1 2.8 %collective-permute-start.6 = (f32[4,16,128]{2,0,1:T(4,128)S(1)}, f32[4,16,128]{2,0,1:T(4,128)S(1)}, u32[]{:S(2)}, u32[]{:S(2)}) collective-permute-start(f32[4,16,128]{2,0,1:T(4,128)S(1)} %fusion.31), channel_id=1, source_target_pairs={{0,32},{32,0},{64,96},{96,64},{128,160},{160,128},{192,224},{224,1... | collective-permute-start | bytes 98312 | tf_op jit(solution)/shard_map/ppermute | solution.py:112
  125.9 1.7 collective-permute-start.7
  129.0 3.0 %collective-permute-start.8 = (f32[4,16,128]{2,0,1:T(4,128)S(1)}, f32[4,16,128]{2,0,1:T(4,128)S(1)}, u32[]{:S(2)}, u32[]{:S(2)}) collective-permute-start(f32[4,16,128]{2,0,1:T(4,128)S(1)} %add.173), channel_id=1, source_target_pairs={{0,128},{32,160},{64,192},{96,224},{128,0},{160,32},{192,64},{224,... | collective-permute-start | bytes 98312 | tf_op jit(solution)/shard_map/ppermute | solution.py:112
  137.1 3.1 %collective-permute-start.10 = (bf16[44,16,128]{2,1,0:T(8,128)(2,1)S(1)}, bf16[44,16,128]{2,1,0:T(8,128)(2,1)S(1)}, u32[]{:S(2)}, u32[]{:S(2)}) collective-permute-start(bf16[44,16,128]{2,1,0:T(8,128)(2,1)S(1)} %get-tuple-element.38), channel_id=1, source_target_pairs={{0,2},{1,3},{2,0},{3,1},{4,6},{5,7},{6,4},{7,5},{8,10},{9,11},{10,... | collective-permute-start | bytes 540680 | tf_op jit(solution)/shard_map/ppermute | solution.py:131
  141.8 4.1 %collective-permute-done.10 = bf16[44,16,128]{2,1,0:T(8,128)(2,1)S(1)} collective-permute-done((bf16[44,16,128]{2,1,0:T(8,128)(2,1)S(1)}, bf16[44,16,128]{2,1,0:T(8,128)(2,1)S(1)}, u32[]{:S(2)}, u32[]{:S(2)}) %collective-permute-start.10) | collective-permute-done | bytes 180256 | tf_op jit(solution)/shard_map/ppermute | solution.py:131
  147.7 71.1 %all-gather.4.cloned.1.call-done = bf16[32,44,16,128]{3,2,1,0:T(8,128)(2,1)} async-done(((bf16[4,44,16,128]{3,2,1,0:T(8,128)(2,1)}), bf16[32,44,16,128]{3,2,1,0:T(8,128)(2,1)}) %all-gather.4.cloned.1.call-update) | async-done | bytes 5767184 | tf_op jit(solution)/shard_map/all_gather | solution.py:133
  218.8 1.8 copy_bitcast_fusion
  222.7 5.7 %gather_fusion.4 = bf16[24,32,16,128]{3,2,1,0:T(8,128)(2,1)} fusion(bf16[32,44,16,128]{3,2,1,0:T(8,128)(2,1)} %all-gather.4.cloned.1.call-done, s32[1024]{0:T(1024)S(1)} %pad_clamp_fusion), kind=kCustom, calls=%fused_computation.4 | custom fusion | bytes 6291552 | tf_op jit(solution)/shard_map/gather | solution.py:139
  228.4 5.8 %convert_bitcast_fusion = bf16[24,128,512]{1,2,0:T(8,128)(2,1)} fusion(bf16[24,128,128]{2,1,0:T(8,128)(2,1)} %param.15, bf16[24,128,512]{2,1,0:T(8,128)(2,1)S(1)} %copy-done.3, bf16[24,512,128]{2,1,0:T(8,128)(2,1)} %bitcast.131, bf16[24,128,128]{2,1,0:T(8,128)(2,1)} %param.16), kind=kOutput, calls=%fused_computation.12 | convolution fusion | flops 811597824 | bytes 11010048 | tf_op jit(solution)/shard_map/nij,nir->njr/dot_general | solution.py:16
  234.2 4.8 %copy.150 = bf16[24,128,512]{2,1,0:T(8,128)(2,1)} copy(bf16[24,128,512]{1,2,0:T(8,128)(2,1)} %convert_bitcast_fusion) | data formatting | bytes 6291456
  239.0 2.3 copy.152
  241.3 2.0 copy.153
  (106 shorter events, 33.8 us)
Async XLA Ops:
  7.2 1.9 copy-start
  7.2 110.1 %all-gather.6.cloned.1.call-start = ((), (), s32[]{:S(2)}) async-start(), calls=%async_computation.3 | async-start | bytes 2162688 | tf_op jit(solution)/shard_map/all_gather | solution.py:71
  9.1 2.2 copy-start.7
  11.3 1.7 copy-start.2
  12.9 2.3 copy-start.4
  17.6 1.3 copy-start.5
  17.7 8.3 %copy-start.12 = (bf16[1,128,128]{2,1,0:T(8,128)(2,1)S(1)}, bf16[1,128,128]{2,1,0:T(8,128)(2,1)}, u32[]{:S(2)}) copy-start(bf16[1,128,128]{2,1,0:T(8,128)(2,1)} %param.20) | copy-start | bytes 98308
  17.7 8.3 %copy-start.13 = (bf16[1,128,128]{2,1,0:T(8,128)(2,1)S(1)}, bf16[1,128,128]{2,1,0:T(8,128)(2,1)}, u32[]{:S(2)}) copy-start(bf16[1,128,128]{2,1,0:T(8,128)(2,1)} %param.19) | copy-start | bytes 98308
  20.1 21.5 %collective-permute-start.3 = (bf16[8,16,16,128]{3,1,2,0:T(8,128)(2,1)}, bf16[8,16,16,128]{3,1,2,0:T(8,128)(2,1)}, u32[]{:S(2)}, u32[]{:S(2)}) collective-permute-start(bf16[8,16,16,128]{3,1,2,0:T(8,128)(2,1)} %get-tuple-element.34), channel_id=1, source_target_pairs={{0,1},{1,2},{2,3},{3,0},{4,5},{5,6},{6,7},{7,4},{8,9},{9,10},{10,1... | collective-permute-start | bytes 1572872 | tf_op jit(solution)/shard_map/ppermute | solution.py:92
  22.3 25.9 %collective-permute-start.4 = (bf16[8,16,16,128]{3,1,2,0:T(8,128)(2,1)}, bf16[8,16,16,128]{3,1,2,0:T(8,128)(2,1)}, u32[]{:S(2)}, u32[]{:S(2)}) collective-permute-start(bf16[8,16,16,128]{3,1,2,0:T(8,128)(2,1)} %get-tuple-element.35), channel_id=1, source_target_pairs={{0,2},{1,3},{2,0},{3,1},{4,6},{5,7},{6,4},{7,5},{8,10},{9,11},{10,... | collective-permute-start | bytes 1572872 | tf_op jit(solution)/shard_map/ppermute | solution.py:92
  24.9 25.4 %collective-permute-start.5 = (bf16[8,16,16,128]{3,1,2,0:T(8,128)(2,1)}, bf16[8,16,16,128]{3,1,2,0:T(8,128)(2,1)}, u32[]{:S(2)}, u32[]{:S(2)}) collective-permute-start(bf16[8,16,16,128]{3,1,2,0:T(8,128)(2,1)} %get-tuple-element.36), channel_id=1, source_target_pairs={{0,3},{1,0},{2,1},{3,2},{4,7},{5,4},{6,5},{7,6},{8,11},{9,8},{10,9... | collective-permute-start | bytes 1572872 | tf_op jit(solution)/shard_map/ppermute | solution.py:92
  30.8 3.8 %copy-start.11 = (bf16[1,128,512]{2,1,0:T(8,128)(2,1)S(1)}, bf16[1,128,512]{2,1,0:T(8,128)(2,1)}, u32[]{:S(2)}) copy-start(bf16[1,128,512]{2,1,0:T(8,128)(2,1)} %param.18) | copy-start | bytes 393220
  38.6 24.1 %collective-permute-start = (bf16[8,17,16,128]{3,2,1,0:T(8,128)(2,1)}, bf16[8,17,16,128]{3,2,1,0:T(8,128)(2,1)S(1)}, u32[]{:S(2)}, u32[]{:S(2)}) collective-permute-start(bf16[8,17,16,128]{3,2,1,0:T(8,128)(2,1)} %bitcast.128), channel_id=1, source_target_pairs={{0,1},{1,2},{2,3},{3,0},{4,5},{5,6},{6,7},{7,4},{8,9},{9,10},{10,1... | collective-permute-start | bytes 1671176 | tf_op jit(solution)/shard_map/ppermute | solution.py:92
  39.9 32.7 %collective-permute-start.1 = (bf16[8,17,16,128]{3,2,1,0:T(8,128)(2,1)}, bf16[8,17,16,128]{3,2,1,0:T(8,128)(2,1)S(1)}, u32[]{:S(2)}, u32[]{:S(2)}) collective-permute-start(bf16[8,17,16,128]{3,2,1,0:T(8,128)(2,1)} %bitcast.127), channel_id=1, source_target_pairs={{0,2},{1,3},{2,0},{3,1},{4,6},{5,7},{6,4},{7,5},{8,10},{9,11},{10,... | collective-permute-start | bytes 1671176 | tf_op jit(solution)/shard_map/ppermute | solution.py:92
  41.6 31.0 %collective-permute-start.2 = (bf16[8,17,16,128]{3,2,1,0:T(8,128)(2,1)}, bf16[8,17,16,128]{3,2,1,0:T(8,128)(2,1)S(1)}, u32[]{:S(2)}, u32[]{:S(2)}) collective-permute-start(bf16[8,17,16,128]{3,2,1,0:T(8,128)(2,1)} %bitcast.126), channel_id=1, source_target_pairs={{0,3},{1,0},{2,1},{3,2},{4,7},{5,4},{6,5},{7,6},{8,11},{9,8},{10,9... | collective-permute-start | bytes 1671176 | tf_op jit(solution)/shard_map/ppermute | solution.py:92
  52.9 32.9 %copy-start.14 = (s32[8]{0:T(128)S(1)}, s32[8]{0:T(128)}, u32[]{:S(2)}) copy-start(s32[8]{0:T(128)} %param.25) | copy-start | bytes 100
  52.9 32.9 %copy-start.15 = (s32[32]{0:T(128)S(1)}, s32[32]{0:T(128)}, u32[]{:S(2)}) copy-start(s32[32]{0:T(128)} %param.21) | copy-start | bytes 388
  52.9 23.3 %all-to-all-start.1 = ((bf16[8,16,16,128]{3,1,2,0:T(8,128)(2,1)}), bf16[8,16,16,128]{3,1,2,0:T(8,128)(2,1)S(1)}, u32[]{:S(2)}, u32[]{:S(2)}) async-start(bf16[8,16,16,128]{3,1,2,0:T(8,128)(2,1)} %fusion.24), calls=%async_computation.1 | async-start | bytes 1048576 | tf_op jit(solution)/shard_map/all_to_all | solution.py:96
  76.2 32.7 %all-to-all-start = ((bf16[8,20,16,128]{3,2,1,0:T(8,128)(2,1)}), bf16[8,20,16,128]{3,2,1,0:T(8,128)(2,1)S(1)}, u32[]{:S(2)}, u32[]{:S(2)}) async-start(bf16[8,20,16,128]{3,2,1,0:T(8,128)(2,1)} %slice_dynamic-update-slice_fusion), calls=%async_computation | async-start | bytes 1310720 | tf_op jit(solution)/shard_map/all_to_all | solution.py:96
  84.3 134.5 %all-gather.4.cloned.1.call-start = ((), (), s32[]{:S(2)}) async-start(), calls=%async_computation.2 | async-start | bytes 6488064 | tf_op jit(solution)/shard_map/all_gather | solution.py:133
  85.6 35.9 %copy-start.8 = (bf16[8,128,128]{2,1,0:T(8,128)(2,1)S(1)}, bf16[8,128,128]{2,1,0:T(8,128)(2,1)}, u32[]{:S(2)}) copy-start(bf16[8,128,128]{2,1,0:T(8,128)(2,1)} %param.23) | copy-start | bytes 786436
  85.8 35.9 %copy-start.9 = (bf16[8,128,128]{2,1,0:T(8,128)(2,1)S(1)}, bf16[8,128,128]{2,1,0:T(8,128)(2,1)}, u32[]{:S(2)}) copy-start(bf16[8,128,128]{2,1,0:T(8,128)(2,1)} %param.24) | copy-start | bytes 786436
  109.5 23.9 %copy-start.10 = (bf16[4,128,128]{2,1,0:T(8,128)(2,1)S(1)}, bf16[4,128,128]{2,1,0:T(8,128)(2,1)}, u32[]{:S(2)}) copy-start(bf16[4,128,128]{2,1,0:T(8,128)(2,1)} %param.27) | copy-start | bytes 393220
  117.2 17.9 %copy-start.6 = (bf16[64,128,128]{2,1,0:T(8,128)(2,1)S(1)}, bf16[64,128,128]{2,1,0:T(8,128)(2,1)}, u32[]{:S(2)}) copy-start(bf16[64,128,128]{2,1,0:T(8,128)(2,1)} %all-gather.6.cloned.1.call-done) | copy-start | bytes 6291460
  122.1 3.8 %collective-permute-start.6 = (f32[4,16,128]{2,0,1:T(4,128)S(1)}, f32[4,16,128]{2,0,1:T(4,128)S(1)}, u32[]{:S(2)}, u32[]{:S(2)}) collective-permute-start(f32[4,16,128]{2,0,1:T(4,128)S(1)} %fusion.31), channel_id=1, source_target_pairs={{0,32},{32,0},{64,96},{96,64},{128,160},{160,128},{192,224},{224,1... | collective-permute-start | bytes 98312 | tf_op jit(solution)/shard_map/ppermute | solution.py:112
  125.9 3.1 %collective-permute-start.7 = (f32[4,16,128]{2,0,1:T(4,128)S(1)}, f32[4,16,128]{2,0,1:T(4,128)S(1)}, u32[]{:S(2)}, u32[]{:S(2)}) collective-permute-start(f32[4,16,128]{2,0,1:T(4,128)S(1)} %add.172), channel_id=1, source_target_pairs={{0,64},{32,96},{64,0},{96,32},{128,192},{160,224},{192,128},{224,1... | collective-permute-start | bytes 98312 | tf_op jit(solution)/shard_map/ppermute | solution.py:112
  129.0 4.4 %collective-permute-start.8 = (f32[4,16,128]{2,0,1:T(4,128)S(1)}, f32[4,16,128]{2,0,1:T(4,128)S(1)}, u32[]{:S(2)}, u32[]{:S(2)}) collective-permute-start(f32[4,16,128]{2,0,1:T(4,128)S(1)} %add.173), channel_id=1, source_target_pairs={{0,128},{32,160},{64,192},{96,224},{128,0},{160,32},{192,64},{224,... | collective-permute-start | bytes 98312 | tf_op jit(solution)/shard_map/ppermute | solution.py:112
  135.9 6.0 %collective-permute-start.9 = (bf16[44,16,128]{2,1,0:T(8,128)(2,1)S(1)}, bf16[44,16,128]{2,1,0:T(8,128)(2,1)S(1)}, u32[]{:S(2)}, u32[]{:S(2)}) collective-permute-start(bf16[44,16,128]{2,1,0:T(8,128)(2,1)S(1)} %get-tuple-element.38), channel_id=1, source_target_pairs={{0,1},{1,2},{2,3},{3,0},{4,5},{5,6},{6,7},{7,4},{8,9},{9,10},{10,1... | collective-permute-start | bytes 540680 | tf_op jit(solution)/shard_map/ppermute | solution.py:131
  137.1 8.8 %collective-permute-start.10 = (bf16[44,16,128]{2,1,0:T(8,128)(2,1)S(1)}, bf16[44,16,128]{2,1,0:T(8,128)(2,1)S(1)}, u32[]{:S(2)}, u32[]{:S(2)}) collective-permute-start(bf16[44,16,128]{2,1,0:T(8,128)(2,1)S(1)} %get-tuple-element.38), channel_id=1, source_target_pairs={{0,2},{1,3},{2,0},{3,1},{4,6},{5,7},{6,4},{7,5},{8,10},{9,11},{10,... | collective-permute-start | bytes 540680 | tf_op jit(solution)/shard_map/ppermute | solution.py:131
  140.1 5.8 %collective-permute-start.11 = (bf16[44,16,128]{2,1,0:T(8,128)(2,1)S(1)}, bf16[44,16,128]{2,1,0:T(8,128)(2,1)S(1)}, u32[]{:S(2)}, u32[]{:S(2)}) collective-permute-start(bf16[44,16,128]{2,1,0:T(8,128)(2,1)S(1)} %get-tuple-element.38), channel_id=1, source_target_pairs={{0,3},{1,0},{2,1},{3,2},{4,7},{5,4},{6,5},{7,6},{8,11},{9,8},{10,9... | collective-permute-start | bytes 540680 | tf_op jit(solution)/shard_map/ppermute | solution.py:131
  222.7 5.7 %copy-start.3 = (bf16[24,128,512]{2,1,0:T(8,128)(2,1)S(1)}, bf16[24,128,512]{2,1,0:T(8,128)(2,1)}, u32[]{:S(2)}) copy-start(bf16[24,128,512]{2,1,0:T(8,128)(2,1)} %copy-done.2) | copy-start | bytes 9437188
  234.2 10.8 %copy-start.1 = (bf16[24,128,512]{2,1,0:T(8,128)(2,1)S(1)}, bf16[24,128,512]{2,1,0:T(8,128)(2,1)}, u32[]{:S(2)}) copy-start(bf16[24,128,512]{2,1,0:T(8,128)(2,1)} %param.14) | copy-start | bytes 9437188
Sparse Core Ops, SparseCore 0:
  26.7 90.4 all-gather.5
  147.8 70.9 all-gather.3

commit v8 on v7

--- a/solution.py
+++ b/solution.py
@@ -68,14 +68,20 @@
     middle_target = node_parent % middle_count
     start = col_index * chunk
 
-    node_mats = lax.all_gather(jnp.concatenate([node_inverse, node_link], axis=0), COL, axis=0, tiled=False)
+    y_index = lax.axis_index("y")
+    own_mats = jnp.concatenate([node_inverse, node_link], axis=0)
+    mats = [own_mats]
+    for shift in range(1, y_size):
+        pairs = [(i, (i + shift) % y_size) for i in range(y_size)]
+        mats.append(lax.ppermute(own_mats, "y", pairs))
+    mats_by_y = jnp.take(jnp.stack(mats), (y_index - lax.iota(jnp.int32, y_size)) % y_size, axis=0)
+    node_mats = lax.all_gather(mats_by_y, "z", axis=0, tiled=True)
     row_inverse = node_mats[:, 0]
     row_link = node_mats[:, 1]
 
     leaf_solved = apply_block(leaf_inverse, leaf_rhs).astype(jnp.bfloat16)
     leaf_update = jnp.einsum("kij,kjr->kri", leaf_link, leaf_solved, preferred_element_type=jnp.float32)
     half = peers // 2
-    y_index = lax.axis_index("y")
     rhs_t = node_rhs.transpose(0, 2, 1)
     sums = []
     for group in range(2):

time: 252 us -> 242 us (0.960)
  waiting for transfers between devices: 130 us -> 111 us
  starting transfers between devices: 35.4 us -> 38.8 us
    ppermute x6, waiting for transfers between devices: 20.4 us -> 12.5 us  [local(): arrivals.append(lax.ppermute(outbound, 'y', pairs))]
    all_gather x1, waiting for transfers between devices: 7.47 us -> 0.02 us  [local(): node_mats = lax.all_gather(mats_by_y, 'z', axis=0, tiled=True)]
    ppermute x0 -> x3, starting transfers between devices: none -> 5.81 us  [local(): mats.append(lax.ppermute(own_mats, 'y', pairs))]
    all_gather x1, waiting for transfers between devices: 71.1 us -> 67.9 us  [local(): gathered = lax.all_gather(by_y, 'z', axis=0, tiled=True)]
    all_to_all x2, starting transfers between devices: 14.5 us -> 11.9 us  [local(): incoming = lax.all_to_all(partial, 'z', 0, 0, tiled=True)]
    unnamed x46 -> x41, local copies, waits for them, and re-layouts: 17.4 us -> 16 us
  transfers between devices with their start and end apart: 16 -> 19, of which waited for: 11 -> 11; matrix products, arithmetic and copies ran while one was open for 10% -> 16% of each run, Pallas kernels for 0% -> 0%
where the time goes in v8:
time: 242 us; the launch traced here: 241 us
  waiting for transfers between devices  111 us (46%)
  starting transfers between devices  38.8 us (16%)
  local copies, waits for them, and re-layouts  35.1 us (15%)
  matrix products  30.5 us (13%)
  between operations  14.4 us (6%)
  other arithmetic  10.7 us (4%)
    all_gather x1, waiting for transfers between devices, local(): gathered = lax.all_gather(by_y, 'z', axis=0, tiled=True)  67.9 us
    all_to_all x2, waiting for transfers between devices, local(): incoming = lax.all_to_all(partial, 'z', 0, 0, tiled=True)  22.2 us
    unnamed x41, local copies, waits for them, and re-layouts  16 us
    ppermute x6, waiting for transfers between devices, local(): arrivals.append(lax.ppermute(outbound, 'y', pairs))  12.5 us
    all_to_all x2, starting transfers between devices, local(): incoming = lax.all_to_all(partial, 'z', 0, 0, tiled=True)  11.9 us
    dot_general x2, matrix products, split_slot_sums(): jnp.einsum('sk,k...->s...', select, high, preferred_element_type=jnp.floa...  8.53 us
    ppermute x3, starting transfers between devices, local(): lax.ppermute(top_sum, ROW, [(i, i ^ step) for i in range(rows)])  7.7 us
    ppermute x6, starting transfers between devices, local(): arrivals.append(lax.ppermute(outbound, 'y', pairs))  7.19 us
  transfers between devices with their start and end apart: 19, of which 11 were waited for; matrix products, arithmetic and copies ran while one was open for 16% of the time, Pallas kernels for 0%

profile of v8, /device:TPU:1, one launch (start us, length us, event | category | flops | bytes accessed | tf_op | source)
XLA Modules:
  0.0 241.1 jit_solution(2905191808964253438)
XLA Ops:
  8.9 2.1 collective-permute-start.6
  11.0 2.6 %collective-permute-start.7 = (bf16[2,128,128]{2,1,0:T(8,128)(2,1)S(1)}, bf16[2,128,128]{2,1,0:T(8,128)(2,1)S(1)}, u32[]{:S(2)}, u32[]{:S(2)}) collective-permute-start(bf16[2,128,128]{2,1,0:T(8,128)(2,1)S(1)} %constant_dynamic-update-slice_fusion), channel_id=1, source_target_pairs={{0,2},{1,3},{2,0},{3,1},{4,6},{5,7},{6,4},{7,5},{8,10},{9,11},{10,... | collective-permute-start | bytes 196616 | tf_op jit(solution)/shard_map/ppermute | solution.py:76
  15.4 2.2 convolution_convert_fusion
  19.3 2.3 fusion.3
  21.5 2.5 %add_convert_fusion = bf16[16,512,128]{2,0,1:T(8,128)(2,1)S(1)} fusion(f32[16,512,128]{2,0,1:T(8,128)S(1)} %fusion.3, bf16[24,512,128]{2,1,0:T(8,128)(2,1)S(1)} %get-tuple-element.28, s32[24]{0:T(128)S(1)} %get-tuple-element.25), kind=kOutput, calls=%fused_computation.9 | convolution fusion | flops 52429184 | bytes 9437280 | tf_op jit(solution)/shard_map/sk,k...->s.../dot_general | solution.py:38
  26.6 4.2 %fusion.5 = f32[16,512,128]{2,0,1:T(8,128)} fusion(bf16[24,512,128]{2,1,0:T(8,128)(2,1)S(1)} %get-tuple-element.29, s32[24]{0:T(128)S(1)} %broadcast_add_fusion), kind=kOutput, calls=%fused_computation.16 | convolution fusion | flops 50332032 | bytes 7340128 | tf_op jit(solution)/shard_map/sk,k...->s.../dot_general | solution.py:39
  30.9 1.7 collective-permute-start.5
  35.7 6.1 %add_convert_fusion.1 = bf16[16,512,128]{2,0,1:T(8,128)(2,1)} fusion(f32[16,512,128]{2,0,1:T(8,128)} %fusion.5, bf16[24,512,128]{2,1,0:T(8,128)(2,1)S(1)} %get-tuple-element.28, s32[24]{0:T(128)S(1)} %broadcast_add_fusion), kind=kOutput, calls=%fused_computation.10 | convolution fusion | flops 52429184 | bytes 9437280 | tf_op jit(solution)/shard_map/sk,k...->s.../dot_general | solution.py:38
  42.0 2.3 pad_maximum_fusion
  47.2 1.8 collective-permute-start.1
  49.8 2.1 collective-permute-start.2
  52.1 2.6 %fusion.24 = bf16[8,16,16,128]{3,1,2,0:T(8,128)(2,1)} fusion(bf16[8,16,16,128]{3,1,2,0:T(8,128)(2,1)} %collective-permute-done.5, bf16[8,16,16,128]{3,1,2,0:T(8,128)(2,1)} %collective-permute-done.4, bf16[8,16,16,128]{3,1,2,0:T(8,128)(2,1)} %collective-permute-done.3, bf16[16,8,4,16,128]{4,0,3,2,1:T(8,128)(2,1)} %bitcast.132, s32[]{:T(128)S(6)} %select_n.125), kind=kLoop, calls=%fused_computation.42 | loop fusion | flops 2097152 | bytes 2621444 | tf_op jit(solution)/shard_map/convert_element_type | solution.py:99
  54.7 8.3 %all-to-all-start.1 = ((bf16[8,16,16,128]{3,1,2,0:T(8,128)(2,1)}), bf16[8,16,16,128]{3,1,2,0:T(8,128)(2,1)S(1)}, u32[]{:S(2)}, u32[]{:S(2)}) async-start(bf16[8,16,16,128]{3,1,2,0:T(8,128)(2,1)} %fusion.24), calls=%async_computation.1 | async-start | bytes 1048576 | tf_op jit(solution)/shard_map/all_to_all | solution.py:102
  63.4 9.5 %collective-permute-done.1 = bf16[8,17,16,128]{3,2,1,0:T(8,128)(2,1)S(1)} collective-permute-done((bf16[8,17,16,128]{3,2,1,0:T(8,128)(2,1)}, bf16[8,17,16,128]{3,2,1,0:T(8,128)(2,1)S(1)}, u32[]{:S(2)}, u32[]{:S(2)}) %collective-permute-start.1) | collective-permute-done | bytes 557088 | tf_op jit(solution)/shard_map/ppermute | solution.py:98
  72.9 2.5 %collective-permute-done.2 = bf16[8,17,16,128]{3,2,1,0:T(8,128)(2,1)S(1)} collective-permute-done((bf16[8,17,16,128]{3,2,1,0:T(8,128)(2,1)}, bf16[8,17,16,128]{3,2,1,0:T(8,128)(2,1)S(1)}, u32[]{:S(2)}, u32[]{:S(2)}) %collective-permute-start.2) | collective-permute-done | bytes 557088 | tf_op jit(solution)/shard_map/ppermute | solution.py:98
  79.0 5.8 %all-to-all-done.1 = bf16[8,16,16,128]{3,1,2,0:T(8,128)(2,1)S(1)} async-done(((bf16[8,16,16,128]{3,1,2,0:T(8,128)(2,1)}), bf16[8,16,16,128]{3,1,2,0:T(8,128)(2,1)S(1)}, u32[]{:S(2)}, u32[]{:S(2)}) %all-to-all-start.1) | async-done | bytes 524320 | tf_op jit(solution)/shard_map/all_to_all | solution.py:102
  84.8 3.5 %all-to-all-start = ((bf16[8,20,16,128]{3,2,1,0:T(8,128)(2,1)}), bf16[8,20,16,128]{3,2,1,0:T(8,128)(2,1)S(1)}, u32[]{:S(2)}, u32[]{:S(2)}) async-start(bf16[8,20,16,128]{3,2,1,0:T(8,128)(2,1)} %slice_dynamic-update-slice_fusion), calls=%async_computation | async-start | bytes 1310720 | tf_op jit(solution)/shard_map/all_to_all | solution.py:102
  89.9 16.3 %all-to-all-done = bf16[8,20,16,128]{3,2,1,0:T(8,128)(2,1)S(1)} async-done(((bf16[8,20,16,128]{3,2,1,0:T(8,128)(2,1)}), bf16[8,20,16,128]{3,2,1,0:T(8,128)(2,1)S(1)}, u32[]{:S(2)}, u32[]{:S(2)}) %all-to-all-start) | async-done | bytes 655392 | tf_op jit(solution)/shard_map/all_to_all | solution.py:102
  107.1 2.0 convolution_convert_fusion.2
  109.1 1.9 fusion.25
  112.0 3.7 %collective-permute-start.9 = (f32[4,16,128]{2,0,1:T(4,128)S(1)}, f32[4,16,128]{2,0,1:T(4,128)S(1)}, u32[]{:S(2)}, u32[]{:S(2)}) collective-permute-start(f32[4,16,128]{2,0,1:T(4,128)S(1)} %fusion.31), channel_id=1, source_target_pairs={{0,32},{32,0},{64,96},{96,64},{128,160},{160,128},{192,224},{224,1... | collective-permute-start | bytes 98312 | tf_op jit(solution)/shard_map/ppermute | solution.py:118
  119.6 2.8 %collective-permute-start.11 = (f32[4,16,128]{2,0,1:T(4,128)S(1)}, f32[4,16,128]{2,0,1:T(4,128)S(1)}, u32[]{:S(2)}, u32[]{:S(2)}) collective-permute-start(f32[4,16,128]{2,0,1:T(4,128)S(1)} %add.177), channel_id=1, source_target_pairs={{0,128},{32,160},{64,192},{96,224},{128,0},{160,32},{192,64},{224,... | collective-permute-start | bytes 98312 | tf_op jit(solution)/shard_map/ppermute | solution.py:118
  127.0 5.6 %collective-permute-start.13 = (bf16[44,16,128]{2,1,0:T(8,128)(2,1)S(1)}, bf16[44,16,128]{2,1,0:T(8,128)(2,1)S(1)}, u32[]{:S(2)}, u32[]{:S(2)}) collective-permute-start(bf16[44,16,128]{2,1,0:T(8,128)(2,1)S(1)} %get-tuple-element.38), channel_id=1, source_target_pairs={{0,2},{1,3},{2,0},{3,1},{4,6},{5,7},{6,4},{7,5},{8,10},{9,11},{10,... | collective-permute-start | bytes 540680 | tf_op jit(solution)/shard_map/ppermute | solution.py:137
  132.6 1.7 collective-permute-done.12
  134.3 4.1 %collective-permute-done.13 = bf16[44,16,128]{2,1,0:T(8,128)(2,1)S(1)} collective-permute-done((bf16[44,16,128]{2,1,0:T(8,128)(2,1)S(1)}, bf16[44,16,128]{2,1,0:T(8,128)(2,1)S(1)}, u32[]{:S(2)}, u32[]{:S(2)}) %collective-permute-start.13) | collective-permute-done | bytes 180256 | tf_op jit(solution)/shard_map/ppermute | solution.py:137
  140.2 67.9 %all-gather.5.cloned.1.call-done = bf16[32,44,16,128]{3,2,1,0:T(8,128)(2,1)} async-done(((bf16[4,44,16,128]{3,2,1,0:T(8,128)(2,1)}), bf16[32,44,16,128]{3,2,1,0:T(8,128)(2,1)}) %all-gather.5.cloned.1.call-update) | async-done | bytes 5767184 | tf_op jit(solution)/shard_map/all_gather | solution.py:139
  208.1 1.8 copy_bitcast_fusion
  211.9 5.7 %gather_fusion.5 = bf16[24,32,16,128]{3,2,1,0:T(8,128)(2,1)} fusion(bf16[32,44,16,128]{3,2,1,0:T(8,128)(2,1)} %all-gather.5.cloned.1.call-done, s32[1024]{0:T(1024)S(1)} %pad_clamp_fusion), kind=kCustom, calls=%fused_computation.5 | custom fusion | bytes 6291552 | tf_op jit(solution)/shard_map/gather | solution.py:145
  217.6 5.8 %convert_bitcast_fusion = bf16[24,128,512]{1,2,0:T(8,128)(2,1)} fusion(bf16[24,128,128]{2,1,0:T(8,128)(2,1)} %param.15, bf16[24,128,512]{2,1,0:T(8,128)(2,1)S(1)} %copy-done.3, bf16[24,512,128]{2,1,0:T(8,128)(2,1)} %bitcast.130, bf16[24,128,128]{2,1,0:T(8,128)(2,1)} %param.16), kind=kOutput, calls=%fused_computation.13 | convolution fusion | flops 811597824 | bytes 11010048 | tf_op jit(solution)/shard_map/nij,nir->njr/dot_general | solution.py:16
  223.5 4.8 %copy.147 = bf16[24,128,512]{2,1,0:T(8,128)(2,1)} copy(bf16[24,128,512]{1,2,0:T(8,128)(2,1)} %convert_bitcast_fusion) | data formatting | bytes 6291456
  228.3 2.3 copy.149
  230.5 2.0 copy.150
  (110 shorter events, 36.2 us)
Async XLA Ops:
  7.2 8.2 %copy-start = (bf16[24,128,512]{2,1,0:T(8,128)(2,1)S(1)}, bf16[24,128,512]{2,1,0:T(8,128)(2,1)}, u32[]{:S(2)}) copy-start(bf16[24,128,512]{2,1,0:T(8,128)(2,1)} %param.14) | copy-start | bytes 9437188
  7.2 99.9 %all-gather.3.cloned.1.call-start = ((), (), s32[]{:S(2)}) async-start(), calls=%async_computation.2 | async-start | bytes 2359296 | tf_op jit(solution)/shard_map/all_gather | solution.py:78
  8.9 22.0 %collective-permute-start.6 = (bf16[2,128,128]{2,1,0:T(8,128)(2,1)S(1)}, bf16[2,128,128]{2,1,0:T(8,128)(2,1)S(1)}, u32[]{:S(2)}, u32[]{:S(2)}) collective-permute-start(bf16[2,128,128]{2,1,0:T(8,128)(2,1)S(1)} %constant_dynamic-update-slice_fusion), channel_id=1, source_target_pairs={{0,1},{1,2},{2,3},{3,0},{4,5},{5,6},{6,7},{7,4},{8,9},{9,10},{10,1... | collective-permute-start | bytes 196616 | tf_op jit(solution)/shard_map/ppermute | solution.py:76
  11.0 21.6 %collective-permute-start.7 = (bf16[2,128,128]{2,1,0:T(8,128)(2,1)S(1)}, bf16[2,128,128]{2,1,0:T(8,128)(2,1)S(1)}, u32[]{:S(2)}, u32[]{:S(2)}) collective-permute-start(bf16[2,128,128]{2,1,0:T(8,128)(2,1)S(1)} %constant_dynamic-update-slice_fusion), channel_id=1, source_target_pairs={{0,2},{1,3},{2,0},{3,1},{4,6},{5,7},{6,4},{7,5},{8,10},{9,11},{10,... | collective-permute-start | bytes 196616 | tf_op jit(solution)/shard_map/ppermute | solution.py:76
  13.7 18.9 %collective-permute-start.8 = (bf16[2,128,128]{2,1,0:T(8,128)(2,1)S(1)}, bf16[2,128,128]{2,1,0:T(8,128)(2,1)S(1)}, u32[]{:S(2)}, u32[]{:S(2)}) collective-permute-start(bf16[2,128,128]{2,1,0:T(8,128)(2,1)S(1)} %constant_dynamic-update-slice_fusion), channel_id=1, source_target_pairs={{0,3},{1,0},{2,1},{3,2},{4,7},{5,4},{6,5},{7,6},{8,11},{9,8},{10,9... | collective-permute-start | bytes 196616 | tf_op jit(solution)/shard_map/ppermute | solution.py:76
  15.4 2.2 copy-start.6
  17.6 1.7 copy-start.2
  24.0 6.9 %copy-start.4 = (bf16[16,512,128]{2,0,1:T(8,128)(2,1)}, bf16[16,512,128]{2,0,1:T(8,128)(2,1)S(1)}, u32[]{:S(2)}) copy-start(bf16[16,512,128]{2,0,1:T(8,128)(2,1)S(1)} %add_convert_fusion) | copy-start | bytes 6291460
  25.4 24.4 %collective-permute-start.3 = (bf16[8,16,16,128]{3,1,2,0:T(8,128)(2,1)}, bf16[8,16,16,128]{3,1,2,0:T(8,128)(2,1)}, u32[]{:S(2)}, u32[]{:S(2)}) collective-permute-start(bf16[8,16,16,128]{3,1,2,0:T(8,128)(2,1)} %get-tuple-element.34), channel_id=1, source_target_pairs={{0,1},{1,2},{2,3},{3,0},{4,5},{5,6},{6,7},{7,4},{8,9},{9,10},{10,1... | collective-permute-start | bytes 1572872 | tf_op jit(solution)/shard_map/ppermute | solution.py:98
  25.8 26.1 %collective-permute-start.4 = (bf16[8,16,16,128]{3,1,2,0:T(8,128)(2,1)}, bf16[8,16,16,128]{3,1,2,0:T(8,128)(2,1)}, u32[]{:S(2)}, u32[]{:S(2)}) collective-permute-start(bf16[8,16,16,128]{3,1,2,0:T(8,128)(2,1)} %get-tuple-element.35), channel_id=1, source_target_pairs={{0,2},{1,3},{2,0},{3,1},{4,6},{5,7},{6,4},{7,5},{8,10},{9,11},{10,... | collective-permute-start | bytes 1572872 | tf_op jit(solution)/shard_map/ppermute | solution.py:98
  30.9 21.3 %collective-permute-start.5 = (bf16[8,16,16,128]{3,1,2,0:T(8,128)(2,1)}, bf16[8,16,16,128]{3,1,2,0:T(8,128)(2,1)}, u32[]{:S(2)}, u32[]{:S(2)}) collective-permute-start(bf16[8,16,16,128]{3,1,2,0:T(8,128)(2,1)} %get-tuple-element.36), channel_id=1, source_target_pairs={{0,3},{1,0},{2,1},{3,2},{4,7},{5,4},{6,5},{7,6},{8,11},{9,8},{10,9... | collective-permute-start | bytes 1572872 | tf_op jit(solution)/shard_map/ppermute | solution.py:98
  35.7 6.1 %copy-start.10 = (bf16[1,128,512]{2,1,0:T(8,128)(2,1)S(1)}, bf16[1,128,512]{2,1,0:T(8,128)(2,1)}, u32[]{:S(2)}) copy-start(bf16[1,128,512]{2,1,0:T(8,128)(2,1)} %param.18) | copy-start | bytes 393220
  45.8 17.6 %collective-permute-start = (bf16[8,17,16,128]{3,2,1,0:T(8,128)(2,1)}, bf16[8,17,16,128]{3,2,1,0:T(8,128)(2,1)S(1)}, u32[]{:S(2)}, u32[]{:S(2)}) collective-permute-start(bf16[8,17,16,128]{3,2,1,0:T(8,128)(2,1)} %bitcast.127), channel_id=1, source_target_pairs={{0,1},{1,2},{2,3},{3,0},{4,5},{5,6},{6,7},{7,4},{8,9},{9,10},{10,1... | collective-permute-start | bytes 1671176 | tf_op jit(solution)/shard_map/ppermute | solution.py:98
  47.2 25.7 %collective-permute-start.1 = (bf16[8,17,16,128]{3,2,1,0:T(8,128)(2,1)}, bf16[8,17,16,128]{3,2,1,0:T(8,128)(2,1)S(1)}, u32[]{:S(2)}, u32[]{:S(2)}) collective-permute-start(bf16[8,17,16,128]{3,2,1,0:T(8,128)(2,1)} %bitcast.126), channel_id=1, source_target_pairs={{0,2},{1,3},{2,0},{3,1},{4,6},{5,7},{6,4},{7,5},{8,10},{9,11},{10,... | collective-permute-start | bytes 1671176 | tf_op jit(solution)/shard_map/ppermute | solution.py:98
  49.8 25.6 %collective-permute-start.2 = (bf16[8,17,16,128]{3,2,1,0:T(8,128)(2,1)}, bf16[8,17,16,128]{3,2,1,0:T(8,128)(2,1)S(1)}, u32[]{:S(2)}, u32[]{:S(2)}) collective-permute-start(bf16[8,17,16,128]{3,2,1,0:T(8,128)(2,1)} %bitcast.125), channel_id=1, source_target_pairs={{0,3},{1,0},{2,1},{3,2},{4,7},{5,4},{6,5},{7,6},{8,11},{9,8},{10,9... | collective-permute-start | bytes 1671176 | tf_op jit(solution)/shard_map/ppermute | solution.py:98
  54.7 35.0 %copy-start.11 = (s32[8]{0:T(128)S(1)}, s32[8]{0:T(128)}, u32[]{:S(2)}) copy-start(s32[8]{0:T(128)} %param.25) | copy-start | bytes 100
  54.7 35.0 %copy-start.12 = (s32[32]{0:T(128)S(1)}, s32[32]{0:T(128)}, u32[]{:S(2)}) copy-start(s32[32]{0:T(128)} %param.21) | copy-start | bytes 388
  54.7 30.1 %all-to-all-start.1 = ((bf16[8,16,16,128]{3,1,2,0:T(8,128)(2,1)}), bf16[8,16,16,128]{3,1,2,0:T(8,128)(2,1)S(1)}, u32[]{:S(2)}, u32[]{:S(2)}) async-start(bf16[8,16,16,128]{3,1,2,0:T(8,128)(2,1)} %fusion.24), calls=%async_computation.1 | async-start | bytes 1048576 | tf_op jit(solution)/shard_map/all_to_all | solution.py:102
  84.8 21.4 %all-to-all-start = ((bf16[8,20,16,128]{3,2,1,0:T(8,128)(2,1)}), bf16[8,20,16,128]{3,2,1,0:T(8,128)(2,1)S(1)}, u32[]{:S(2)}, u32[]{:S(2)}) async-start(bf16[8,20,16,128]{3,2,1,0:T(8,128)(2,1)} %slice_dynamic-update-slice_fusion), calls=%async_computation | async-start | bytes 1310720 | tf_op jit(solution)/shard_map/all_to_all | solution.py:102
  88.4 119.7 %all-gather.5.cloned.1.call-start = ((), (), s32[]{:S(2)}) async-start(), calls=%async_computation.3 | async-start | bytes 6488064 | tf_op jit(solution)/shard_map/all_gather | solution.py:139
  89.6 21.7 %copy-start.7 = (bf16[8,128,128]{2,1,0:T(8,128)(2,1)S(1)}, bf16[8,128,128]{2,1,0:T(8,128)(2,1)}, u32[]{:S(2)}) copy-start(bf16[8,128,128]{2,1,0:T(8,128)(2,1)} %param.23) | copy-start | bytes 786436
  89.8 21.8 %copy-start.8 = (bf16[8,128,128]{2,1,0:T(8,128)(2,1)S(1)}, bf16[8,128,128]{2,1,0:T(8,128)(2,1)}, u32[]{:S(2)}) copy-start(bf16[8,128,128]{2,1,0:T(8,128)(2,1)} %param.24) | copy-start | bytes 786436
  106.8 17.1 %copy-start.9 = (bf16[4,128,128]{2,1,0:T(8,128)(2,1)S(1)}, bf16[4,128,128]{2,1,0:T(8,128)(2,1)}, u32[]{:S(2)}) copy-start(bf16[4,128,128]{2,1,0:T(8,128)(2,1)} %param.27) | copy-start | bytes 393220
  107.1 18.6 %copy-start.5 = (bf16[32,2,128,128]{3,2,0,1:T(8,128)(2,1)S(1)}, bf16[32,2,128,128]{3,2,0,1:T(8,128)(2,1)}, u32[]{:S(2)}) copy-start(bf16[32,2,128,128]{3,2,0,1:T(8,128)(2,1)} %all-gather.3.cloned.1.call-done) | copy-start | bytes 6291460
  112.0 4.7 %collective-permute-start.9 = (f32[4,16,128]{2,0,1:T(4,128)S(1)}, f32[4,16,128]{2,0,1:T(4,128)S(1)}, u32[]{:S(2)}, u32[]{:S(2)}) collective-permute-start(f32[4,16,128]{2,0,1:T(4,128)S(1)} %fusion.31), channel_id=1, source_target_pairs={{0,32},{32,0},{64,96},{96,64},{128,160},{160,128},{192,224},{224,1... | collective-permute-start | bytes 98312 | tf_op jit(solution)/shard_map/ppermute | solution.py:118
  116.7 2.9 %collective-permute-start.10 = (f32[4,16,128]{2,0,1:T(4,128)S(1)}, f32[4,16,128]{2,0,1:T(4,128)S(1)}, u32[]{:S(2)}, u32[]{:S(2)}) collective-permute-start(f32[4,16,128]{2,0,1:T(4,128)S(1)} %add.176), channel_id=1, source_target_pairs={{0,64},{32,96},{64,0},{96,32},{128,192},{160,224},{192,128},{224,1... | collective-permute-start | bytes 98312 | tf_op jit(solution)/shard_map/ppermute | solution.py:118
  119.6 4.4 %collective-permute-start.11 = (f32[4,16,128]{2,0,1:T(4,128)S(1)}, f32[4,16,128]{2,0,1:T(4,128)S(1)}, u32[]{:S(2)}, u32[]{:S(2)}) collective-permute-start(f32[4,16,128]{2,0,1:T(4,128)S(1)} %add.177), channel_id=1, source_target_pairs={{0,128},{32,160},{64,192},{96,224},{128,0},{160,32},{192,64},{224,... | collective-permute-start | bytes 98312 | tf_op jit(solution)/shard_map/ppermute | solution.py:118
  126.4 7.9 %collective-permute-start.12 = (bf16[44,16,128]{2,1,0:T(8,128)(2,1)S(1)}, bf16[44,16,128]{2,1,0:T(8,128)(2,1)S(1)}, u32[]{:S(2)}, u32[]{:S(2)}) collective-permute-start(bf16[44,16,128]{2,1,0:T(8,128)(2,1)S(1)} %get-tuple-element.38), channel_id=1, source_target_pairs={{0,1},{1,2},{2,3},{3,0},{4,5},{5,6},{6,7},{7,4},{8,9},{9,10},{10,1... | collective-permute-start | bytes 540680 | tf_op jit(solution)/shard_map/ppermute | solution.py:137
  127.0 11.4 %collective-permute-start.13 = (bf16[44,16,128]{2,1,0:T(8,128)(2,1)S(1)}, bf16[44,16,128]{2,1,0:T(8,128)(2,1)S(1)}, u32[]{:S(2)}, u32[]{:S(2)}) collective-permute-start(bf16[44,16,128]{2,1,0:T(8,128)(2,1)S(1)} %get-tuple-element.38), channel_id=1, source_target_pairs={{0,2},{1,3},{2,0},{3,1},{4,6},{5,7},{6,4},{7,5},{8,10},{9,11},{10,... | collective-permute-start | bytes 540680 | tf_op jit(solution)/shard_map/ppermute | solution.py:137
  132.6 5.8 %collective-permute-start.14 = (bf16[44,16,128]{2,1,0:T(8,128)(2,1)S(1)}, bf16[44,16,128]{2,1,0:T(8,128)(2,1)S(1)}, u32[]{:S(2)}, u32[]{:S(2)}) collective-permute-start(bf16[44,16,128]{2,1,0:T(8,128)(2,1)S(1)} %get-tuple-element.38), channel_id=1, source_target_pairs={{0,3},{1,0},{2,1},{3,2},{4,7},{5,4},{6,5},{7,6},{8,11},{9,8},{10,9... | collective-permute-start | bytes 540680 | tf_op jit(solution)/shard_map/ppermute | solution.py:137
  211.9 5.7 %copy-start.3 = (bf16[24,128,512]{2,1,0:T(8,128)(2,1)S(1)}, bf16[24,128,512]{2,1,0:T(8,128)(2,1)}, u32[]{:S(2)}) copy-start(bf16[24,128,512]{2,1,0:T(8,128)(2,1)} %copy-done.2) | copy-start | bytes 9437188
  223.5 10.8 %copy-start.1 = (bf16[24,128,512]{2,1,0:T(8,128)(2,1)S(1)}, bf16[24,128,512]{2,1,0:T(8,128)(2,1)}, u32[]{:S(2)}) copy-start(bf16[24,128,512]{2,1,0:T(8,128)(2,1)} %param.14) | copy-start | bytes 9437188
Sparse Core Ops, SparseCore 0:
  35.8 51.7 all-gather.2
  140.3 67.7 all-gather.4

commit v9 on v8

--- a/solution.py
+++ b/solution.py
@@ -1,6 +1,7 @@
 import jax
 import jax.numpy as jnp
 from jax import lax
+from jax.experimental import pallas as pl
 from jax.sharding import Mesh
 from jax.sharding import PartitionSpec as P
 
@@ -37,6 +38,45 @@
     low = (values - high.astype(jnp.float32)).astype(jnp.bfloat16)
     total = jnp.einsum("sk,k...->s...", select, high, preferred_element_type=jnp.float32)
     return total + jnp.einsum("sk,k...->s...", select, low, preferred_element_type=jnp.float32)
+
+
+def leaf_backward_kernel(parent_ref, solved_ref, link_t_ref, inverse_t_ref, out_ref):
+    for k in range(parent_ref.shape[0]):
+        pieces = parent_ref[k]
+        parent_t = pieces.reshape(pieces.shape[0] * pieces.shape[1], pieces.shape[2])
+        correction = lax.dot_general(
+            link_t_ref[k], parent_t, (((1,), (1,)), ((), ())), preferred_element_type=jnp.float32
+        )
+        w = (solved_ref[k].astype(jnp.float32) - correction).astype(jnp.bfloat16)
+        out_ref[k] = jnp.dot(inverse_t_ref[k], w, preferred_element_type=jnp.float32).astype(out_ref.dtype)
+
+
+def leaf_backward(parents, leaf_solved, leaf_link, leaf_inverse):
+    count, width, columns = leaf_solved.shape
+    per_step = max(d for d in range(1, 5) if count % d == 0)
+    pieces = parents.shape[1:]
+
+    def own(step):
+        return (step, 0, 0)
+
+    cost = pl.CostEstimate(
+        flops=4 * count * width * width * columns,
+        transcendentals=0,
+        bytes_accessed=2 * count * (3 * width * columns + 2 * width * width),
+    )
+    return pl.pallas_call(
+        leaf_backward_kernel,
+        grid=(count // per_step,),
+        in_specs=[
+            pl.BlockSpec((per_step, *pieces), lambda step: (step, 0, 0, 0)),
+            pl.BlockSpec((per_step, width, columns), own),
+            pl.BlockSpec((per_step, width, width), own),
+            pl.BlockSpec((per_step, width, width), own),
+        ],
+        out_specs=pl.BlockSpec((per_step, width, columns), own),
+        out_shape=jax.ShapeDtypeStruct(leaf_solved.shape, jnp.bfloat16),
+        cost_estimate=cost,
+    )(parents, leaf_solved, leaf_link.transpose(0, 2, 1), leaf_inverse.transpose(0, 2, 1))
 
 
 def local(
@@ -142,10 +182,8 @@
     top_result = upper[middle_count:]
     node_result = lax.dynamic_index_in_dim(gathered, col_index, 1).transpose(1, 3, 0, 2).reshape(1, width, columns)
 
-    parent_t = gathered[:, leaf_target].transpose(1, 0, 2, 3).reshape(leaf_target.shape[0], columns, width)
-    correction = jnp.einsum("kij,kci->kjc", leaf_link, parent_t, preferred_element_type=jnp.float32)
-    leaf_w = (leaf_solved.astype(jnp.float32) - correction).astype(jnp.bfloat16)
-    leaf_result = apply_transposed(leaf_inverse, leaf_w).astype(jnp.bfloat16)
+    parents = gathered[:, leaf_target].transpose(1, 0, 2, 3)
+    leaf_result = leaf_backward(parents, leaf_solved, leaf_link, leaf_inverse)
     return (leaf_result, node_result, middle_result, top_result)
 
 

time: 242 us -> 236 us (0.975)
  Pallas kernels: 0 us -> 9.18 us
  local copies, waits for them, and re-layouts: 35.1 us -> 28.7 us
  matrix products: 30.5 us -> 24.6 us
    pallas_call x0 -> x1, Pallas kernels: none -> 9.18 us  [leaf_backward(): pl.pallas_call(leaf_backward_kernel, grid=(count // per_step,), in_specs=...]
    dot_general x1 -> x0, matrix products: 5.83 us -> none  [apply_transposed(): jnp.einsum('nij,nir->njr', matrix, vectors, preferred_element_type=jnp.fl...]
    unnamed x41 -> x44, local copies, waits for them, and re-layouts: 16 us -> 11.6 us
  transfers between devices with their start and end apart: 19 -> 19, of which waited for: 11 -> 11; matrix products, arithmetic and copies ran while one was open for 16% -> 18% of each run, Pallas kernels for 0% -> 0%
where the time goes in v9:
time: 236 us
  waiting for transfers between devices  109 us (46%)
  starting transfers between devices  38.7 us (16%)
  local copies, waits for them, and re-layouts  28.7 us (12%)
  matrix products  24.6 us (10%)
  between operations  14.5 us (6%)
  other arithmetic  10.7 us (5%)
  Pallas kernels  9.18 us (4%)
    all_gather x1, waiting for transfers between devices, local(): gathered = lax.all_gather(by_y, 'z', axis=0, tiled=True)  65.7 us
    all_to_all x2, waiting for transfers between devices, local(): incoming = lax.all_to_all(partial, 'z', 0, 0, tiled=True)  22.3 us
    ppermute x6, waiting for transfers between devices, local(): arrivals.append(lax.ppermute(outbound, 'y', pairs))  12.5 us
    all_to_all x2, starting transfers between devices, local(): incoming = lax.all_to_all(partial, 'z', 0, 0, tiled=True)  11.9 us
    unnamed x44, local copies, waits for them, and re-layouts  11.6 us
    pallas_call x1, Pallas kernels, leaf_backward(): pl.pallas_call(leaf_backward_kernel, grid=(count // per_step,), in_specs=...  9.18 us
    dot_general x2, matrix products, split_slot_sums(): jnp.einsum('sk,k...->s...', select, high, preferred_element_type=jnp.floa...  8.46 us
    ppermute x3, starting transfers between devices, local(): lax.ppermute(top_sum, ROW, [(i, i ^ step) for i in range(rows)])  7.7 us
  transfers between devices with their start and end apart: 19, of which 11 were waited for; matrix products, arithmetic and copies ran while one was open for 18% of the time, Pallas kernels for 0%

profile of v9, /device:TPU:1, one launch (start us, length us, event | category | flops | bytes accessed | tf_op | source)
XLA Modules:
  0.0 235.8 jit_solution(585884689937969200)
XLA Ops:
  8.9 2.1 collective-permute-start.6
  11.0 2.6 %collective-permute-start.7 = (bf16[2,128,128]{2,1,0:T(8,128)(2,1)S(1)}, bf16[2,128,128]{2,1,0:T(8,128)(2,1)S(1)}, u32[]{:S(2)}, u32[]{:S(2)}) collective-permute-start(bf16[2,128,128]{2,1,0:T(8,128)(2,1)S(1)} %constant_dynamic-update-slice_fusion), channel_id=1, source_target_pairs={{0,2},{1,3},{2,0},{3,1},{4,6},{5,7},{6,4},{7,5},{8,10},{9,11},{10,... | collective-permute-start | bytes 196616 | tf_op jit(solution)/shard_map/ppermute | solution.py:116
  15.4 2.2 convolution_convert_fusion.solved_ref
  19.3 2.3 fusion
  21.5 2.5 %add_convert_fusion = bf16[16,512,128]{2,0,1:T(8,128)(2,1)S(1)} fusion(f32[16,512,128]{2,0,1:T(8,128)S(1)} %fusion, bf16[24,512,128]{2,1,0:T(8,128)(2,1)S(1)} %get-tuple-element.28, s32[24]{0:T(128)S(1)} %get-tuple-element.25), kind=kOutput, calls=%fused_computation.7 | convolution fusion | flops 52429184 | bytes 9437280 | tf_op jit(solution)/shard_map/sk,k...->s.../dot_general | solution.py:39
  26.6 4.2 %fusion.2 = f32[16,512,128]{2,0,1:T(8,128)} fusion(bf16[24,512,128]{2,1,0:T(8,128)(2,1)S(1)} %get-tuple-element.29, s32[24]{0:T(128)S(1)} %broadcast_add_fusion), kind=kOutput, calls=%fused_computation.12 | convolution fusion | flops 50332032 | bytes 7340128 | tf_op jit(solution)/shard_map/sk,k...->s.../dot_general | solution.py:40
  30.9 1.7 collective-permute-start.5
  33.3 1.5 gather_fusion.1
  35.7 6.0 %add_convert_fusion.1 = bf16[16,512,128]{2,0,1:T(8,128)(2,1)} fusion(f32[16,512,128]{2,0,1:T(8,128)} %fusion.2, bf16[24,512,128]{2,1,0:T(8,128)(2,1)S(1)} %get-tuple-element.28, s32[24]{0:T(128)S(1)} %broadcast_add_fusion), kind=kOutput, calls=%fused_computation.8 | convolution fusion | flops 52429184 | bytes 9437280 | tf_op jit(solution)/shard_map/sk,k...->s.../dot_general | solution.py:39
  41.9 2.3 pad_maximum_fusion
  47.1 1.8 collective-permute-start.1
  49.7 2.1 collective-permute-start.2
  52.2 2.6 %fusion.17 = bf16[8,16,16,128]{3,1,2,0:T(8,128)(2,1)} fusion(bf16[8,16,16,128]{3,1,2,0:T(8,128)(2,1)} %collective-permute-done.5, bf16[8,16,16,128]{3,1,2,0:T(8,128)(2,1)} %collective-permute-done.4, bf16[8,16,16,128]{3,1,2,0:T(8,128)(2,1)} %collective-permute-done.3, bf16[16,8,4,16,128]{4,0,3,2,1:T(8,128)(2,1)} %bitcast.120, s32[]{:T(128)S(6)} %select_n.125), kind=kLoop, calls=%fused_computation.37 | loop fusion | flops 2097152 | bytes 2621444 | tf_op jit(solution)/shard_map/convert_element_type | solution.py:139
  54.8 8.3 %all-to-all-start.1 = ((bf16[8,16,16,128]{3,1,2,0:T(8,128)(2,1)}), bf16[8,16,16,128]{3,1,2,0:T(8,128)(2,1)S(1)}, u32[]{:S(2)}, u32[]{:S(2)}) async-start(bf16[8,16,16,128]{3,1,2,0:T(8,128)(2,1)} %fusion.17), calls=%async_computation.1 | async-start | bytes 1048576 | tf_op jit(solution)/shard_map/all_to_all | solution.py:142
  63.5 9.5 %collective-permute-done.1 = bf16[8,17,16,128]{3,2,1,0:T(8,128)(2,1)S(1)} collective-permute-done((bf16[8,17,16,128]{3,2,1,0:T(8,128)(2,1)}, bf16[8,17,16,128]{3,2,1,0:T(8,128)(2,1)S(1)}, u32[]{:S(2)}, u32[]{:S(2)}) %collective-permute-start.1) | collective-permute-done | bytes 557088 | tf_op jit(solution)/shard_map/ppermute | solution.py:138
  73.0 2.4 %collective-permute-done.2 = bf16[8,17,16,128]{3,2,1,0:T(8,128)(2,1)S(1)} collective-permute-done((bf16[8,17,16,128]{3,2,1,0:T(8,128)(2,1)}, bf16[8,17,16,128]{3,2,1,0:T(8,128)(2,1)S(1)}, u32[]{:S(2)}, u32[]{:S(2)}) %collective-permute-start.2) | collective-permute-done | bytes 557088 | tf_op jit(solution)/shard_map/ppermute | solution.py:138
  78.9 6.0 %all-to-all-done.1 = bf16[8,16,16,128]{3,1,2,0:T(8,128)(2,1)S(1)} async-done(((bf16[8,16,16,128]{3,1,2,0:T(8,128)(2,1)}), bf16[8,16,16,128]{3,1,2,0:T(8,128)(2,1)S(1)}, u32[]{:S(2)}, u32[]{:S(2)}) %all-to-all-start.1) | async-done | bytes 524320 | tf_op jit(solution)/shard_map/all_to_all | solution.py:142
  84.9 3.5 %all-to-all-start = ((bf16[8,20,16,128]{3,2,1,0:T(8,128)(2,1)}), bf16[8,20,16,128]{3,2,1,0:T(8,128)(2,1)S(1)}, u32[]{:S(2)}, u32[]{:S(2)}) async-start(bf16[8,20,16,128]{3,2,1,0:T(8,128)(2,1)} %slice_dynamic-update-slice_fusion), calls=%async_computation | async-start | bytes 1310720 | tf_op jit(solution)/shard_map/all_to_all | solution.py:142
  89.9 16.3 %all-to-all-done = bf16[8,20,16,128]{3,2,1,0:T(8,128)(2,1)S(1)} async-done(((bf16[8,20,16,128]{3,2,1,0:T(8,128)(2,1)}), bf16[8,20,16,128]{3,2,1,0:T(8,128)(2,1)S(1)}, u32[]{:S(2)}, u32[]{:S(2)}) %all-to-all-start) | async-done | bytes 655392 | tf_op jit(solution)/shard_map/all_to_all | solution.py:142
  107.2 2.0 convolution_convert_fusion.2
  109.2 1.9 fusion.18
  112.1 3.7 %collective-permute-start.9 = (f32[4,16,128]{2,0,1:T(4,128)S(1)}, f32[4,16,128]{2,0,1:T(4,128)S(1)}, u32[]{:S(2)}, u32[]{:S(2)}) collective-permute-start(f32[4,16,128]{2,0,1:T(4,128)S(1)} %fusion.24), channel_id=1, source_target_pairs={{0,32},{32,0},{64,96},{96,64},{128,160},{160,128},{192,224},{224,1... | collective-permute-start | bytes 98312 | tf_op jit(solution)/shard_map/ppermute | solution.py:158
  118.0 1.6 collective-permute-done.10
  119.6 2.8 %collective-permute-start.11 = (f32[4,16,128]{2,0,1:T(4,128)S(1)}, f32[4,16,128]{2,0,1:T(4,128)S(1)}, u32[]{:S(2)}, u32[]{:S(2)}) collective-permute-start(f32[4,16,128]{2,0,1:T(4,128)S(1)} %add.177), channel_id=1, source_target_pairs={{0,128},{32,160},{64,192},{96,224},{128,0},{160,32},{192,64},{224,... | collective-permute-start | bytes 98312 | tf_op jit(solution)/shard_map/ppermute | solution.py:158
  122.5 1.5 collective-permute-done.11
  127.1 5.5 %collective-permute-start.13 = (bf16[44,16,128]{2,1,0:T(8,128)(2,1)S(1)}, bf16[44,16,128]{2,1,0:T(8,128)(2,1)S(1)}, u32[]{:S(2)}, u32[]{:S(2)}) collective-permute-start(bf16[44,16,128]{2,1,0:T(8,128)(2,1)S(1)} %get-tuple-element.38), channel_id=1, source_target_pairs={{0,2},{1,3},{2,0},{3,1},{4,6},{5,7},{6,4},{7,5},{8,10},{9,11},{10,... | collective-permute-start | bytes 540680 | tf_op jit(solution)/shard_map/ppermute | solution.py:177
  132.5 1.7 collective-permute-done.12
  134.2 4.1 %collective-permute-done.13 = bf16[44,16,128]{2,1,0:T(8,128)(2,1)S(1)} collective-permute-done((bf16[44,16,128]{2,1,0:T(8,128)(2,1)S(1)}, bf16[44,16,128]{2,1,0:T(8,128)(2,1)S(1)}, u32[]{:S(2)}, u32[]{:S(2)}) %collective-permute-start.13) | collective-permute-done | bytes 180256 | tf_op jit(solution)/shard_map/ppermute | solution.py:177
  142.5 65.7 %all-gather.5.cloned.1.call-done = bf16[32,44,16,128]{3,2,1,0:T(8,128)(2,1)} async-done(((bf16[4,44,16,128]{3,2,1,0:T(8,128)(2,1)}), bf16[32,44,16,128]{3,2,1,0:T(8,128)(2,1)}) %all-gather.5.cloned.1.call-update) | async-done | bytes 5767184 | tf_op jit(solution)/shard_map/all_gather | solution.py:179
  208.2 1.8 copy_bitcast_fusion
  214.2 5.5 %gather_fusion.5 = bf16[24,32,16,128]{3,2,1,0:T(8,128)(2,1)} fusion(bf16[32,44,16,128]{3,2,1,0:T(8,128)(2,1)} %all-gather.5.cloned.1.call-done, s32[1024]{0:T(1024)S(1)} %pad_clamp_fusion), kind=kCustom, calls=%fused_computation.5 | custom fusion | bytes 6291552 | tf_op jit(solution)/shard_map/gather | solution.py:185
  219.7 9.2 %shard_map.165 = bf16[24,128,512]{2,1,0:T(8,128)(2,1)} custom-call(bf16[24,32,16,128]{3,2,1,0:T(8,128)(2,1)} %gather_fusion.5, bf16[24,128,512]{2,1,0:T(8,128)(2,1)} %copy-done.2, bf16[24,128,128]{2,1,0:T(8,128)(2,1)} %bitcast.122, bf16[24,128,128]{2,1,0:T(8,128)(2,1)} %bitcast.123), custom_call_target="tpu_custom_call" | custom-call | flops 805306368 | bytes 11010048 | tf_op jit(solution)/shard_map/pallas_call | solution.py:67
  (113 shorter events, 34.6 us)
Async XLA Ops:
  7.2 8.2 %copy-start = (bf16[24,128,512]{2,1,0:T(8,128)(2,1)S(1)}, bf16[24,128,512]{2,1,0:T(8,128)(2,1)}, u32[]{:S(2)}) copy-start(bf16[24,128,512]{2,1,0:T(8,128)(2,1)} %param.14) | copy-start | bytes 9437188
  7.2 100.0 %all-gather.3.cloned.1.call-start = ((), (), s32[]{:S(2)}) async-start(), calls=%async_computation.2 | async-start | bytes 2359296 | tf_op jit(solution)/shard_map/all_gather | solution.py:118
  8.9 22.0 %collective-permute-start.6 = (bf16[2,128,128]{2,1,0:T(8,128)(2,1)S(1)}, bf16[2,128,128]{2,1,0:T(8,128)(2,1)S(1)}, u32[]{:S(2)}, u32[]{:S(2)}) collective-permute-start(bf16[2,128,128]{2,1,0:T(8,128)(2,1)S(1)} %constant_dynamic-update-slice_fusion), channel_id=1, source_target_pairs={{0,1},{1,2},{2,3},{3,0},{4,5},{5,6},{6,7},{7,4},{8,9},{9,10},{10,1... | collective-permute-start | bytes 196616 | tf_op jit(solution)/shard_map/ppermute | solution.py:116
  11.0 21.5 %collective-permute-start.7 = (bf16[2,128,128]{2,1,0:T(8,128)(2,1)S(1)}, bf16[2,128,128]{2,1,0:T(8,128)(2,1)S(1)}, u32[]{:S(2)}, u32[]{:S(2)}) collective-permute-start(bf16[2,128,128]{2,1,0:T(8,128)(2,1)S(1)} %constant_dynamic-update-slice_fusion), channel_id=1, source_target_pairs={{0,2},{1,3},{2,0},{3,1},{4,6},{5,7},{6,4},{7,5},{8,10},{9,11},{10,... | collective-permute-start | bytes 196616 | tf_op jit(solution)/shard_map/ppermute | solution.py:116
  13.7 18.9 %collective-permute-start.8 = (bf16[2,128,128]{2,1,0:T(8,128)(2,1)S(1)}, bf16[2,128,128]{2,1,0:T(8,128)(2,1)S(1)}, u32[]{:S(2)}, u32[]{:S(2)}) collective-permute-start(bf16[2,128,128]{2,1,0:T(8,128)(2,1)S(1)} %constant_dynamic-update-slice_fusion), channel_id=1, source_target_pairs={{0,3},{1,0},{2,1},{3,2},{4,7},{5,4},{6,5},{7,6},{8,11},{9,8},{10,9... | collective-permute-start | bytes 196616 | tf_op jit(solution)/shard_map/ppermute | solution.py:116
  15.4 2.2 copy-start.5
  24.0 6.9 %copy-start.3 = (bf16[16,512,128]{2,0,1:T(8,128)(2,1)}, bf16[16,512,128]{2,0,1:T(8,128)(2,1)S(1)}, u32[]{:S(2)}) copy-start(bf16[16,512,128]{2,0,1:T(8,128)(2,1)S(1)} %add_convert_fusion) | copy-start | bytes 6291460
  25.4 24.3 %collective-permute-start.3 = (bf16[8,16,16,128]{3,1,2,0:T(8,128)(2,1)}, bf16[8,16,16,128]{3,1,2,0:T(8,128)(2,1)}, u32[]{:S(2)}, u32[]{:S(2)}) collective-permute-start(bf16[8,16,16,128]{3,1,2,0:T(8,128)(2,1)} %get-tuple-element.34), channel_id=1, source_target_pairs={{0,1},{1,2},{2,3},{3,0},{4,5},{5,6},{6,7},{7,4},{8,9},{9,10},{10,1... | collective-permute-start | bytes 1572872 | tf_op jit(solution)/shard_map/ppermute | solution.py:138
  25.8 26.1 %collective-permute-start.4 = (bf16[8,16,16,128]{3,1,2,0:T(8,128)(2,1)}, bf16[8,16,16,128]{3,1,2,0:T(8,128)(2,1)}, u32[]{:S(2)}, u32[]{:S(2)}) collective-permute-start(bf16[8,16,16,128]{3,1,2,0:T(8,128)(2,1)} %get-tuple-element.35), channel_id=1, source_target_pairs={{0,2},{1,3},{2,0},{3,1},{4,6},{5,7},{6,4},{7,5},{8,10},{9,11},{10,... | collective-permute-start | bytes 1572872 | tf_op jit(solution)/shard_map/ppermute | solution.py:138
  30.9 21.3 %collective-permute-start.5 = (bf16[8,16,16,128]{3,1,2,0:T(8,128)(2,1)}, bf16[8,16,16,128]{3,1,2,0:T(8,128)(2,1)}, u32[]{:S(2)}, u32[]{:S(2)}) collective-permute-start(bf16[8,16,16,128]{3,1,2,0:T(8,128)(2,1)} %get-tuple-element.36), channel_id=1, source_target_pairs={{0,3},{1,0},{2,1},{3,2},{4,7},{5,4},{6,5},{7,6},{8,11},{9,8},{10,9... | collective-permute-start | bytes 1572872 | tf_op jit(solution)/shard_map/ppermute | solution.py:138
  35.7 6.0 %copy-start.11 = (bf16[1,128,512]{2,1,0:T(8,128)(2,1)S(1)}, bf16[1,128,512]{2,1,0:T(8,128)(2,1)}, u32[]{:S(2)}) copy-start(bf16[1,128,512]{2,1,0:T(8,128)(2,1)} %param.18) | copy-start | bytes 393220
  45.7 17.8 %collective-permute-start = (bf16[8,17,16,128]{3,2,1,0:T(8,128)(2,1)}, bf16[8,17,16,128]{3,2,1,0:T(8,128)(2,1)S(1)}, u32[]{:S(2)}, u32[]{:S(2)}) collective-permute-start(bf16[8,17,16,128]{3,2,1,0:T(8,128)(2,1)} %bitcast.116), channel_id=1, source_target_pairs={{0,1},{1,2},{2,3},{3,0},{4,5},{5,6},{6,7},{7,4},{8,9},{9,10},{10,1... | collective-permute-start | bytes 1671176 | tf_op jit(solution)/shard_map/ppermute | solution.py:138
  47.1 25.9 %collective-permute-start.1 = (bf16[8,17,16,128]{3,2,1,0:T(8,128)(2,1)}, bf16[8,17,16,128]{3,2,1,0:T(8,128)(2,1)S(1)}, u32[]{:S(2)}, u32[]{:S(2)}) collective-permute-start(bf16[8,17,16,128]{3,2,1,0:T(8,128)(2,1)} %bitcast.115), channel_id=1, source_target_pairs={{0,2},{1,3},{2,0},{3,1},{4,6},{5,7},{6,4},{7,5},{8,10},{9,11},{10,... | collective-permute-start | bytes 1671176 | tf_op jit(solution)/shard_map/ppermute | solution.py:138
  49.7 25.6 %collective-permute-start.2 = (bf16[8,17,16,128]{3,2,1,0:T(8,128)(2,1)}, bf16[8,17,16,128]{3,2,1,0:T(8,128)(2,1)S(1)}, u32[]{:S(2)}, u32[]{:S(2)}) collective-permute-start(bf16[8,17,16,128]{3,2,1,0:T(8,128)(2,1)} %bitcast.114), channel_id=1, source_target_pairs={{0,3},{1,0},{2,1},{3,2},{4,7},{5,4},{6,5},{7,6},{8,11},{9,8},{10,9... | collective-permute-start | bytes 1671176 | tf_op jit(solution)/shard_map/ppermute | solution.py:138
  54.8 35.0 %copy-start.12 = (s32[8]{0:T(128)S(1)}, s32[8]{0:T(128)}, u32[]{:S(2)}) copy-start(s32[8]{0:T(128)} %param.25) | copy-start | bytes 100
  54.8 35.0 %copy-start.13 = (s32[32]{0:T(128)S(1)}, s32[32]{0:T(128)}, u32[]{:S(2)}) copy-start(s32[32]{0:T(128)} %param.21) | copy-start | bytes 388
  54.8 30.1 %all-to-all-start.1 = ((bf16[8,16,16,128]{3,1,2,0:T(8,128)(2,1)}), bf16[8,16,16,128]{3,1,2,0:T(8,128)(2,1)S(1)}, u32[]{:S(2)}, u32[]{:S(2)}) async-start(bf16[8,16,16,128]{3,1,2,0:T(8,128)(2,1)} %fusion.17), calls=%async_computation.1 | async-start | bytes 1048576 | tf_op jit(solution)/shard_map/all_to_all | solution.py:142
  84.9 21.4 %all-to-all-start = ((bf16[8,20,16,128]{3,2,1,0:T(8,128)(2,1)}), bf16[8,20,16,128]{3,2,1,0:T(8,128)(2,1)S(1)}, u32[]{:S(2)}, u32[]{:S(2)}) async-start(bf16[8,20,16,128]{3,2,1,0:T(8,128)(2,1)} %slice_dynamic-update-slice_fusion), calls=%async_computation | async-start | bytes 1310720 | tf_op jit(solution)/shard_map/all_to_all | solution.py:142
  88.4 119.8 %all-gather.5.cloned.1.call-start = ((), (), s32[]{:S(2)}) async-start(), calls=%async_computation.3 | async-start | bytes 6488064 | tf_op jit(solution)/shard_map/all_gather | solution.py:179
  89.7 21.7 %copy-start.8 = (bf16[8,128,128]{2,1,0:T(8,128)(2,1)S(1)}, bf16[8,128,128]{2,1,0:T(8,128)(2,1)}, u32[]{:S(2)}) copy-start(bf16[8,128,128]{2,1,0:T(8,128)(2,1)} %param.23) | copy-start | bytes 786436
  89.9 21.8 %copy-start.9 = (bf16[8,128,128]{2,1,0:T(8,128)(2,1)S(1)}, bf16[8,128,128]{2,1,0:T(8,128)(2,1)}, u32[]{:S(2)}) copy-start(bf16[8,128,128]{2,1,0:T(8,128)(2,1)} %param.24) | copy-start | bytes 786436
  106.9 17.1 %copy-start.10 = (bf16[4,128,128]{2,1,0:T(8,128)(2,1)S(1)}, bf16[4,128,128]{2,1,0:T(8,128)(2,1)}, u32[]{:S(2)}) copy-start(bf16[4,128,128]{2,1,0:T(8,128)(2,1)} %param.27) | copy-start | bytes 393220
  107.2 18.6 %copy-start.4 = (bf16[32,2,128,128]{3,2,0,1:T(8,128)(2,1)S(1)}, bf16[32,2,128,128]{3,2,0,1:T(8,128)(2,1)}, u32[]{:S(2)}) copy-start(bf16[32,2,128,128]{3,2,0,1:T(8,128)(2,1)} %all-gather.3.cloned.1.call-done) | copy-start | bytes 6291460
  112.1 4.7 %collective-permute-start.9 = (f32[4,16,128]{2,0,1:T(4,128)S(1)}, f32[4,16,128]{2,0,1:T(4,128)S(1)}, u32[]{:S(2)}, u32[]{:S(2)}) collective-permute-start(f32[4,16,128]{2,0,1:T(4,128)S(1)} %fusion.24), channel_id=1, source_target_pairs={{0,32},{32,0},{64,96},{96,64},{128,160},{160,128},{192,224},{224,1... | collective-permute-start | bytes 98312 | tf_op jit(solution)/shard_map/ppermute | solution.py:158
  116.8 2.9 %collective-permute-start.10 = (f32[4,16,128]{2,0,1:T(4,128)S(1)}, f32[4,16,128]{2,0,1:T(4,128)S(1)}, u32[]{:S(2)}, u32[]{:S(2)}) collective-permute-start(f32[4,16,128]{2,0,1:T(4,128)S(1)} %add.176), channel_id=1, source_target_pairs={{0,64},{32,96},{64,0},{96,32},{128,192},{160,224},{192,128},{224,1... | collective-permute-start | bytes 98312 | tf_op jit(solution)/shard_map/ppermute | solution.py:158
  119.6 4.4 %collective-permute-start.11 = (f32[4,16,128]{2,0,1:T(4,128)S(1)}, f32[4,16,128]{2,0,1:T(4,128)S(1)}, u32[]{:S(2)}, u32[]{:S(2)}) collective-permute-start(f32[4,16,128]{2,0,1:T(4,128)S(1)} %add.177), channel_id=1, source_target_pairs={{0,128},{32,160},{64,192},{96,224},{128,0},{160,32},{192,64},{224,... | collective-permute-start | bytes 98312 | tf_op jit(solution)/shard_map/ppermute | solution.py:158
  126.4 13.7 %copy-start.6 = (bf16[24,128,128]{2,1,0:T(8,128)(2,1)S(1)}, bf16[24,128,128]{2,1,0:T(8,128)(2,1)}, u32[]{:S(2)}) copy-start(bf16[24,128,128]{2,1,0:T(8,128)(2,1)} %param.16) | copy-start | bytes 2359300
  126.5 7.8 %collective-permute-start.12 = (bf16[44,16,128]{2,1,0:T(8,128)(2,1)S(1)}, bf16[44,16,128]{2,1,0:T(8,128)(2,1)S(1)}, u32[]{:S(2)}, u32[]{:S(2)}) collective-permute-start(bf16[44,16,128]{2,1,0:T(8,128)(2,1)S(1)} %get-tuple-element.38), channel_id=1, source_target_pairs={{0,1},{1,2},{2,3},{3,0},{4,5},{5,6},{6,7},{7,4},{8,9},{9,10},{10,1... | collective-permute-start | bytes 540680 | tf_op jit(solution)/shard_map/ppermute | solution.py:177
  127.1 11.2 %collective-permute-start.13 = (bf16[44,16,128]{2,1,0:T(8,128)(2,1)S(1)}, bf16[44,16,128]{2,1,0:T(8,128)(2,1)S(1)}, u32[]{:S(2)}, u32[]{:S(2)}) collective-permute-start(bf16[44,16,128]{2,1,0:T(8,128)(2,1)S(1)} %get-tuple-element.38), channel_id=1, source_target_pairs={{0,2},{1,3},{2,0},{3,1},{4,6},{5,7},{6,4},{7,5},{8,10},{9,11},{10,... | collective-permute-start | bytes 540680 | tf_op jit(solution)/shard_map/ppermute | solution.py:177
  132.5 5.8 %collective-permute-start.14 = (bf16[44,16,128]{2,1,0:T(8,128)(2,1)S(1)}, bf16[44,16,128]{2,1,0:T(8,128)(2,1)S(1)}, u32[]{:S(2)}, u32[]{:S(2)}) collective-permute-start(bf16[44,16,128]{2,1,0:T(8,128)(2,1)S(1)} %get-tuple-element.38), channel_id=1, source_target_pairs={{0,3},{1,0},{2,1},{3,2},{4,7},{5,4},{6,5},{7,6},{8,11},{9,8},{10,9... | collective-permute-start | bytes 540680 | tf_op jit(solution)/shard_map/ppermute | solution.py:177
  138.3 3.0 %copy-start.7 = (bf16[24,128,128]{2,1,0:T(8,128)(2,1)S(1)}, bf16[24,128,128]{2,1,0:T(8,128)(2,1)}, u32[]{:S(2)}) copy-start(bf16[24,128,128]{2,1,0:T(8,128)(2,1)} %param.15) | copy-start | bytes 2359300
  219.7 9.2 %copy-start.1 = (bf16[24,128,512]{2,1,0:T(8,128)(2,1)S(1)}, bf16[24,128,512]{2,1,0:T(8,128)(2,1)}, u32[]{:S(2)}) copy-start(bf16[24,128,512]{2,1,0:T(8,128)(2,1)} %param.14) | copy-start | bytes 9437188
  (1 other events, 1.7 us)
Sparse Core Ops, SparseCore 0:
  35.8 51.7 all-gather.2
  140.2 67.9 all-gather.4

commit v10 on v9

--- a/solution.py
+++ b/solution.py
@@ -41,7 +41,7 @@
 
 
 def leaf_backward_kernel(parent_ref, solved_ref, link_t_ref, inverse_t_ref, out_ref):
-    for k in range(parent_ref.shape[0]):
+    def one_leaf(k, carry):
         pieces = parent_ref[k]
         parent_t = pieces.reshape(pieces.shape[0] * pieces.shape[1], pieces.shape[2])
         correction = lax.dot_general(
@@ -49,6 +49,9 @@
         )
         w = (solved_ref[k].astype(jnp.float32) - correction).astype(jnp.bfloat16)
         out_ref[k] = jnp.dot(inverse_t_ref[k], w, preferred_element_type=jnp.float32).astype(out_ref.dtype)
+        return carry
+
+    lax.fori_loop(0, parent_ref.shape[0], one_leaf, 0)
 
 
 def leaf_backward(parents, leaf_solved, leaf_link, leaf_inverse):

time: 236 us -> 238 us (level)
  transfers between devices with their start and end apart: 19 -> 19, of which waited for: 11 -> 11; matrix products, arithmetic and copies ran while one was open for 18% -> 17% of each run, Pallas kernels for 0% -> 0%
where the time goes in v10:
time: 238 us; the launch traced here: 237 us
  waiting for transfers between devices  109 us (46%)
  starting transfers between devices  38.7 us (16%)
  local copies, waits for them, and re-layouts  28.7 us (12%)
  matrix products  24.6 us (10%)
  between operations  14.5 us (6%)
  Pallas kernels  10.8 us (5%)
  other arithmetic  10.7 us (4%)
    all_gather x1, waiting for transfers between devices, local(): gathered = lax.all_gather(by_y, 'z', axis=0, tiled=True)  65.7 us
    all_to_all x2, waiting for transfers between devices, local(): incoming = lax.all_to_all(partial, 'z', 0, 0, tiled=True)  22.3 us
    ppermute x6, waiting for transfers between devices, local(): arrivals.append(lax.ppermute(outbound, 'y', pairs))  12.5 us
    all_to_all x2, starting transfers between devices, local(): incoming = lax.all_to_all(partial, 'z', 0, 0, tiled=True)  11.9 us
    unnamed x44, local copies, waits for them, and re-layouts  11.6 us
    pallas_call x1, Pallas kernels, leaf_backward(): pl.pallas_call(leaf_backward_kernel, grid=(count // per_step,), in_specs=...  10.8 us
    dot_general x2, matrix products, split_slot_sums(): jnp.einsum('sk,k...->s...', select, high, preferred_element_type=jnp.floa...  8.46 us
    ppermute x3, starting transfers between devices, local(): lax.ppermute(top_sum, ROW, [(i, i ^ step) for i in range(rows)])  7.7 us
  transfers between devices with their start and end apart: 19, of which 11 were waited for; matrix products, arithmetic and copies ran while one was open for 17% of the time, Pallas kernels for 0%

profile of v10, /device:TPU:1, one launch (start us, length us, event | category | flops | bytes accessed | tf_op | source)
XLA Modules:
  0.0 237.4 jit_solution(16048505998993760628)
XLA Ops:
  8.9 2.1 collective-permute-start.6
  11.0 2.6 %collective-permute-start.7 = (bf16[2,128,128]{2,1,0:T(8,128)(2,1)S(1)}, bf16[2,128,128]{2,1,0:T(8,128)(2,1)S(1)}, u32[]{:S(2)}, u32[]{:S(2)}) collective-permute-start(bf16[2,128,128]{2,1,0:T(8,128)(2,1)S(1)} %constant_dynamic-update-slice_fusion), channel_id=1, source_target_pairs={{0,2},{1,3},{2,0},{3,1},{4,6},{5,7},{6,4},{7,5},{8,10},{9,11},{10,... | collective-permute-start | bytes 196616 | tf_op jit(solution)/shard_map/ppermute | solution.py:119
  15.4 2.2 convolution_convert_fusion.solved_ref
  19.3 2.3 fusion
  21.5 2.5 %add_convert_fusion = bf16[16,512,128]{2,0,1:T(8,128)(2,1)S(1)} fusion(f32[16,512,128]{2,0,1:T(8,128)S(1)} %fusion, bf16[24,512,128]{2,1,0:T(8,128)(2,1)S(1)} %get-tuple-element.28, s32[24]{0:T(128)S(1)} %get-tuple-element.25), kind=kOutput, calls=%fused_computation.7 | convolution fusion | flops 52429184 | bytes 9437280 | tf_op jit(solution)/shard_map/sk,k...->s.../dot_general | solution.py:39
  26.6 4.2 %fusion.2 = f32[16,512,128]{2,0,1:T(8,128)} fusion(bf16[24,512,128]{2,1,0:T(8,128)(2,1)S(1)} %get-tuple-element.29, s32[24]{0:T(128)S(1)} %broadcast_add_fusion), kind=kOutput, calls=%fused_computation.12 | convolution fusion | flops 50332032 | bytes 7340128 | tf_op jit(solution)/shard_map/sk,k...->s.../dot_general | solution.py:40
  30.9 1.7 collective-permute-start.5
  33.3 1.5 gather_fusion.1
  35.7 6.0 %add_convert_fusion.1 = bf16[16,512,128]{2,0,1:T(8,128)(2,1)} fusion(f32[16,512,128]{2,0,1:T(8,128)} %fusion.2, bf16[24,512,128]{2,1,0:T(8,128)(2,1)S(1)} %get-tuple-element.28, s32[24]{0:T(128)S(1)} %broadcast_add_fusion), kind=kOutput, calls=%fused_computation.8 | convolution fusion | flops 52429184 | bytes 9437280 | tf_op jit(solution)/shard_map/sk,k...->s.../dot_general | solution.py:39
  41.9 2.3 pad_maximum_fusion
  47.1 1.8 collective-permute-start.1
  49.7 2.1 collective-permute-start.2
  52.2 2.6 %fusion.17 = bf16[8,16,16,128]{3,1,2,0:T(8,128)(2,1)} fusion(bf16[8,16,16,128]{3,1,2,0:T(8,128)(2,1)} %collective-permute-done.5, bf16[8,16,16,128]{3,1,2,0:T(8,128)(2,1)} %collective-permute-done.4, bf16[8,16,16,128]{3,1,2,0:T(8,128)(2,1)} %collective-permute-done.3, bf16[16,8,4,16,128]{4,0,3,2,1:T(8,128)(2,1)} %bitcast.120, s32[]{:T(128)S(6)} %select_n.125), kind=kLoop, calls=%fused_computation.37 | loop fusion | flops 2097152 | bytes 2621444 | tf_op jit(solution)/shard_map/convert_element_type | solution.py:142
  54.8 8.3 %all-to-all-start.1 = ((bf16[8,16,16,128]{3,1,2,0:T(8,128)(2,1)}), bf16[8,16,16,128]{3,1,2,0:T(8,128)(2,1)S(1)}, u32[]{:S(2)}, u32[]{:S(2)}) async-start(bf16[8,16,16,128]{3,1,2,0:T(8,128)(2,1)} %fusion.17), calls=%async_computation.1 | async-start | bytes 1048576 | tf_op jit(solution)/shard_map/all_to_all | solution.py:145
  63.5 9.5 %collective-permute-done.1 = bf16[8,17,16,128]{3,2,1,0:T(8,128)(2,1)S(1)} collective-permute-done((bf16[8,17,16,128]{3,2,1,0:T(8,128)(2,1)}, bf16[8,17,16,128]{3,2,1,0:T(8,128)(2,1)S(1)}, u32[]{:S(2)}, u32[]{:S(2)}) %collective-permute-start.1) | collective-permute-done | bytes 557088 | tf_op jit(solution)/shard_map/ppermute | solution.py:141
  73.0 2.4 %collective-permute-done.2 = bf16[8,17,16,128]{3,2,1,0:T(8,128)(2,1)S(1)} collective-permute-done((bf16[8,17,16,128]{3,2,1,0:T(8,128)(2,1)}, bf16[8,17,16,128]{3,2,1,0:T(8,128)(2,1)S(1)}, u32[]{:S(2)}, u32[]{:S(2)}) %collective-permute-start.2) | collective-permute-done | bytes 557088 | tf_op jit(solution)/shard_map/ppermute | solution.py:141
  78.9 6.0 %all-to-all-done.1 = bf16[8,16,16,128]{3,1,2,0:T(8,128)(2,1)S(1)} async-done(((bf16[8,16,16,128]{3,1,2,0:T(8,128)(2,1)}), bf16[8,16,16,128]{3,1,2,0:T(8,128)(2,1)S(1)}, u32[]{:S(2)}, u32[]{:S(2)}) %all-to-all-start.1) | async-done | bytes 524320 | tf_op jit(solution)/shard_map/all_to_all | solution.py:145
  84.9 3.5 %all-to-all-start = ((bf16[8,20,16,128]{3,2,1,0:T(8,128)(2,1)}), bf16[8,20,16,128]{3,2,1,0:T(8,128)(2,1)S(1)}, u32[]{:S(2)}, u32[]{:S(2)}) async-start(bf16[8,20,16,128]{3,2,1,0:T(8,128)(2,1)} %slice_dynamic-update-slice_fusion), calls=%async_computation | async-start | bytes 1310720 | tf_op jit(solution)/shard_map/all_to_all | solution.py:145
  89.9 16.3 %all-to-all-done = bf16[8,20,16,128]{3,2,1,0:T(8,128)(2,1)S(1)} async-done(((bf16[8,20,16,128]{3,2,1,0:T(8,128)(2,1)}), bf16[8,20,16,128]{3,2,1,0:T(8,128)(2,1)S(1)}, u32[]{:S(2)}, u32[]{:S(2)}) %all-to-all-start) | async-done | bytes 655392 | tf_op jit(solution)/shard_map/all_to_all | solution.py:145
  107.2 2.0 convolution_convert_fusion.2
  109.2 1.9 fusion.18
  112.1 3.7 %collective-permute-start.9 = (f32[4,16,128]{2,0,1:T(4,128)S(1)}, f32[4,16,128]{2,0,1:T(4,128)S(1)}, u32[]{:S(2)}, u32[]{:S(2)}) collective-permute-start(f32[4,16,128]{2,0,1:T(4,128)S(1)} %fusion.24), channel_id=1, source_target_pairs={{0,32},{32,0},{64,96},{96,64},{128,160},{160,128},{192,224},{224,1... | collective-permute-start | bytes 98312 | tf_op jit(solution)/shard_map/ppermute | solution.py:161
  118.0 1.6 collective-permute-done.10
  119.6 2.8 %collective-permute-start.11 = (f32[4,16,128]{2,0,1:T(4,128)S(1)}, f32[4,16,128]{2,0,1:T(4,128)S(1)}, u32[]{:S(2)}, u32[]{:S(2)}) collective-permute-start(f32[4,16,128]{2,0,1:T(4,128)S(1)} %add.177), channel_id=1, source_target_pairs={{0,128},{32,160},{64,192},{96,224},{128,0},{160,32},{192,64},{224,... | collective-permute-start | bytes 98312 | tf_op jit(solution)/shard_map/ppermute | solution.py:161
  122.5 1.5 collective-permute-done.11
  127.1 5.5 %collective-permute-start.13 = (bf16[44,16,128]{2,1,0:T(8,128)(2,1)S(1)}, bf16[44,16,128]{2,1,0:T(8,128)(2,1)S(1)}, u32[]{:S(2)}, u32[]{:S(2)}) collective-permute-start(bf16[44,16,128]{2,1,0:T(8,128)(2,1)S(1)} %get-tuple-element.38), channel_id=1, source_target_pairs={{0,2},{1,3},{2,0},{3,1},{4,6},{5,7},{6,4},{7,5},{8,10},{9,11},{10,... | collective-permute-start | bytes 540680 | tf_op jit(solution)/shard_map/ppermute | solution.py:180
  132.5 1.7 collective-permute-done.12
  134.2 4.1 %collective-permute-done.13 = bf16[44,16,128]{2,1,0:T(8,128)(2,1)S(1)} collective-permute-done((bf16[44,16,128]{2,1,0:T(8,128)(2,1)S(1)}, bf16[44,16,128]{2,1,0:T(8,128)(2,1)S(1)}, u32[]{:S(2)}, u32[]{:S(2)}) %collective-permute-start.13) | collective-permute-done | bytes 180256 | tf_op jit(solution)/shard_map/ppermute | solution.py:180
  142.5 65.7 %all-gather.5.cloned.1.call-done = bf16[32,44,16,128]{3,2,1,0:T(8,128)(2,1)} async-done(((bf16[4,44,16,128]{3,2,1,0:T(8,128)(2,1)}), bf16[32,44,16,128]{3,2,1,0:T(8,128)(2,1)}) %all-gather.5.cloned.1.call-update) | async-done | bytes 5767184 | tf_op jit(solution)/shard_map/all_gather | solution.py:182
  208.2 1.8 copy_bitcast_fusion
  214.2 5.5 %gather_fusion.5 = bf16[24,32,16,128]{3,2,1,0:T(8,128)(2,1)} fusion(bf16[32,44,16,128]{3,2,1,0:T(8,128)(2,1)} %all-gather.5.cloned.1.call-done, s32[1024]{0:T(1024)S(1)} %pad_clamp_fusion), kind=kCustom, calls=%fused_computation.5 | custom fusion | bytes 6291552 | tf_op jit(solution)/shard_map/gather | solution.py:188
  219.7 10.8 %shard_map.165 = bf16[24,128,512]{2,1,0:T(8,128)(2,1)} custom-call(bf16[24,32,16,128]{3,2,1,0:T(8,128)(2,1)} %gather_fusion.5, bf16[24,128,512]{2,1,0:T(8,128)(2,1)} %copy-done.2, bf16[24,128,128]{2,1,0:T(8,128)(2,1)} %bitcast.122, bf16[24,128,128]{2,1,0:T(8,128)(2,1)} %bitcast.123), custom_call_target="tpu_custom_call" | custom-call | flops 805306368 | bytes 11010048 | tf_op jit(solution)/shard_map/pallas_call | solution.py:70
  (113 shorter events, 34.6 us)
Async XLA Ops:
  7.2 8.2 %copy-start = (bf16[24,128,512]{2,1,0:T(8,128)(2,1)S(1)}, bf16[24,128,512]{2,1,0:T(8,128)(2,1)}, u32[]{:S(2)}) copy-start(bf16[24,128,512]{2,1,0:T(8,128)(2,1)} %param.14) | copy-start | bytes 9437188
  7.2 100.0 %all-gather.3.cloned.1.call-start = ((), (), s32[]{:S(2)}) async-start(), calls=%async_computation.2 | async-start | bytes 2359296 | tf_op jit(solution)/shard_map/all_gather | solution.py:121
  8.9 22.0 %collective-permute-start.6 = (bf16[2,128,128]{2,1,0:T(8,128)(2,1)S(1)}, bf16[2,128,128]{2,1,0:T(8,128)(2,1)S(1)}, u32[]{:S(2)}, u32[]{:S(2)}) collective-permute-start(bf16[2,128,128]{2,1,0:T(8,128)(2,1)S(1)} %constant_dynamic-update-slice_fusion), channel_id=1, source_target_pairs={{0,1},{1,2},{2,3},{3,0},{4,5},{5,6},{6,7},{7,4},{8,9},{9,10},{10,1... | collective-permute-start | bytes 196616 | tf_op jit(solution)/shard_map/ppermute | solution.py:119
  11.0 21.5 %collective-permute-start.7 = (bf16[2,128,128]{2,1,0:T(8,128)(2,1)S(1)}, bf16[2,128,128]{2,1,0:T(8,128)(2,1)S(1)}, u32[]{:S(2)}, u32[]{:S(2)}) collective-permute-start(bf16[2,128,128]{2,1,0:T(8,128)(2,1)S(1)} %constant_dynamic-update-slice_fusion), channel_id=1, source_target_pairs={{0,2},{1,3},{2,0},{3,1},{4,6},{5,7},{6,4},{7,5},{8,10},{9,11},{10,... | collective-permute-start | bytes 196616 | tf_op jit(solution)/shard_map/ppermute | solution.py:119
  13.7 18.9 %collective-permute-start.8 = (bf16[2,128,128]{2,1,0:T(8,128)(2,1)S(1)}, bf16[2,128,128]{2,1,0:T(8,128)(2,1)S(1)}, u32[]{:S(2)}, u32[]{:S(2)}) collective-permute-start(bf16[2,128,128]{2,1,0:T(8,128)(2,1)S(1)} %constant_dynamic-update-slice_fusion), channel_id=1, source_target_pairs={{0,3},{1,0},{2,1},{3,2},{4,7},{5,4},{6,5},{7,6},{8,11},{9,8},{10,9... | collective-permute-start | bytes 196616 | tf_op jit(solution)/shard_map/ppermute | solution.py:119
  15.4 2.2 copy-start.5
  24.0 6.9 %copy-start.3 = (bf16[16,512,128]{2,0,1:T(8,128)(2,1)}, bf16[16,512,128]{2,0,1:T(8,128)(2,1)S(1)}, u32[]{:S(2)}) copy-start(bf16[16,512,128]{2,0,1:T(8,128)(2,1)S(1)} %add_convert_fusion) | copy-start | bytes 6291460
  25.4 24.3 %collective-permute-start.3 = (bf16[8,16,16,128]{3,1,2,0:T(8,128)(2,1)}, bf16[8,16,16,128]{3,1,2,0:T(8,128)(2,1)}, u32[]{:S(2)}, u32[]{:S(2)}) collective-permute-start(bf16[8,16,16,128]{3,1,2,0:T(8,128)(2,1)} %get-tuple-element.34), channel_id=1, source_target_pairs={{0,1},{1,2},{2,3},{3,0},{4,5},{5,6},{6,7},{7,4},{8,9},{9,10},{10,1... | collective-permute-start | bytes 1572872 | tf_op jit(solution)/shard_map/ppermute | solution.py:141
  25.8 26.1 %collective-permute-start.4 = (bf16[8,16,16,128]{3,1,2,0:T(8,128)(2,1)}, bf16[8,16,16,128]{3,1,2,0:T(8,128)(2,1)}, u32[]{:S(2)}, u32[]{:S(2)}) collective-permute-start(bf16[8,16,16,128]{3,1,2,0:T(8,128)(2,1)} %get-tuple-element.35), channel_id=1, source_target_pairs={{0,2},{1,3},{2,0},{3,1},{4,6},{5,7},{6,4},{7,5},{8,10},{9,11},{10,... | collective-permute-start | bytes 1572872 | tf_op jit(solution)/shard_map/ppermute | solution.py:141
  30.9 21.3 %collective-permute-start.5 = (bf16[8,16,16,128]{3,1,2,0:T(8,128)(2,1)}, bf16[8,16,16,128]{3,1,2,0:T(8,128)(2,1)}, u32[]{:S(2)}, u32[]{:S(2)}) collective-permute-start(bf16[8,16,16,128]{3,1,2,0:T(8,128)(2,1)} %get-tuple-element.36), channel_id=1, source_target_pairs={{0,3},{1,0},{2,1},{3,2},{4,7},{5,4},{6,5},{7,6},{8,11},{9,8},{10,9... | collective-permute-start | bytes 1572872 | tf_op jit(solution)/shard_map/ppermute | solution.py:141
  35.7 6.0 %copy-start.11 = (bf16[1,128,512]{2,1,0:T(8,128)(2,1)S(1)}, bf16[1,128,512]{2,1,0:T(8,128)(2,1)}, u32[]{:S(2)}) copy-start(bf16[1,128,512]{2,1,0:T(8,128)(2,1)} %param.18) | copy-start | bytes 393220
  45.7 17.8 %collective-permute-start = (bf16[8,17,16,128]{3,2,1,0:T(8,128)(2,1)}, bf16[8,17,16,128]{3,2,1,0:T(8,128)(2,1)S(1)}, u32[]{:S(2)}, u32[]{:S(2)}) collective-permute-start(bf16[8,17,16,128]{3,2,1,0:T(8,128)(2,1)} %bitcast.116), channel_id=1, source_target_pairs={{0,1},{1,2},{2,3},{3,0},{4,5},{5,6},{6,7},{7,4},{8,9},{9,10},{10,1... | collective-permute-start | bytes 1671176 | tf_op jit(solution)/shard_map/ppermute | solution.py:141
  47.1 25.9 %collective-permute-start.1 = (bf16[8,17,16,128]{3,2,1,0:T(8,128)(2,1)}, bf16[8,17,16,128]{3,2,1,0:T(8,128)(2,1)S(1)}, u32[]{:S(2)}, u32[]{:S(2)}) collective-permute-start(bf16[8,17,16,128]{3,2,1,0:T(8,128)(2,1)} %bitcast.115), channel_id=1, source_target_pairs={{0,2},{1,3},{2,0},{3,1},{4,6},{5,7},{6,4},{7,5},{8,10},{9,11},{10,... | collective-permute-start | bytes 1671176 | tf_op jit(solution)/shard_map/ppermute | solution.py:141
  49.7 25.6 %collective-permute-start.2 = (bf16[8,17,16,128]{3,2,1,0:T(8,128)(2,1)}, bf16[8,17,16,128]{3,2,1,0:T(8,128)(2,1)S(1)}, u32[]{:S(2)}, u32[]{:S(2)}) collective-permute-start(bf16[8,17,16,128]{3,2,1,0:T(8,128)(2,1)} %bitcast.114), channel_id=1, source_target_pairs={{0,3},{1,0},{2,1},{3,2},{4,7},{5,4},{6,5},{7,6},{8,11},{9,8},{10,9... | collective-permute-start | bytes 1671176 | tf_op jit(solution)/shard_map/ppermute | solution.py:141
  54.8 35.0 %copy-start.12 = (s32[8]{0:T(128)S(1)}, s32[8]{0:T(128)}, u32[]{:S(2)}) copy-start(s32[8]{0:T(128)} %param.25) | copy-start | bytes 100
  54.8 35.0 %copy-start.13 = (s32[32]{0:T(128)S(1)}, s32[32]{0:T(128)}, u32[]{:S(2)}) copy-start(s32[32]{0:T(128)} %param.21) | copy-start | bytes 388
  54.8 30.1 %all-to-all-start.1 = ((bf16[8,16,16,128]{3,1,2,0:T(8,128)(2,1)}), bf16[8,16,16,128]{3,1,2,0:T(8,128)(2,1)S(1)}, u32[]{:S(2)}, u32[]{:S(2)}) async-start(bf16[8,16,16,128]{3,1,2,0:T(8,128)(2,1)} %fusion.17), calls=%async_computation.1 | async-start | bytes 1048576 | tf_op jit(solution)/shard_map/all_to_all | solution.py:145
  84.9 21.4 %all-to-all-start = ((bf16[8,20,16,128]{3,2,1,0:T(8,128)(2,1)}), bf16[8,20,16,128]{3,2,1,0:T(8,128)(2,1)S(1)}, u32[]{:S(2)}, u32[]{:S(2)}) async-start(bf16[8,20,16,128]{3,2,1,0:T(8,128)(2,1)} %slice_dynamic-update-slice_fusion), calls=%async_computation | async-start | bytes 1310720 | tf_op jit(solution)/shard_map/all_to_all | solution.py:145
  88.4 119.8 %all-gather.5.cloned.1.call-start = ((), (), s32[]{:S(2)}) async-start(), calls=%async_computation.3 | async-start | bytes 6488064 | tf_op jit(solution)/shard_map/all_gather | solution.py:182
  89.7 21.7 %copy-start.8 = (bf16[8,128,128]{2,1,0:T(8,128)(2,1)S(1)}, bf16[8,128,128]{2,1,0:T(8,128)(2,1)}, u32[]{:S(2)}) copy-start(bf16[8,128,128]{2,1,0:T(8,128)(2,1)} %param.23) | copy-start | bytes 786436
  89.9 21.8 %copy-start.9 = (bf16[8,128,128]{2,1,0:T(8,128)(2,1)S(1)}, bf16[8,128,128]{2,1,0:T(8,128)(2,1)}, u32[]{:S(2)}) copy-start(bf16[8,128,128]{2,1,0:T(8,128)(2,1)} %param.24) | copy-start | bytes 786436
  106.9 17.1 %copy-start.10 = (bf16[4,128,128]{2,1,0:T(8,128)(2,1)S(1)}, bf16[4,128,128]{2,1,0:T(8,128)(2,1)}, u32[]{:S(2)}) copy-start(bf16[4,128,128]{2,1,0:T(8,128)(2,1)} %param.27) | copy-start | bytes 393220
  107.2 18.6 %copy-start.4 = (bf16[32,2,128,128]{3,2,0,1:T(8,128)(2,1)S(1)}, bf16[32,2,128,128]{3,2,0,1:T(8,128)(2,1)}, u32[]{:S(2)}) copy-start(bf16[32,2,128,128]{3,2,0,1:T(8,128)(2,1)} %all-gather.3.cloned.1.call-done) | copy-start | bytes 6291460
  112.1 4.7 %collective-permute-start.9 = (f32[4,16,128]{2,0,1:T(4,128)S(1)}, f32[4,16,128]{2,0,1:T(4,128)S(1)}, u32[]{:S(2)}, u32[]{:S(2)}) collective-permute-start(f32[4,16,128]{2,0,1:T(4,128)S(1)} %fusion.24), channel_id=1, source_target_pairs={{0,32},{32,0},{64,96},{96,64},{128,160},{160,128},{192,224},{224,1... | collective-permute-start | bytes 98312 | tf_op jit(solution)/shard_map/ppermute | solution.py:161
  116.8 2.9 %collective-permute-start.10 = (f32[4,16,128]{2,0,1:T(4,128)S(1)}, f32[4,16,128]{2,0,1:T(4,128)S(1)}, u32[]{:S(2)}, u32[]{:S(2)}) collective-permute-start(f32[4,16,128]{2,0,1:T(4,128)S(1)} %add.176), channel_id=1, source_target_pairs={{0,64},{32,96},{64,0},{96,32},{128,192},{160,224},{192,128},{224,1... | collective-permute-start | bytes 98312 | tf_op jit(solution)/shard_map/ppermute | solution.py:161
  119.6 4.4 %collective-permute-start.11 = (f32[4,16,128]{2,0,1:T(4,128)S(1)}, f32[4,16,128]{2,0,1:T(4,128)S(1)}, u32[]{:S(2)}, u32[]{:S(2)}) collective-permute-start(f32[4,16,128]{2,0,1:T(4,128)S(1)} %add.177), channel_id=1, source_target_pairs={{0,128},{32,160},{64,192},{96,224},{128,0},{160,32},{192,64},{224,... | collective-permute-start | bytes 98312 | tf_op jit(solution)/shard_map/ppermute | solution.py:161
  126.4 13.7 %copy-start.6 = (bf16[24,128,128]{2,1,0:T(8,128)(2,1)S(1)}, bf16[24,128,128]{2,1,0:T(8,128)(2,1)}, u32[]{:S(2)}) copy-start(bf16[24,128,128]{2,1,0:T(8,128)(2,1)} %param.16) | copy-start | bytes 2359300
  126.5 7.8 %collective-permute-start.12 = (bf16[44,16,128]{2,1,0:T(8,128)(2,1)S(1)}, bf16[44,16,128]{2,1,0:T(8,128)(2,1)S(1)}, u32[]{:S(2)}, u32[]{:S(2)}) collective-permute-start(bf16[44,16,128]{2,1,0:T(8,128)(2,1)S(1)} %get-tuple-element.38), channel_id=1, source_target_pairs={{0,1},{1,2},{2,3},{3,0},{4,5},{5,6},{6,7},{7,4},{8,9},{9,10},{10,1... | collective-permute-start | bytes 540680 | tf_op jit(solution)/shard_map/ppermute | solution.py:180
  127.1 11.2 %collective-permute-start.13 = (bf16[44,16,128]{2,1,0:T(8,128)(2,1)S(1)}, bf16[44,16,128]{2,1,0:T(8,128)(2,1)S(1)}, u32[]{:S(2)}, u32[]{:S(2)}) collective-permute-start(bf16[44,16,128]{2,1,0:T(8,128)(2,1)S(1)} %get-tuple-element.38), channel_id=1, source_target_pairs={{0,2},{1,3},{2,0},{3,1},{4,6},{5,7},{6,4},{7,5},{8,10},{9,11},{10,... | collective-permute-start | bytes 540680 | tf_op jit(solution)/shard_map/ppermute | solution.py:180
  132.5 5.8 %collective-permute-start.14 = (bf16[44,16,128]{2,1,0:T(8,128)(2,1)S(1)}, bf16[44,16,128]{2,1,0:T(8,128)(2,1)S(1)}, u32[]{:S(2)}, u32[]{:S(2)}) collective-permute-start(bf16[44,16,128]{2,1,0:T(8,128)(2,1)S(1)} %get-tuple-element.38), channel_id=1, source_target_pairs={{0,3},{1,0},{2,1},{3,2},{4,7},{5,4},{6,5},{7,6},{8,11},{9,8},{10,9... | collective-permute-start | bytes 540680 | tf_op jit(solution)/shard_map/ppermute | solution.py:180
  138.3 3.0 %copy-start.7 = (bf16[24,128,128]{2,1,0:T(8,128)(2,1)S(1)}, bf16[24,128,128]{2,1,0:T(8,128)(2,1)}, u32[]{:S(2)}) copy-start(bf16[24,128,128]{2,1,0:T(8,128)(2,1)} %param.15) | copy-start | bytes 2359300
  219.7 10.8 %copy-start.1 = (bf16[24,128,512]{2,1,0:T(8,128)(2,1)S(1)}, bf16[24,128,512]{2,1,0:T(8,128)(2,1)}, u32[]{:S(2)}) copy-start(bf16[24,128,512]{2,1,0:T(8,128)(2,1)} %param.14) | copy-start | bytes 9437188
  (1 other events, 1.7 us)
Sparse Core Ops, SparseCore 0:
  35.8 51.7 all-gather.2
  140.2 67.9 all-gather.4

commit v11 on v9

--- a/solution.py
+++ b/solution.py
@@ -151,12 +151,12 @@
     middle_y = (middle_piece.astype(jnp.float32) - middle_sum).astype(jnp.bfloat16)
     middle_solved = piece_block(middle_inverse, middle_y).astype(jnp.bfloat16)
     top_term = slot_sums(middle_parent, top_count, piece_block(middle_link, middle_solved))
-    top_sum = top_term
     rows = lax.axis_size(ROW)
-    step = 1
-    while step < rows:
-        top_sum = top_sum + lax.ppermute(top_sum, ROW, [(i, i ^ step) for i in range(rows)])
-        step *= 2
+    terms = [top_term]
+    for shift in range(1, rows):
+        terms.append(lax.ppermute(top_term, ROW, [(i, (i + shift) % rows) for i in range(rows)]))
+    in_row_order = jnp.take(jnp.stack(terms), (lax.axis_index(ROW) - lax.iota(jnp.int32, rows)) % rows, axis=0)
+    top_sum = jnp.sum(in_row_order, axis=0)
     top_piece = lax.dynamic_slice_in_dim(top_rhs, start, chunk, 2).transpose(0, 2, 1)
     top_y = (top_piece.astype(jnp.float32) - top_sum).astype(jnp.bfloat16)
     top_solved = piece_block(top_inverse, top_y).astype(jnp.bfloat16)

time: 236 us -> 242 us (1.025)
  local copies, waits for them, and re-layouts: 28.7 us -> 34.7 us
  waiting for transfers between devices: 109 us -> 104 us
  starting transfers between devices: 38.7 us -> 42.8 us
    all_gather x1, waiting for transfers between devices: 65.7 us -> 61 us  [local(): gathered = lax.all_gather(by_y, 'z', axis=0, tiled=True)]
    ppermute x3 -> x7, starting transfers between devices: 7.7 us -> 11.9 us  [local(): lax.ppermute(top_term, ROW, [(i, (i + shift) % rows) for i in range(rows)])]
    unnamed x44 -> x50, local copies, waits for them, and re-layouts: 11.6 us -> 15.4 us
    ppermute x3 -> x7, waiting for transfers between devices: 3.05 us -> 0.02 us  [local(): lax.ppermute(top_term, ROW, [(i, (i + shift) % rows) for i in range(rows)])]
    ppermute x3, waiting for transfers between devices: 5.76 us -> 8.58 us  [local(): arrivals.append(lax.ppermute(parts, 'y', pairs))]
  transfers between devices with their start and end apart: 19 -> 23, of which waited for: 11 -> 7; matrix products, arithmetic and copies ran while one was open for 18% -> 19% of each run, Pallas kernels for 0% -> 0%
where the time goes in v11:
time: 242 us; the launch traced here: 241 us
  waiting for transfers between devices  104 us (43%)
  starting transfers between devices  42.8 us (18%)
  local copies, waits for them, and re-layouts  34.7 us (14%)
  matrix products  25.3 us (10%)
  between operations  14.5 us (6%)
  other arithmetic  10.9 us (5%)
  Pallas kernels  9.19 us (4%)
    all_gather x1, waiting for transfers between devices, local(): gathered = lax.all_gather(by_y, 'z', axis=0, tiled=True)  61 us
    all_to_all x2, waiting for transfers between devices, local(): incoming = lax.all_to_all(partial, 'z', 0, 0, tiled=True)  22.8 us
    unnamed x50, local copies, waits for them, and re-layouts  15.4 us
    ppermute x7, starting transfers between devices, local(): lax.ppermute(top_term, ROW, [(i, (i + shift) % rows) for i in range(rows)])  11.9 us
    all_to_all x2, starting transfers between devices, local(): incoming = lax.all_to_all(partial, 'z', 0, 0, tiled=True)  11.9 us
    ppermute x6, waiting for transfers between devices, local(): arrivals.append(lax.ppermute(outbound, 'y', pairs))  11.2 us
    pallas_call x1, Pallas kernels, leaf_backward(): pl.pallas_call(leaf_backward_kernel, grid=(count // per_step,), in_specs=...  9.19 us
    ppermute x3, waiting for transfers between devices, local(): arrivals.append(lax.ppermute(parts, 'y', pairs))  8.58 us
  transfers between devices with their start and end apart: 23, of which 7 were waited for; matrix products, arithmetic and copies ran while one was open for 19% of the time, Pallas kernels for 0%

profile of v11, /device:TPU:1, one launch (start us, length us, event | category | flops | bytes accessed | tf_op | source)
XLA Modules:
  0.0 241.0 jit_solution(838070955808374919)
XLA Ops:
  8.9 2.1 collective-permute-start.6
  11.0 2.6 %collective-permute-start.7 = (bf16[2,128,128]{2,1,0:T(8,128)(2,1)S(1)}, bf16[2,128,128]{2,1,0:T(8,128)(2,1)S(1)}, u32[]{:S(2)}, u32[]{:S(2)}) collective-permute-start(bf16[2,128,128]{2,1,0:T(8,128)(2,1)S(1)} %constant_dynamic-update-slice_fusion), channel_id=1, source_target_pairs={{0,2},{1,3},{2,0},{3,1},{4,6},{5,7},{6,4},{7,5},{8,10},{9,11},{10,... | collective-permute-start | bytes 196616 | tf_op jit(solution)/shard_map/ppermute | solution.py:116
  15.4 2.2 convolution_convert_fusion.solved_ref
  19.3 2.3 fusion
  21.5 2.5 %add_convert_fusion = bf16[16,512,128]{2,0,1:T(8,128)(2,1)S(1)} fusion(f32[16,512,128]{2,0,1:T(8,128)S(1)} %fusion, bf16[24,512,128]{2,1,0:T(8,128)(2,1)S(1)} %get-tuple-element.28, s32[24]{0:T(128)S(1)} %get-tuple-element.25), kind=kOutput, calls=%fused_computation.8 | convolution fusion | flops 52429184 | bytes 9437280 | tf_op jit(solution)/shard_map/sk,k...->s.../dot_general | solution.py:39
  26.6 4.2 %fusion.2 = f32[16,512,128]{2,0,1:T(8,128)} fusion(bf16[24,512,128]{2,1,0:T(8,128)(2,1)S(1)} %get-tuple-element.29, s32[24]{0:T(128)S(1)} %broadcast_add_fusion), kind=kOutput, calls=%fused_computation.13 | convolution fusion | flops 50332032 | bytes 7340128 | tf_op jit(solution)/shard_map/sk,k...->s.../dot_general | solution.py:40
  30.9 1.7 collective-permute-start.5
  33.3 1.5 gather_fusion.1
  35.7 6.0 %add_convert_fusion.1 = bf16[16,512,128]{2,0,1:T(8,128)(2,1)} fusion(f32[16,512,128]{2,0,1:T(8,128)} %fusion.2, bf16[24,512,128]{2,1,0:T(8,128)(2,1)S(1)} %get-tuple-element.28, s32[24]{0:T(128)S(1)} %broadcast_add_fusion), kind=kOutput, calls=%fused_computation.9 | convolution fusion | flops 52429184 | bytes 9437280 | tf_op jit(solution)/shard_map/sk,k...->s.../dot_general | solution.py:39
  41.9 2.3 pad_maximum_fusion
  47.0 1.8 collective-permute-start.1
  49.7 2.1 collective-permute-start.2
  53.2 2.6 %fusion.17 = bf16[8,16,16,128]{3,1,2,0:T(8,128)(2,1)} fusion(bf16[8,16,16,128]{3,1,2,0:T(8,128)(2,1)} %collective-permute-done.5, bf16[8,16,16,128]{3,1,2,0:T(8,128)(2,1)} %collective-permute-done.4, bf16[8,16,16,128]{3,1,2,0:T(8,128)(2,1)} %collective-permute-done.3, bf16[16,8,4,16,128]{4,0,3,2,1:T(8,128)(2,1)} %bitcast.140, s32[]{:T(128)S(6)} %select_n.162), kind=kLoop, calls=%fused_computation.38 | loop fusion | flops 2097152 | bytes 2621444 | tf_op jit(solution)/shard_map/convert_element_type | solution.py:139
  55.8 8.3 %all-to-all-start.1 = ((bf16[8,16,16,128]{3,1,2,0:T(8,128)(2,1)}), bf16[8,16,16,128]{3,1,2,0:T(8,128)(2,1)S(1)}, u32[]{:S(2)}, u32[]{:S(2)}) async-start(bf16[8,16,16,128]{3,1,2,0:T(8,128)(2,1)} %fusion.17), calls=%async_computation.1 | async-start | bytes 1048576 | tf_op jit(solution)/shard_map/all_to_all | solution.py:142
  64.1 8.8 %collective-permute-done.1 = bf16[8,17,16,128]{3,2,1,0:T(8,128)(2,1)S(1)} collective-permute-done((bf16[8,17,16,128]{3,2,1,0:T(8,128)(2,1)}, bf16[8,17,16,128]{3,2,1,0:T(8,128)(2,1)S(1)}, u32[]{:S(2)}, u32[]{:S(2)}) %collective-permute-start.1) | collective-permute-done | bytes 557088 | tf_op jit(solution)/shard_map/ppermute | solution.py:138
  73.0 2.4 collective-permute-done.2
  78.9 6.6 %all-to-all-done.1 = bf16[8,16,16,128]{3,1,2,0:T(8,128)(2,1)S(1)} async-done(((bf16[8,16,16,128]{3,1,2,0:T(8,128)(2,1)}), bf16[8,16,16,128]{3,1,2,0:T(8,128)(2,1)S(1)}, u32[]{:S(2)}, u32[]{:S(2)}) %all-to-all-start.1) | async-done | bytes 524320 | tf_op jit(solution)/shard_map/all_to_all | solution.py:142
  85.4 3.5 %all-to-all-start = ((bf16[8,20,16,128]{3,2,1,0:T(8,128)(2,1)}), bf16[8,20,16,128]{3,2,1,0:T(8,128)(2,1)S(1)}, u32[]{:S(2)}, u32[]{:S(2)}) async-start(bf16[8,20,16,128]{3,2,1,0:T(8,128)(2,1)} %slice_dynamic-update-slice_fusion), calls=%async_computation | async-start | bytes 1310720 | tf_op jit(solution)/shard_map/all_to_all | solution.py:142
  90.5 16.2 %all-to-all-done = bf16[8,20,16,128]{3,2,1,0:T(8,128)(2,1)S(1)} async-done(((bf16[8,20,16,128]{3,2,1,0:T(8,128)(2,1)}), bf16[8,20,16,128]{3,2,1,0:T(8,128)(2,1)S(1)}, u32[]{:S(2)}, u32[]{:S(2)}) %all-to-all-start) | async-done | bytes 655392 | tf_op jit(solution)/shard_map/all_to_all | solution.py:142
  107.7 2.0 convolution_convert_fusion.2
  109.7 1.9 fusion.18
  113.2 4.5 %collective-permute-start.9 = (f32[4,16,128]{2,0,1:T(4,128)S(1)}, f32[4,16,128]{2,0,1:T(4,128)S(1)}, u32[]{:S(2)}, u32[]{:S(2)}) collective-permute-start(f32[4,16,128]{2,0,1:T(4,128)S(1)} %get-tuple-element.40), channel_id=1, source_target_pairs={{0,32},{32,64},{64,96},{96,128},{128,160},{160,192},{192,224},{224... | collective-permute-start | bytes 98312 | tf_op jit(solution)/shard_map/ppermute | solution.py:157
  121.1 2.0 collective-permute-start.13
  124.2 1.6 collective-permute-start.15
  129.5 1.7 gather_fusion.2
  133.9 5.6 %collective-permute-start.17 = (bf16[44,16,128]{2,1,0:T(8,128)(2,1)S(1)}, bf16[44,16,128]{2,1,0:T(8,128)(2,1)S(1)}, u32[]{:S(2)}, u32[]{:S(2)}) collective-permute-start(bf16[44,16,128]{2,1,0:T(8,128)(2,1)S(1)} %get-tuple-element.38), channel_id=1, source_target_pairs={{0,2},{1,3},{2,0},{3,1},{4,6},{5,7},{6,4},{7,5},{8,10},{9,11},{10,... | collective-permute-start | bytes 540680 | tf_op jit(solution)/shard_map/ppermute | solution.py:177
  139.5 3.7 %collective-permute-done.16 = bf16[44,16,128]{2,1,0:T(8,128)(2,1)S(1)} collective-permute-done((bf16[44,16,128]{2,1,0:T(8,128)(2,1)S(1)}, bf16[44,16,128]{2,1,0:T(8,128)(2,1)S(1)}, u32[]{:S(2)}, u32[]{:S(2)}) %collective-permute-start.16) | collective-permute-done | bytes 180256 | tf_op jit(solution)/shard_map/ppermute | solution.py:177
  143.3 4.8 %collective-permute-done.17 = bf16[44,16,128]{2,1,0:T(8,128)(2,1)S(1)} collective-permute-done((bf16[44,16,128]{2,1,0:T(8,128)(2,1)S(1)}, bf16[44,16,128]{2,1,0:T(8,128)(2,1)S(1)}, u32[]{:S(2)}, u32[]{:S(2)}) %collective-permute-start.17) | collective-permute-done | bytes 180256 | tf_op jit(solution)/shard_map/ppermute | solution.py:177
  152.3 61.0 %all-gather.5.cloned.1.call-done = bf16[32,44,16,128]{3,2,1,0:T(8,128)(2,1)} async-done(((bf16[4,44,16,128]{3,2,1,0:T(8,128)(2,1)}), bf16[32,44,16,128]{3,2,1,0:T(8,128)(2,1)}) %all-gather.5.cloned.1.call-update) | async-done | bytes 5767184 | tf_op jit(solution)/shard_map/all_gather | solution.py:179
  213.4 1.8 copy_bitcast_fusion
  219.4 5.5 %gather_fusion.6 = bf16[24,32,16,128]{3,2,1,0:T(8,128)(2,1)} fusion(bf16[32,44,16,128]{3,2,1,0:T(8,128)(2,1)} %all-gather.5.cloned.1.call-done, s32[1024]{0:T(1024)S(1)} %pad_clamp_fusion), kind=kCustom, calls=%fused_computation.6 | custom fusion | bytes 6291552 | tf_op jit(solution)/shard_map/gather | solution.py:185
  224.9 9.2 %shard_map.165 = bf16[24,128,512]{2,1,0:T(8,128)(2,1)} custom-call(bf16[24,32,16,128]{3,2,1,0:T(8,128)(2,1)} %gather_fusion.6, bf16[24,128,512]{2,1,0:T(8,128)(2,1)} %copy-done.2, bf16[24,128,128]{2,1,0:T(8,128)(2,1)} %bitcast.142, bf16[24,128,128]{2,1,0:T(8,128)(2,1)} %bitcast.143), custom_call_target="tpu_custom_call" | custom-call | flops 805306368 | bytes 11010048 | tf_op jit(solution)/shard_map/pallas_call | solution.py:67
  (131 shorter events, 41.3 us)
Async XLA Ops:
  7.2 8.2 %copy-start = (bf16[24,128,512]{2,1,0:T(8,128)(2,1)S(1)}, bf16[24,128,512]{2,1,0:T(8,128)(2,1)}, u32[]{:S(2)}) copy-start(bf16[24,128,512]{2,1,0:T(8,128)(2,1)} %param.14) | copy-start | bytes 9437188
  7.2 100.5 %all-gather.3.cloned.1.call-start = ((), (), s32[]{:S(2)}) async-start(), calls=%async_computation.2 | async-start | bytes 2359296 | tf_op jit(solution)/shard_map/all_gather | solution.py:118
  8.9 22.0 %collective-permute-start.6 = (bf16[2,128,128]{2,1,0:T(8,128)(2,1)S(1)}, bf16[2,128,128]{2,1,0:T(8,128)(2,1)S(1)}, u32[]{:S(2)}, u32[]{:S(2)}) collective-permute-start(bf16[2,128,128]{2,1,0:T(8,128)(2,1)S(1)} %constant_dynamic-update-slice_fusion), channel_id=1, source_target_pairs={{0,1},{1,2},{2,3},{3,0},{4,5},{5,6},{6,7},{7,4},{8,9},{9,10},{10,1... | collective-permute-start | bytes 196616 | tf_op jit(solution)/shard_map/ppermute | solution.py:116
  11.0 21.5 %collective-permute-start.7 = (bf16[2,128,128]{2,1,0:T(8,128)(2,1)S(1)}, bf16[2,128,128]{2,1,0:T(8,128)(2,1)S(1)}, u32[]{:S(2)}, u32[]{:S(2)}) collective-permute-start(bf16[2,128,128]{2,1,0:T(8,128)(2,1)S(1)} %constant_dynamic-update-slice_fusion), channel_id=1, source_target_pairs={{0,2},{1,3},{2,0},{3,1},{4,6},{5,7},{6,4},{7,5},{8,10},{9,11},{10,... | collective-permute-start | bytes 196616 | tf_op jit(solution)/shard_map/ppermute | solution.py:116
  13.7 18.9 %collective-permute-start.8 = (bf16[2,128,128]{2,1,0:T(8,128)(2,1)S(1)}, bf16[2,128,128]{2,1,0:T(8,128)(2,1)S(1)}, u32[]{:S(2)}, u32[]{:S(2)}) collective-permute-start(bf16[2,128,128]{2,1,0:T(8,128)(2,1)S(1)} %constant_dynamic-update-slice_fusion), channel_id=1, source_target_pairs={{0,3},{1,0},{2,1},{3,2},{4,7},{5,4},{6,5},{7,6},{8,11},{9,8},{10,9... | collective-permute-start | bytes 196616 | tf_op jit(solution)/shard_map/ppermute | solution.py:116
  25.4 24.3 %collective-permute-start.3 = (bf16[8,16,16,128]{3,1,2,0:T(8,128)(2,1)}, bf16[8,16,16,128]{3,1,2,0:T(8,128)(2,1)}, u32[]{:S(2)}, u32[]{:S(2)}) collective-permute-start(bf16[8,16,16,128]{3,1,2,0:T(8,128)(2,1)} %get-tuple-element.34), channel_id=1, source_target_pairs={{0,1},{1,2},{2,3},{3,0},{4,5},{5,6},{6,7},{7,4},{8,9},{9,10},{10,1... | collective-permute-start | bytes 1572872 | tf_op jit(solution)/shard_map/ppermute | solution.py:138
  25.8 27.4 %collective-permute-start.4 = (bf16[8,16,16,128]{3,1,2,0:T(8,128)(2,1)}, bf16[8,16,16,128]{3,1,2,0:T(8,128)(2,1)}, u32[]{:S(2)}, u32[]{:S(2)}) collective-permute-start(bf16[8,16,16,128]{3,1,2,0:T(8,128)(2,1)} %get-tuple-element.35), channel_id=1, source_target_pairs={{0,2},{1,3},{2,0},{3,1},{4,6},{5,7},{6,4},{7,5},{8,10},{9,11},{10,... | collective-permute-start | bytes 1572872 | tf_op jit(solution)/shard_map/ppermute | solution.py:138
  30.9 22.3 %collective-permute-start.5 = (bf16[8,16,16,128]{3,1,2,0:T(8,128)(2,1)}, bf16[8,16,16,128]{3,1,2,0:T(8,128)(2,1)}, u32[]{:S(2)}, u32[]{:S(2)}) collective-permute-start(bf16[8,16,16,128]{3,1,2,0:T(8,128)(2,1)} %get-tuple-element.36), channel_id=1, source_target_pairs={{0,3},{1,0},{2,1},{3,2},{4,7},{5,4},{6,5},{7,6},{8,11},{9,8},{10,9... | collective-permute-start | bytes 1572872 | tf_op jit(solution)/shard_map/ppermute | solution.py:138
  45.7 18.5 %collective-permute-start = (bf16[8,17,16,128]{3,2,1,0:T(8,128)(2,1)}, bf16[8,17,16,128]{3,2,1,0:T(8,128)(2,1)S(1)}, u32[]{:S(2)}, u32[]{:S(2)}) collective-permute-start(bf16[8,17,16,128]{3,2,1,0:T(8,128)(2,1)} %bitcast.136), channel_id=1, source_target_pairs={{0,1},{1,2},{2,3},{3,0},{4,5},{5,6},{6,7},{7,4},{8,9},{9,10},{10,1... | collective-permute-start | bytes 1671176 | tf_op jit(solution)/shard_map/ppermute | solution.py:138
  47.0 25.9 %collective-permute-start.1 = (bf16[8,17,16,128]{3,2,1,0:T(8,128)(2,1)}, bf16[8,17,16,128]{3,2,1,0:T(8,128)(2,1)S(1)}, u32[]{:S(2)}, u32[]{:S(2)}) collective-permute-start(bf16[8,17,16,128]{3,2,1,0:T(8,128)(2,1)} %bitcast.135), channel_id=1, source_target_pairs={{0,2},{1,3},{2,0},{3,1},{4,6},{5,7},{6,4},{7,5},{8,10},{9,11},{10,... | collective-permute-start | bytes 1671176 | tf_op jit(solution)/shard_map/ppermute | solution.py:138
  49.7 25.6 %collective-permute-start.2 = (bf16[8,17,16,128]{3,2,1,0:T(8,128)(2,1)}, bf16[8,17,16,128]{3,2,1,0:T(8,128)(2,1)S(1)}, u32[]{:S(2)}, u32[]{:S(2)}) collective-permute-start(bf16[8,17,16,128]{3,2,1,0:T(8,128)(2,1)} %bitcast.134), channel_id=1, source_target_pairs={{0,3},{1,0},{2,1},{3,2},{4,7},{5,4},{6,5},{7,6},{8,11},{9,8},{10,9... | collective-permute-start | bytes 1671176 | tf_op jit(solution)/shard_map/ppermute | solution.py:138
  55.8 33.5 %copy-start.12 = (s32[8]{0:T(128)S(1)}, s32[8]{0:T(128)}, u32[]{:S(2)}) copy-start(s32[8]{0:T(128)} %param.25) | copy-start | bytes 100
  55.8 33.5 %copy-start.13 = (s32[32]{0:T(128)S(1)}, s32[32]{0:T(128)}, u32[]{:S(2)}) copy-start(s32[32]{0:T(128)} %param.21) | copy-start | bytes 388
  55.8 29.6 %all-to-all-start.1 = ((bf16[8,16,16,128]{3,1,2,0:T(8,128)(2,1)}), bf16[8,16,16,128]{3,1,2,0:T(8,128)(2,1)S(1)}, u32[]{:S(2)}, u32[]{:S(2)}) async-start(bf16[8,16,16,128]{3,1,2,0:T(8,128)(2,1)} %fusion.17), calls=%async_computation.1 | async-start | bytes 1048576 | tf_op jit(solution)/shard_map/all_to_all | solution.py:142
  85.4 21.3 %all-to-all-start = ((bf16[8,20,16,128]{3,2,1,0:T(8,128)(2,1)}), bf16[8,20,16,128]{3,2,1,0:T(8,128)(2,1)S(1)}, u32[]{:S(2)}, u32[]{:S(2)}) async-start(bf16[8,20,16,128]{3,2,1,0:T(8,128)(2,1)} %slice_dynamic-update-slice_fusion), calls=%async_computation | async-start | bytes 1310720 | tf_op jit(solution)/shard_map/all_to_all | solution.py:142
  89.0 124.4 %all-gather.5.cloned.1.call-start = ((), (), s32[]{:S(2)}) async-start(), calls=%async_computation.3 | async-start | bytes 6488064 | tf_op jit(solution)/shard_map/all_gather | solution.py:179
  89.4 22.5 %copy-start.8 = (bf16[8,128,128]{2,1,0:T(8,128)(2,1)S(1)}, bf16[8,128,128]{2,1,0:T(8,128)(2,1)}, u32[]{:S(2)}) copy-start(bf16[8,128,128]{2,1,0:T(8,128)(2,1)} %param.23) | copy-start | bytes 786436
  90.4 21.7 %copy-start.9 = (bf16[8,128,128]{2,1,0:T(8,128)(2,1)S(1)}, bf16[8,128,128]{2,1,0:T(8,128)(2,1)}, u32[]{:S(2)}) copy-start(bf16[8,128,128]{2,1,0:T(8,128)(2,1)} %param.24) | copy-start | bytes 786436
  107.5 23.9 %copy-start.10 = (bf16[4,128,128]{2,1,0:T(8,128)(2,1)S(1)}, bf16[4,128,128]{2,1,0:T(8,128)(2,1)}, u32[]{:S(2)}) copy-start(bf16[4,128,128]{2,1,0:T(8,128)(2,1)} %param.27) | copy-start | bytes 393220
  107.7 25.5 %copy-start.4 = (bf16[32,2,128,128]{3,2,0,1:T(8,128)(2,1)S(1)}, bf16[32,2,128,128]{3,2,0,1:T(8,128)(2,1)}, u32[]{:S(2)}) copy-start(bf16[32,2,128,128]{3,2,0,1:T(8,128)(2,1)} %all-gather.3.cloned.1.call-done) | copy-start | bytes 6291460
  113.2 10.0 %collective-permute-start.9 = (f32[4,16,128]{2,0,1:T(4,128)S(1)}, f32[4,16,128]{2,0,1:T(4,128)S(1)}, u32[]{:S(2)}, u32[]{:S(2)}) collective-permute-start(f32[4,16,128]{2,0,1:T(4,128)S(1)} %get-tuple-element.40), channel_id=1, source_target_pairs={{0,32},{32,64},{64,96},{96,128},{128,160},{160,192},{192,224},{224... | collective-permute-start | bytes 98312 | tf_op jit(solution)/shard_map/ppermute | solution.py:157
  117.8 6.4 %collective-permute-start.10 = (f32[4,16,128]{2,0,1:T(4,128)S(1)}, f32[4,16,128]{2,0,1:T(4,128)S(1)}, u32[]{:S(2)}, u32[]{:S(2)}) collective-permute-start(f32[4,16,128]{2,0,1:T(4,128)S(1)} %get-tuple-element.40), channel_id=1, source_target_pairs={{0,64},{32,96},{64,128},{96,160},{128,192},{160,224},{192,0},{224,... | collective-permute-start | bytes 98312 | tf_op jit(solution)/shard_map/ppermute | solution.py:157
  118.9 7.6 %collective-permute-start.11 = (f32[4,16,128]{2,0,1:T(4,128)S(1)}, f32[4,16,128]{2,0,1:T(4,128)S(1)}, u32[]{:S(2)}, u32[]{:S(2)}) collective-permute-start(f32[4,16,128]{2,0,1:T(4,128)S(1)} %get-tuple-element.40), channel_id=1, source_target_pairs={{0,96},{32,128},{64,160},{96,192},{128,224},{160,0},{192,32},{224,... | collective-permute-start | bytes 98312 | tf_op jit(solution)/shard_map/ppermute | solution.py:157
  120.4 6.7 %collective-permute-start.12 = (f32[4,16,128]{2,0,1:T(4,128)S(1)}, f32[4,16,128]{2,0,1:T(4,128)S(1)}, u32[]{:S(2)}, u32[]{:S(2)}) collective-permute-start(f32[4,16,128]{2,0,1:T(4,128)S(1)} %get-tuple-element.40), channel_id=1, source_target_pairs={{0,128},{32,160},{64,192},{96,224},{128,0},{160,32},{192,64},{224,... | collective-permute-start | bytes 98312 | tf_op jit(solution)/shard_map/ppermute | solution.py:157
  121.1 6.6 %collective-permute-start.13 = (f32[4,16,128]{2,0,1:T(4,128)S(1)}, f32[4,16,128]{2,0,1:T(4,128)S(1)}, u32[]{:S(2)}, u32[]{:S(2)}) collective-permute-start(f32[4,16,128]{2,0,1:T(4,128)S(1)} %get-tuple-element.40), channel_id=1, source_target_pairs={{0,160},{32,192},{64,224},{96,0},{128,32},{160,64},{192,96},{224,1... | collective-permute-start | bytes 98312 | tf_op jit(solution)/shard_map/ppermute | solution.py:157
  123.1 5.2 %collective-permute-start.14 = (f32[4,16,128]{2,0,1:T(4,128)S(1)}, f32[4,16,128]{2,0,1:T(4,128)S(1)}, u32[]{:S(2)}, u32[]{:S(2)}) collective-permute-start(f32[4,16,128]{2,0,1:T(4,128)S(1)} %get-tuple-element.40), channel_id=1, source_target_pairs={{0,192},{32,224},{64,0},{96,32},{128,64},{160,96},{192,128},{224,1... | collective-permute-start | bytes 98312 | tf_op jit(solution)/shard_map/ppermute | solution.py:157
  124.2 4.7 %collective-permute-start.15 = (f32[4,16,128]{2,0,1:T(4,128)S(1)}, f32[4,16,128]{2,0,1:T(4,128)S(1)}, u32[]{:S(2)}, u32[]{:S(2)}) collective-permute-start(f32[4,16,128]{2,0,1:T(4,128)S(1)} %get-tuple-element.40), channel_id=1, source_target_pairs={{0,224},{32,0},{64,32},{96,64},{128,96},{160,128},{192,160},{224,1... | collective-permute-start | bytes 98312 | tf_op jit(solution)/shard_map/ppermute | solution.py:157
  133.8 16.1 %copy-start.6 = (bf16[24,128,128]{2,1,0:T(8,128)(2,1)S(1)}, bf16[24,128,128]{2,1,0:T(8,128)(2,1)}, u32[]{:S(2)}) copy-start(bf16[24,128,128]{2,1,0:T(8,128)(2,1)} %param.16) | copy-start | bytes 2359300
  133.8 9.4 %collective-permute-start.16 = (bf16[44,16,128]{2,1,0:T(8,128)(2,1)S(1)}, bf16[44,16,128]{2,1,0:T(8,128)(2,1)S(1)}, u32[]{:S(2)}, u32[]{:S(2)}) collective-permute-start(bf16[44,16,128]{2,1,0:T(8,128)(2,1)S(1)} %get-tuple-element.38), channel_id=1, source_target_pairs={{0,1},{1,2},{2,3},{3,0},{4,5},{5,6},{6,7},{7,4},{8,9},{9,10},{10,1... | collective-permute-start | bytes 540680 | tf_op jit(solution)/shard_map/ppermute | solution.py:177
  133.9 14.2 %collective-permute-start.17 = (bf16[44,16,128]{2,1,0:T(8,128)(2,1)S(1)}, bf16[44,16,128]{2,1,0:T(8,128)(2,1)S(1)}, u32[]{:S(2)}, u32[]{:S(2)}) collective-permute-start(bf16[44,16,128]{2,1,0:T(8,128)(2,1)S(1)} %get-tuple-element.38), channel_id=1, source_target_pairs={{0,2},{1,3},{2,0},{3,1},{4,6},{5,7},{6,4},{7,5},{8,10},{9,11},{10,... | collective-permute-start | bytes 540680 | tf_op jit(solution)/shard_map/ppermute | solution.py:177
  139.5 8.6 %collective-permute-start.18 = (bf16[44,16,128]{2,1,0:T(8,128)(2,1)S(1)}, bf16[44,16,128]{2,1,0:T(8,128)(2,1)S(1)}, u32[]{:S(2)}, u32[]{:S(2)}) collective-permute-start(bf16[44,16,128]{2,1,0:T(8,128)(2,1)S(1)} %get-tuple-element.38), channel_id=1, source_target_pairs={{0,3},{1,0},{2,1},{3,2},{4,7},{5,4},{6,5},{7,6},{8,11},{9,8},{10,9... | collective-permute-start | bytes 540680 | tf_op jit(solution)/shard_map/ppermute | solution.py:177
  224.9 9.2 %copy-start.1 = (bf16[24,128,512]{2,1,0:T(8,128)(2,1)S(1)}, bf16[24,128,512]{2,1,0:T(8,128)(2,1)}, u32[]{:S(2)}) copy-start(bf16[24,128,512]{2,1,0:T(8,128)(2,1)} %param.14) | copy-start | bytes 9437188
  (5 other events, 19.8 us)
Sparse Core Ops, SparseCore 0:
  35.8 51.6 all-gather.2
  150.0 63.2 all-gather.4

commit v12 on v9

--- a/solution.py
+++ b/solution.py
@@ -53,7 +53,7 @@
 
 def leaf_backward(parents, leaf_solved, leaf_link, leaf_inverse):
     count, width, columns = leaf_solved.shape
-    per_step = max(d for d in range(1, 5) if count % d == 0)
+    per_step = max(d for d in range(1, 9) if count % d == 0)
     pieces = parents.shape[1:]
 
     def own(step):

time: 236 us -> 236 us (level)
  no operation moved by 1% of the time
where the time goes in v12:
time: 236 us; the launch traced here: 235 us
  waiting for transfers between devices  109 us (46%)
  starting transfers between devices  38.7 us (16%)
  local copies, waits for them, and re-layouts  28.7 us (12%)
  matrix products  24.6 us (10%)
  between operations  14.5 us (6%)
  other arithmetic  10.7 us (5%)
  Pallas kernels  8.37 us (4%)
    all_gather x1, waiting for transfers between devices, local(): gathered = lax.all_gather(by_y, 'z', axis=0, tiled=True)  65.7 us
    all_to_all x2, waiting for transfers between devices, local(): incoming = lax.all_to_all(partial, 'z', 0, 0, tiled=True)  22.3 us
    ppermute x6, waiting for transfers between devices, local(): arrivals.append(lax.ppermute(outbound, 'y', pairs))  12.5 us
    all_to_all x2, starting transfers between devices, local(): incoming = lax.all_to_all(partial, 'z', 0, 0, tiled=True)  11.9 us
    unnamed x44, local copies, waits for them, and re-layouts  11.6 us
    dot_general x2, matrix products, split_slot_sums(): jnp.einsum('sk,k...->s...', select, high, preferred_element_type=jnp.floa...  8.46 us
    pallas_call x1, Pallas kernels, leaf_backward(): pl.pallas_call(leaf_backward_kernel, grid=(count // per_step,), in_specs=...  8.37 us
    ppermute x3, starting transfers between devices, local(): lax.ppermute(top_sum, ROW, [(i, i ^ step) for i in range(rows)])  7.7 us
  transfers between devices with their start and end apart: 19, of which 11 were waited for; matrix products, arithmetic and copies ran while one was open for 18% of the time, Pallas kernels for 0%

profile of v12, /device:TPU:1, one launch (start us, length us, event | category | flops | bytes accessed | tf_op | source)
XLA Modules:
  0.0 235.0 jit_solution(14070794275968884376)
XLA Ops:
  8.9 2.1 collective-permute-start.6
  11.0 2.6 %collective-permute-start.7 = (bf16[2,128,128]{2,1,0:T(8,128)(2,1)S(1)}, bf16[2,128,128]{2,1,0:T(8,128)(2,1)S(1)}, u32[]{:S(2)}, u32[]{:S(2)}) collective-permute-start(bf16[2,128,128]{2,1,0:T(8,128)(2,1)S(1)} %constant_dynamic-update-slice_fusion), channel_id=1, source_target_pairs={{0,2},{1,3},{2,0},{3,1},{4,6},{5,7},{6,4},{7,5},{8,10},{9,11},{10,... | collective-permute-start | bytes 196616 | tf_op jit(solution)/shard_map/ppermute | solution.py:116
  15.4 2.2 convolution_convert_fusion.solved_ref
  19.3 2.3 fusion
  21.5 2.5 %add_convert_fusion = bf16[16,512,128]{2,0,1:T(8,128)(2,1)S(1)} fusion(f32[16,512,128]{2,0,1:T(8,128)S(1)} %fusion, bf16[24,512,128]{2,1,0:T(8,128)(2,1)S(1)} %get-tuple-element.28, s32[24]{0:T(128)S(1)} %get-tuple-element.25), kind=kOutput, calls=%fused_computation.7 | convolution fusion | flops 52429184 | bytes 9437280 | tf_op jit(solution)/shard_map/sk,k...->s.../dot_general | solution.py:39
  26.6 4.2 %fusion.2 = f32[16,512,128]{2,0,1:T(8,128)} fusion(bf16[24,512,128]{2,1,0:T(8,128)(2,1)S(1)} %get-tuple-element.29, s32[24]{0:T(128)S(1)} %broadcast_add_fusion), kind=kOutput, calls=%fused_computation.12 | convolution fusion | flops 50332032 | bytes 7340128 | tf_op jit(solution)/shard_map/sk,k...->s.../dot_general | solution.py:40
  30.9 1.7 collective-permute-start.5
  33.3 1.5 gather_fusion.1
  35.7 6.0 %add_convert_fusion.1 = bf16[16,512,128]{2,0,1:T(8,128)(2,1)} fusion(f32[16,512,128]{2,0,1:T(8,128)} %fusion.2, bf16[24,512,128]{2,1,0:T(8,128)(2,1)S(1)} %get-tuple-element.28, s32[24]{0:T(128)S(1)} %broadcast_add_fusion), kind=kOutput, calls=%fused_computation.8 | convolution fusion | flops 52429184 | bytes 9437280 | tf_op jit(solution)/shard_map/sk,k...->s.../dot_general | solution.py:39
  41.9 2.3 pad_maximum_fusion
  47.1 1.8 collective-permute-start.1
  49.7 2.1 collective-permute-start.2
  52.2 2.6 %fusion.17 = bf16[8,16,16,128]{3,1,2,0:T(8,128)(2,1)} fusion(bf16[8,16,16,128]{3,1,2,0:T(8,128)(2,1)} %collective-permute-done.5, bf16[8,16,16,128]{3,1,2,0:T(8,128)(2,1)} %collective-permute-done.4, bf16[8,16,16,128]{3,1,2,0:T(8,128)(2,1)} %collective-permute-done.3, bf16[16,8,4,16,128]{4,0,3,2,1:T(8,128)(2,1)} %bitcast.120, s32[]{:T(128)S(6)} %select_n.125), kind=kLoop, calls=%fused_computation.37 | loop fusion | flops 2097152 | bytes 2621444 | tf_op jit(solution)/shard_map/convert_element_type | solution.py:139
  54.8 8.3 %all-to-all-start.1 = ((bf16[8,16,16,128]{3,1,2,0:T(8,128)(2,1)}), bf16[8,16,16,128]{3,1,2,0:T(8,128)(2,1)S(1)}, u32[]{:S(2)}, u32[]{:S(2)}) async-start(bf16[8,16,16,128]{3,1,2,0:T(8,128)(2,1)} %fusion.17), calls=%async_computation.1 | async-start | bytes 1048576 | tf_op jit(solution)/shard_map/all_to_all | solution.py:142
  63.5 9.5 %collective-permute-done.1 = bf16[8,17,16,128]{3,2,1,0:T(8,128)(2,1)S(1)} collective-permute-done((bf16[8,17,16,128]{3,2,1,0:T(8,128)(2,1)}, bf16[8,17,16,128]{3,2,1,0:T(8,128)(2,1)S(1)}, u32[]{:S(2)}, u32[]{:S(2)}) %collective-permute-start.1) | collective-permute-done | bytes 557088 | tf_op jit(solution)/shard_map/ppermute | solution.py:138
  73.0 2.4 %collective-permute-done.2 = bf16[8,17,16,128]{3,2,1,0:T(8,128)(2,1)S(1)} collective-permute-done((bf16[8,17,16,128]{3,2,1,0:T(8,128)(2,1)}, bf16[8,17,16,128]{3,2,1,0:T(8,128)(2,1)S(1)}, u32[]{:S(2)}, u32[]{:S(2)}) %collective-permute-start.2) | collective-permute-done | bytes 557088 | tf_op jit(solution)/shard_map/ppermute | solution.py:138
  78.9 6.0 %all-to-all-done.1 = bf16[8,16,16,128]{3,1,2,0:T(8,128)(2,1)S(1)} async-done(((bf16[8,16,16,128]{3,1,2,0:T(8,128)(2,1)}), bf16[8,16,16,128]{3,1,2,0:T(8,128)(2,1)S(1)}, u32[]{:S(2)}, u32[]{:S(2)}) %all-to-all-start.1) | async-done | bytes 524320 | tf_op jit(solution)/shard_map/all_to_all | solution.py:142
  84.9 3.5 %all-to-all-start = ((bf16[8,20,16,128]{3,2,1,0:T(8,128)(2,1)}), bf16[8,20,16,128]{3,2,1,0:T(8,128)(2,1)S(1)}, u32[]{:S(2)}, u32[]{:S(2)}) async-start(bf16[8,20,16,128]{3,2,1,0:T(8,128)(2,1)} %slice_dynamic-update-slice_fusion), calls=%async_computation | async-start | bytes 1310720 | tf_op jit(solution)/shard_map/all_to_all | solution.py:142
  89.9 16.3 %all-to-all-done = bf16[8,20,16,128]{3,2,1,0:T(8,128)(2,1)S(1)} async-done(((bf16[8,20,16,128]{3,2,1,0:T(8,128)(2,1)}), bf16[8,20,16,128]{3,2,1,0:T(8,128)(2,1)S(1)}, u32[]{:S(2)}, u32[]{:S(2)}) %all-to-all-start) | async-done | bytes 655392 | tf_op jit(solution)/shard_map/all_to_all | solution.py:142
  107.2 2.0 convolution_convert_fusion.2
  109.2 1.9 fusion.18
  112.1 3.7 %collective-permute-start.9 = (f32[4,16,128]{2,0,1:T(4,128)S(1)}, f32[4,16,128]{2,0,1:T(4,128)S(1)}, u32[]{:S(2)}, u32[]{:S(2)}) collective-permute-start(f32[4,16,128]{2,0,1:T(4,128)S(1)} %fusion.24), channel_id=1, source_target_pairs={{0,32},{32,0},{64,96},{96,64},{128,160},{160,128},{192,224},{224,1... | collective-permute-start | bytes 98312 | tf_op jit(solution)/shard_map/ppermute | solution.py:158
  118.0 1.6 collective-permute-done.10
  119.6 2.8 %collective-permute-start.11 = (f32[4,16,128]{2,0,1:T(4,128)S(1)}, f32[4,16,128]{2,0,1:T(4,128)S(1)}, u32[]{:S(2)}, u32[]{:S(2)}) collective-permute-start(f32[4,16,128]{2,0,1:T(4,128)S(1)} %add.177), channel_id=1, source_target_pairs={{0,128},{32,160},{64,192},{96,224},{128,0},{160,32},{192,64},{224,... | collective-permute-start | bytes 98312 | tf_op jit(solution)/shard_map/ppermute | solution.py:158
  122.5 1.5 collective-permute-done.11
  127.1 5.5 %collective-permute-start.13 = (bf16[44,16,128]{2,1,0:T(8,128)(2,1)S(1)}, bf16[44,16,128]{2,1,0:T(8,128)(2,1)S(1)}, u32[]{:S(2)}, u32[]{:S(2)}) collective-permute-start(bf16[44,16,128]{2,1,0:T(8,128)(2,1)S(1)} %get-tuple-element.38), channel_id=1, source_target_pairs={{0,2},{1,3},{2,0},{3,1},{4,6},{5,7},{6,4},{7,5},{8,10},{9,11},{10,... | collective-permute-start | bytes 540680 | tf_op jit(solution)/shard_map/ppermute | solution.py:177
  132.5 1.7 collective-permute-done.12
  134.2 4.1 %collective-permute-done.13 = bf16[44,16,128]{2,1,0:T(8,128)(2,1)S(1)} collective-permute-done((bf16[44,16,128]{2,1,0:T(8,128)(2,1)S(1)}, bf16[44,16,128]{2,1,0:T(8,128)(2,1)S(1)}, u32[]{:S(2)}, u32[]{:S(2)}) %collective-permute-start.13) | collective-permute-done | bytes 180256 | tf_op jit(solution)/shard_map/ppermute | solution.py:177
  142.5 65.7 %all-gather.5.cloned.1.call-done = bf16[32,44,16,128]{3,2,1,0:T(8,128)(2,1)} async-done(((bf16[4,44,16,128]{3,2,1,0:T(8,128)(2,1)}), bf16[32,44,16,128]{3,2,1,0:T(8,128)(2,1)}) %all-gather.5.cloned.1.call-update) | async-done | bytes 5767184 | tf_op jit(solution)/shard_map/all_gather | solution.py:179
  208.2 1.8 copy_bitcast_fusion
  214.2 5.5 %gather_fusion.5 = bf16[24,32,16,128]{3,2,1,0:T(8,128)(2,1)} fusion(bf16[32,44,16,128]{3,2,1,0:T(8,128)(2,1)} %all-gather.5.cloned.1.call-done, s32[1024]{0:T(1024)S(1)} %pad_clamp_fusion), kind=kCustom, calls=%fused_computation.5 | custom fusion | bytes 6291552 | tf_op jit(solution)/shard_map/gather | solution.py:185
  219.7 8.4 %shard_map.165 = bf16[24,128,512]{2,1,0:T(8,128)(2,1)} custom-call(bf16[24,32,16,128]{3,2,1,0:T(8,128)(2,1)} %gather_fusion.5, bf16[24,128,512]{2,1,0:T(8,128)(2,1)} %copy-done.2, bf16[24,128,128]{2,1,0:T(8,128)(2,1)} %bitcast.122, bf16[24,128,128]{2,1,0:T(8,128)(2,1)} %bitcast.123), custom_call_target="tpu_custom_call" | custom-call | flops 805306368 | bytes 11010048 | tf_op jit(solution)/shard_map/pallas_call | solution.py:67
  (113 shorter events, 34.6 us)
Async XLA Ops:
  7.2 8.2 %copy-start = (bf16[24,128,512]{2,1,0:T(8,128)(2,1)S(1)}, bf16[24,128,512]{2,1,0:T(8,128)(2,1)}, u32[]{:S(2)}) copy-start(bf16[24,128,512]{2,1,0:T(8,128)(2,1)} %param.14) | copy-start | bytes 9437188
  7.2 100.0 %all-gather.3.cloned.1.call-start = ((), (), s32[]{:S(2)}) async-start(), calls=%async_computation.2 | async-start | bytes 2359296 | tf_op jit(solution)/shard_map/all_gather | solution.py:118
  8.9 22.0 %collective-permute-start.6 = (bf16[2,128,128]{2,1,0:T(8,128)(2,1)S(1)}, bf16[2,128,128]{2,1,0:T(8,128)(2,1)S(1)}, u32[]{:S(2)}, u32[]{:S(2)}) collective-permute-start(bf16[2,128,128]{2,1,0:T(8,128)(2,1)S(1)} %constant_dynamic-update-slice_fusion), channel_id=1, source_target_pairs={{0,1},{1,2},{2,3},{3,0},{4,5},{5,6},{6,7},{7,4},{8,9},{9,10},{10,1... | collective-permute-start | bytes 196616 | tf_op jit(solution)/shard_map/ppermute | solution.py:116
  11.0 21.5 %collective-permute-start.7 = (bf16[2,128,128]{2,1,0:T(8,128)(2,1)S(1)}, bf16[2,128,128]{2,1,0:T(8,128)(2,1)S(1)}, u32[]{:S(2)}, u32[]{:S(2)}) collective-permute-start(bf16[2,128,128]{2,1,0:T(8,128)(2,1)S(1)} %constant_dynamic-update-slice_fusion), channel_id=1, source_target_pairs={{0,2},{1,3},{2,0},{3,1},{4,6},{5,7},{6,4},{7,5},{8,10},{9,11},{10,... | collective-permute-start | bytes 196616 | tf_op jit(solution)/shard_map/ppermute | solution.py:116
  13.7 18.9 %collective-permute-start.8 = (bf16[2,128,128]{2,1,0:T(8,128)(2,1)S(1)}, bf16[2,128,128]{2,1,0:T(8,128)(2,1)S(1)}, u32[]{:S(2)}, u32[]{:S(2)}) collective-permute-start(bf16[2,128,128]{2,1,0:T(8,128)(2,1)S(1)} %constant_dynamic-update-slice_fusion), channel_id=1, source_target_pairs={{0,3},{1,0},{2,1},{3,2},{4,7},{5,4},{6,5},{7,6},{8,11},{9,8},{10,9... | collective-permute-start | bytes 196616 | tf_op jit(solution)/shard_map/ppermute | solution.py:116
  15.4 2.2 copy-start.5
  24.0 6.9 %copy-start.3 = (bf16[16,512,128]{2,0,1:T(8,128)(2,1)}, bf16[16,512,128]{2,0,1:T(8,128)(2,1)S(1)}, u32[]{:S(2)}) copy-start(bf16[16,512,128]{2,0,1:T(8,128)(2,1)S(1)} %add_convert_fusion) | copy-start | bytes 6291460
  25.4 24.3 %collective-permute-start.3 = (bf16[8,16,16,128]{3,1,2,0:T(8,128)(2,1)}, bf16[8,16,16,128]{3,1,2,0:T(8,128)(2,1)}, u32[]{:S(2)}, u32[]{:S(2)}) collective-permute-start(bf16[8,16,16,128]{3,1,2,0:T(8,128)(2,1)} %get-tuple-element.34), channel_id=1, source_target_pairs={{0,1},{1,2},{2,3},{3,0},{4,5},{5,6},{6,7},{7,4},{8,9},{9,10},{10,1... | collective-permute-start | bytes 1572872 | tf_op jit(solution)/shard_map/ppermute | solution.py:138
  25.8 26.1 %collective-permute-start.4 = (bf16[8,16,16,128]{3,1,2,0:T(8,128)(2,1)}, bf16[8,16,16,128]{3,1,2,0:T(8,128)(2,1)}, u32[]{:S(2)}, u32[]{:S(2)}) collective-permute-start(bf16[8,16,16,128]{3,1,2,0:T(8,128)(2,1)} %get-tuple-element.35), channel_id=1, source_target_pairs={{0,2},{1,3},{2,0},{3,1},{4,6},{5,7},{6,4},{7,5},{8,10},{9,11},{10,... | collective-permute-start | bytes 1572872 | tf_op jit(solution)/shard_map/ppermute | solution.py:138
  30.9 21.3 %collective-permute-start.5 = (bf16[8,16,16,128]{3,1,2,0:T(8,128)(2,1)}, bf16[8,16,16,128]{3,1,2,0:T(8,128)(2,1)}, u32[]{:S(2)}, u32[]{:S(2)}) collective-permute-start(bf16[8,16,16,128]{3,1,2,0:T(8,128)(2,1)} %get-tuple-element.36), channel_id=1, source_target_pairs={{0,3},{1,0},{2,1},{3,2},{4,7},{5,4},{6,5},{7,6},{8,11},{9,8},{10,9... | collective-permute-start | bytes 1572872 | tf_op jit(solution)/shard_map/ppermute | solution.py:138
  35.7 6.0 %copy-start.11 = (bf16[1,128,512]{2,1,0:T(8,128)(2,1)S(1)}, bf16[1,128,512]{2,1,0:T(8,128)(2,1)}, u32[]{:S(2)}) copy-start(bf16[1,128,512]{2,1,0:T(8,128)(2,1)} %param.18) | copy-start | bytes 393220
  45.7 17.8 %collective-permute-start = (bf16[8,17,16,128]{3,2,1,0:T(8,128)(2,1)}, bf16[8,17,16,128]{3,2,1,0:T(8,128)(2,1)S(1)}, u32[]{:S(2)}, u32[]{:S(2)}) collective-permute-start(bf16[8,17,16,128]{3,2,1,0:T(8,128)(2,1)} %bitcast.116), channel_id=1, source_target_pairs={{0,1},{1,2},{2,3},{3,0},{4,5},{5,6},{6,7},{7,4},{8,9},{9,10},{10,1... | collective-permute-start | bytes 1671176 | tf_op jit(solution)/shard_map/ppermute | solution.py:138
  47.1 25.9 %collective-permute-start.1 = (bf16[8,17,16,128]{3,2,1,0:T(8,128)(2,1)}, bf16[8,17,16,128]{3,2,1,0:T(8,128)(2,1)S(1)}, u32[]{:S(2)}, u32[]{:S(2)}) collective-permute-start(bf16[8,17,16,128]{3,2,1,0:T(8,128)(2,1)} %bitcast.115), channel_id=1, source_target_pairs={{0,2},{1,3},{2,0},{3,1},{4,6},{5,7},{6,4},{7,5},{8,10},{9,11},{10,... | collective-permute-start | bytes 1671176 | tf_op jit(solution)/shard_map/ppermute | solution.py:138
  49.7 25.6 %collective-permute-start.2 = (bf16[8,17,16,128]{3,2,1,0:T(8,128)(2,1)}, bf16[8,17,16,128]{3,2,1,0:T(8,128)(2,1)S(1)}, u32[]{:S(2)}, u32[]{:S(2)}) collective-permute-start(bf16[8,17,16,128]{3,2,1,0:T(8,128)(2,1)} %bitcast.114), channel_id=1, source_target_pairs={{0,3},{1,0},{2,1},{3,2},{4,7},{5,4},{6,5},{7,6},{8,11},{9,8},{10,9... | collective-permute-start | bytes 1671176 | tf_op jit(solution)/shard_map/ppermute | solution.py:138
  54.8 35.0 %copy-start.12 = (s32[8]{0:T(128)S(1)}, s32[8]{0:T(128)}, u32[]{:S(2)}) copy-start(s32[8]{0:T(128)} %param.25) | copy-start | bytes 100
  54.8 35.0 %copy-start.13 = (s32[32]{0:T(128)S(1)}, s32[32]{0:T(128)}, u32[]{:S(2)}) copy-start(s32[32]{0:T(128)} %param.21) | copy-start | bytes 388
  54.8 30.1 %all-to-all-start.1 = ((bf16[8,16,16,128]{3,1,2,0:T(8,128)(2,1)}), bf16[8,16,16,128]{3,1,2,0:T(8,128)(2,1)S(1)}, u32[]{:S(2)}, u32[]{:S(2)}) async-start(bf16[8,16,16,128]{3,1,2,0:T(8,128)(2,1)} %fusion.17), calls=%async_computation.1 | async-start | bytes 1048576 | tf_op jit(solution)/shard_map/all_to_all | solution.py:142
  84.9 21.4 %all-to-all-start = ((bf16[8,20,16,128]{3,2,1,0:T(8,128)(2,1)}), bf16[8,20,16,128]{3,2,1,0:T(8,128)(2,1)S(1)}, u32[]{:S(2)}, u32[]{:S(2)}) async-start(bf16[8,20,16,128]{3,2,1,0:T(8,128)(2,1)} %slice_dynamic-update-slice_fusion), calls=%async_computation | async-start | bytes 1310720 | tf_op jit(solution)/shard_map/all_to_all | solution.py:142
  88.4 119.8 %all-gather.5.cloned.1.call-start = ((), (), s32[]{:S(2)}) async-start(), calls=%async_computation.3 | async-start | bytes 6488064 | tf_op jit(solution)/shard_map/all_gather | solution.py:179
  89.7 21.7 %copy-start.8 = (bf16[8,128,128]{2,1,0:T(8,128)(2,1)S(1)}, bf16[8,128,128]{2,1,0:T(8,128)(2,1)}, u32[]{:S(2)}) copy-start(bf16[8,128,128]{2,1,0:T(8,128)(2,1)} %param.23) | copy-start | bytes 786436
  89.9 21.8 %copy-start.9 = (bf16[8,128,128]{2,1,0:T(8,128)(2,1)S(1)}, bf16[8,128,128]{2,1,0:T(8,128)(2,1)}, u32[]{:S(2)}) copy-start(bf16[8,128,128]{2,1,0:T(8,128)(2,1)} %param.24) | copy-start | bytes 786436
  106.9 17.1 %copy-start.10 = (bf16[4,128,128]{2,1,0:T(8,128)(2,1)S(1)}, bf16[4,128,128]{2,1,0:T(8,128)(2,1)}, u32[]{:S(2)}) copy-start(bf16[4,128,128]{2,1,0:T(8,128)(2,1)} %param.27) | copy-start | bytes 393220
  107.2 18.6 %copy-start.4 = (bf16[32,2,128,128]{3,2,0,1:T(8,128)(2,1)S(1)}, bf16[32,2,128,128]{3,2,0,1:T(8,128)(2,1)}, u32[]{:S(2)}) copy-start(bf16[32,2,128,128]{3,2,0,1:T(8,128)(2,1)} %all-gather.3.cloned.1.call-done) | copy-start | bytes 6291460
  112.1 4.7 %collective-permute-start.9 = (f32[4,16,128]{2,0,1:T(4,128)S(1)}, f32[4,16,128]{2,0,1:T(4,128)S(1)}, u32[]{:S(2)}, u32[]{:S(2)}) collective-permute-start(f32[4,16,128]{2,0,1:T(4,128)S(1)} %fusion.24), channel_id=1, source_target_pairs={{0,32},{32,0},{64,96},{96,64},{128,160},{160,128},{192,224},{224,1... | collective-permute-start | bytes 98312 | tf_op jit(solution)/shard_map/ppermute | solution.py:158
  116.8 2.9 %collective-permute-start.10 = (f32[4,16,128]{2,0,1:T(4,128)S(1)}, f32[4,16,128]{2,0,1:T(4,128)S(1)}, u32[]{:S(2)}, u32[]{:S(2)}) collective-permute-start(f32[4,16,128]{2,0,1:T(4,128)S(1)} %add.176), channel_id=1, source_target_pairs={{0,64},{32,96},{64,0},{96,32},{128,192},{160,224},{192,128},{224,1... | collective-permute-start | bytes 98312 | tf_op jit(solution)/shard_map/ppermute | solution.py:158
  119.6 4.4 %collective-permute-start.11 = (f32[4,16,128]{2,0,1:T(4,128)S(1)}, f32[4,16,128]{2,0,1:T(4,128)S(1)}, u32[]{:S(2)}, u32[]{:S(2)}) collective-permute-start(f32[4,16,128]{2,0,1:T(4,128)S(1)} %add.177), channel_id=1, source_target_pairs={{0,128},{32,160},{64,192},{96,224},{128,0},{160,32},{192,64},{224,... | collective-permute-start | bytes 98312 | tf_op jit(solution)/shard_map/ppermute | solution.py:158
  126.4 13.7 %copy-start.6 = (bf16[24,128,128]{2,1,0:T(8,128)(2,1)S(1)}, bf16[24,128,128]{2,1,0:T(8,128)(2,1)}, u32[]{:S(2)}) copy-start(bf16[24,128,128]{2,1,0:T(8,128)(2,1)} %param.16) | copy-start | bytes 2359300
  126.5 7.8 %collective-permute-start.12 = (bf16[44,16,128]{2,1,0:T(8,128)(2,1)S(1)}, bf16[44,16,128]{2,1,0:T(8,128)(2,1)S(1)}, u32[]{:S(2)}, u32[]{:S(2)}) collective-permute-start(bf16[44,16,128]{2,1,0:T(8,128)(2,1)S(1)} %get-tuple-element.38), channel_id=1, source_target_pairs={{0,1},{1,2},{2,3},{3,0},{4,5},{5,6},{6,7},{7,4},{8,9},{9,10},{10,1... | collective-permute-start | bytes 540680 | tf_op jit(solution)/shard_map/ppermute | solution.py:177
  127.1 11.2 %collective-permute-start.13 = (bf16[44,16,128]{2,1,0:T(8,128)(2,1)S(1)}, bf16[44,16,128]{2,1,0:T(8,128)(2,1)S(1)}, u32[]{:S(2)}, u32[]{:S(2)}) collective-permute-start(bf16[44,16,128]{2,1,0:T(8,128)(2,1)S(1)} %get-tuple-element.38), channel_id=1, source_target_pairs={{0,2},{1,3},{2,0},{3,1},{4,6},{5,7},{6,4},{7,5},{8,10},{9,11},{10,... | collective-permute-start | bytes 540680 | tf_op jit(solution)/shard_map/ppermute | solution.py:177
  132.5 5.8 %collective-permute-start.14 = (bf16[44,16,128]{2,1,0:T(8,128)(2,1)S(1)}, bf16[44,16,128]{2,1,0:T(8,128)(2,1)S(1)}, u32[]{:S(2)}, u32[]{:S(2)}) collective-permute-start(bf16[44,16,128]{2,1,0:T(8,128)(2,1)S(1)} %get-tuple-element.38), channel_id=1, source_target_pairs={{0,3},{1,0},{2,1},{3,2},{4,7},{5,4},{6,5},{7,6},{8,11},{9,8},{10,9... | collective-permute-start | bytes 540680 | tf_op jit(solution)/shard_map/ppermute | solution.py:177
  138.3 3.0 %copy-start.7 = (bf16[24,128,128]{2,1,0:T(8,128)(2,1)S(1)}, bf16[24,128,128]{2,1,0:T(8,128)(2,1)}, u32[]{:S(2)}) copy-start(bf16[24,128,128]{2,1,0:T(8,128)(2,1)} %param.15) | copy-start | bytes 2359300
  219.7 8.4 %copy-start.1 = (bf16[24,128,512]{2,1,0:T(8,128)(2,1)S(1)}, bf16[24,128,512]{2,1,0:T(8,128)(2,1)}, u32[]{:S(2)}) copy-start(bf16[24,128,512]{2,1,0:T(8,128)(2,1)} %param.14) | copy-start | bytes 9437188
  (1 other events, 1.7 us)
Sparse Core Ops, SparseCore 0:
  35.8 51.7 all-gather.2
  140.2 67.9 all-gather.4

commit v13 on v12

--- a/solution.py
+++ b/solution.py
@@ -146,11 +146,11 @@
     own_rhs = jnp.take(incoming[:, half:], offsets, axis=1).reshape(peers, chunk, width)
     node_y = (own_rhs.astype(jnp.float32) - node_sum).astype(jnp.bfloat16)
     node_solved = piece_block(row_inverse, node_y).astype(jnp.bfloat16)
-    middle_sum = slot_sums(middle_target, middle_count, piece_block(row_link, node_solved))
+    middle_sum = split_slot_sums(middle_target, middle_count, piece_block(row_link, node_solved))
     middle_piece = lax.dynamic_slice_in_dim(middle_rhs, start, chunk, 2).transpose(0, 2, 1)
     middle_y = (middle_piece.astype(jnp.float32) - middle_sum).astype(jnp.bfloat16)
     middle_solved = piece_block(middle_inverse, middle_y).astype(jnp.bfloat16)
-    top_term = slot_sums(middle_parent, top_count, piece_block(middle_link, middle_solved))
+    top_term = split_slot_sums(middle_parent, top_count, piece_block(middle_link, middle_solved))
     top_sum = top_term
     rows = lax.axis_size(ROW)
     step = 1

time: 236 us -> 236 us (level)
    dot_general x2 -> x4, matrix products: 8.46 us -> 8.76 us  [split_slot_sums(): jnp.einsum('sk,k...->s...', select, high, preferred_element_type=jnp.floa...]
    dot_general x2 -> x4, matrix products: 6.5 us -> 6.76 us  [split_slot_sums(): jnp.einsum('sk,k...->s...', select, low, preferred_element_type=jnp.float32)]
where the time goes in v13:
time: 236 us; the launch traced here: 235 us
  waiting for transfers between devices  109 us (46%)
  starting transfers between devices  38.8 us (16%)
  local copies, waits for them, and re-layouts  28.7 us (12%)
  matrix products  24.7 us (10%)
  between operations  14.5 us (6%)
  other arithmetic  10.7 us (5%)
  Pallas kernels  8.38 us (4%)
    all_gather x1, waiting for transfers between devices, local(): gathered = lax.all_gather(by_y, 'z', axis=0, tiled=True)  65.4 us
    all_to_all x2, waiting for transfers between devices, local(): incoming = lax.all_to_all(partial, 'z', 0, 0, tiled=True)  22.3 us
    ppermute x6, waiting for transfers between devices, local(): arrivals.append(lax.ppermute(outbound, 'y', pairs))  12.6 us
    all_to_all x2, starting transfers between devices, local(): incoming = lax.all_to_all(partial, 'z', 0, 0, tiled=True)  11.9 us
    unnamed x44, local copies, waits for them, and re-layouts  11.7 us
    dot_general x4, matrix products, split_slot_sums(): jnp.einsum('sk,k...->s...', select, high, preferred_element_type=jnp.floa...  8.76 us
    pallas_call x1, Pallas kernels, leaf_backward(): pl.pallas_call(leaf_backward_kernel, grid=(count // per_step,), in_specs=...  8.38 us
    ppermute x3, starting transfers between devices, local(): lax.ppermute(top_sum, ROW, [(i, i ^ step) for i in range(rows)])  7.65 us
  transfers between devices with their start and end apart: 19, of which 11 were waited for; matrix products, arithmetic and copies ran while one was open for 18% of the time, Pallas kernels for 0%

profile of v13, /device:TPU:1, one launch (start us, length us, event | category | flops | bytes accessed | tf_op | source)
XLA Modules:
  0.0 234.9 jit_solution(4386299634274451037)
XLA Ops:
  8.9 2.1 collective-permute-start.6
  11.0 2.6 %collective-permute-start.7 = (bf16[2,128,128]{2,1,0:T(8,128)(2,1)S(1)}, bf16[2,128,128]{2,1,0:T(8,128)(2,1)S(1)}, u32[]{:S(2)}, u32[]{:S(2)}) collective-permute-start(bf16[2,128,128]{2,1,0:T(8,128)(2,1)S(1)} %constant_dynamic-update-slice_fusion), channel_id=1, source_target_pairs={{0,2},{1,3},{2,0},{3,1},{4,6},{5,7},{6,4},{7,5},{8,10},{9,11},{10,... | collective-permute-start | bytes 196616 | tf_op jit(solution)/shard_map/ppermute | solution.py:116
  15.4 2.2 convolution_convert_fusion.solved_ref
  19.3 2.3 fusion
  21.5 2.5 %add_convert_fusion = bf16[16,512,128]{2,0,1:T(8,128)(2,1)S(1)} fusion(f32[16,512,128]{2,0,1:T(8,128)S(1)} %fusion, bf16[24,512,128]{2,1,0:T(8,128)(2,1)S(1)} %get-tuple-element.32, s32[24]{0:T(128)S(1)} %get-tuple-element.25), kind=kOutput, calls=%fused_computation.7 | convolution fusion | flops 52429184 | bytes 9437280 | tf_op jit(solution)/shard_map/sk,k...->s.../dot_general | solution.py:39
  26.6 4.2 %fusion.2 = f32[16,512,128]{2,0,1:T(8,128)} fusion(bf16[24,512,128]{2,1,0:T(8,128)(2,1)S(1)} %get-tuple-element.33, s32[24]{0:T(128)S(1)} %broadcast_add_fusion), kind=kOutput, calls=%fused_computation.12 | convolution fusion | flops 50332032 | bytes 7340128 | tf_op jit(solution)/shard_map/sk,k...->s.../dot_general | solution.py:40
  30.9 1.7 collective-permute-start.5
  33.3 1.5 gather_fusion.1
  35.7 6.0 %add_convert_fusion.1 = bf16[16,512,128]{2,0,1:T(8,128)(2,1)} fusion(f32[16,512,128]{2,0,1:T(8,128)} %fusion.2, bf16[24,512,128]{2,1,0:T(8,128)(2,1)S(1)} %get-tuple-element.32, s32[24]{0:T(128)S(1)} %broadcast_add_fusion), kind=kOutput, calls=%fused_computation.8 | convolution fusion | flops 52429184 | bytes 9437280 | tf_op jit(solution)/shard_map/sk,k...->s.../dot_general | solution.py:39
  41.9 2.3 pad_maximum_fusion
  47.0 1.8 collective-permute-start.1
  49.7 2.1 collective-permute-start.2
  52.2 2.6 %fusion.18 = bf16[8,16,16,128]{3,1,2,0:T(8,128)(2,1)} fusion(bf16[8,16,16,128]{3,1,2,0:T(8,128)(2,1)} %collective-permute-done.5, bf16[8,16,16,128]{3,1,2,0:T(8,128)(2,1)} %collective-permute-done.4, bf16[8,16,16,128]{3,1,2,0:T(8,128)(2,1)} %collective-permute-done.3, bf16[16,8,4,16,128]{4,0,3,2,1:T(8,128)(2,1)} %bitcast.124, s32[]{:T(128)S(6)} %select_n.125), kind=kLoop, calls=%fused_computation.39 | loop fusion | flops 2097152 | bytes 2621444 | tf_op jit(solution)/shard_map/convert_element_type | solution.py:139
  54.8 8.3 %all-to-all-start.1 = ((bf16[8,16,16,128]{3,1,2,0:T(8,128)(2,1)}), bf16[8,16,16,128]{3,1,2,0:T(8,128)(2,1)S(1)}, u32[]{:S(2)}, u32[]{:S(2)}) async-start(bf16[8,16,16,128]{3,1,2,0:T(8,128)(2,1)} %fusion.18), calls=%async_computation.1 | async-start | bytes 1048576 | tf_op jit(solution)/shard_map/all_to_all | solution.py:142
  63.5 9.5 %collective-permute-done.1 = bf16[8,17,16,128]{3,2,1,0:T(8,128)(2,1)S(1)} collective-permute-done((bf16[8,17,16,128]{3,2,1,0:T(8,128)(2,1)}, bf16[8,17,16,128]{3,2,1,0:T(8,128)(2,1)S(1)}, u32[]{:S(2)}, u32[]{:S(2)}) %collective-permute-start.1) | collective-permute-done | bytes 557088 | tf_op jit(solution)/shard_map/ppermute | solution.py:138
  73.0 2.4 %collective-permute-done.2 = bf16[8,17,16,128]{3,2,1,0:T(8,128)(2,1)S(1)} collective-permute-done((bf16[8,17,16,128]{3,2,1,0:T(8,128)(2,1)}, bf16[8,17,16,128]{3,2,1,0:T(8,128)(2,1)S(1)}, u32[]{:S(2)}, u32[]{:S(2)}) %collective-permute-start.2) | collective-permute-done | bytes 557088 | tf_op jit(solution)/shard_map/ppermute | solution.py:138
  78.9 6.0 %all-to-all-done.1 = bf16[8,16,16,128]{3,1,2,0:T(8,128)(2,1)S(1)} async-done(((bf16[8,16,16,128]{3,1,2,0:T(8,128)(2,1)}), bf16[8,16,16,128]{3,1,2,0:T(8,128)(2,1)S(1)}, u32[]{:S(2)}, u32[]{:S(2)}) %all-to-all-start.1) | async-done | bytes 524320 | tf_op jit(solution)/shard_map/all_to_all | solution.py:142
  84.8 3.5 %all-to-all-start = ((bf16[8,20,16,128]{3,2,1,0:T(8,128)(2,1)}), bf16[8,20,16,128]{3,2,1,0:T(8,128)(2,1)S(1)}, u32[]{:S(2)}, u32[]{:S(2)}) async-start(bf16[8,20,16,128]{3,2,1,0:T(8,128)(2,1)} %slice_dynamic-update-slice_fusion), calls=%async_computation | async-start | bytes 1310720 | tf_op jit(solution)/shard_map/all_to_all | solution.py:142
  89.9 16.3 %all-to-all-done = bf16[8,20,16,128]{3,2,1,0:T(8,128)(2,1)S(1)} async-done(((bf16[8,20,16,128]{3,2,1,0:T(8,128)(2,1)}), bf16[8,20,16,128]{3,2,1,0:T(8,128)(2,1)S(1)}, u32[]{:S(2)}, u32[]{:S(2)}) %all-to-all-start) | async-done | bytes 655392 | tf_op jit(solution)/shard_map/all_to_all | solution.py:142
  107.2 2.0 convolution_convert_fusion.2
  109.2 1.9 subtract_convert_fusion.1
  112.1 3.6 %collective-permute-start.9 = (f32[4,16,128]{2,0,1:T(4,128)S(1)}, f32[4,16,128]{2,0,1:T(4,128)S(1)}, u32[]{:S(2)}, u32[]{:S(2)}) collective-permute-start(f32[4,16,128]{2,0,1:T(4,128)S(1)} %convolution_add_fusion.1), channel_id=1, source_target_pairs={{0,32},{32,0},{64,96},{96,64},{128,160},{160,128},{192,224},{224,1... | collective-permute-start | bytes 98312 | tf_op jit(solution)/shard_map/ppermute | solution.py:158
  118.1 1.6 collective-permute-done.10
  119.7 2.8 %collective-permute-start.11 = (f32[4,16,128]{2,0,1:T(4,128)S(1)}, f32[4,16,128]{2,0,1:T(4,128)S(1)}, u32[]{:S(2)}, u32[]{:S(2)}) collective-permute-start(f32[4,16,128]{2,0,1:T(4,128)S(1)} %add.185), channel_id=1, source_target_pairs={{0,128},{32,160},{64,192},{96,224},{128,0},{160,32},{192,64},{224,... | collective-permute-start | bytes 98312 | tf_op jit(solution)/shard_map/ppermute | solution.py:158
  122.5 1.5 collective-permute-done.11
  127.0 5.7 %collective-permute-start.13 = (bf16[44,16,128]{2,1,0:T(8,128)(2,1)S(1)}, bf16[44,16,128]{2,1,0:T(8,128)(2,1)S(1)}, u32[]{:S(2)}, u32[]{:S(2)}) collective-permute-start(bf16[44,16,128]{2,1,0:T(8,128)(2,1)S(1)} %get-tuple-element.42), channel_id=1, source_target_pairs={{0,2},{1,3},{2,0},{3,1},{4,6},{5,7},{6,4},{7,5},{8,10},{9,11},{10,... | collective-permute-start | bytes 540680 | tf_op jit(solution)/shard_map/ppermute | solution.py:177
  132.7 1.7 collective-permute-done.12
  134.4 4.1 %collective-permute-done.13 = bf16[44,16,128]{2,1,0:T(8,128)(2,1)S(1)} collective-permute-done((bf16[44,16,128]{2,1,0:T(8,128)(2,1)S(1)}, bf16[44,16,128]{2,1,0:T(8,128)(2,1)S(1)}, u32[]{:S(2)}, u32[]{:S(2)}) %collective-permute-start.13) | collective-permute-done | bytes 180256 | tf_op jit(solution)/shard_map/ppermute | solution.py:177
  142.7 65.4 %all-gather.5.cloned.1.call-done = bf16[32,44,16,128]{3,2,1,0:T(8,128)(2,1)} async-done(((bf16[4,44,16,128]{3,2,1,0:T(8,128)(2,1)}), bf16[32,44,16,128]{3,2,1,0:T(8,128)(2,1)}) %all-gather.5.cloned.1.call-update) | async-done | bytes 5767184 | tf_op jit(solution)/shard_map/all_gather | solution.py:179
  208.1 1.8 copy_bitcast_fusion
  214.2 5.5 %gather_fusion.5 = bf16[24,32,16,128]{3,2,1,0:T(8,128)(2,1)} fusion(bf16[32,44,16,128]{3,2,1,0:T(8,128)(2,1)} %all-gather.5.cloned.1.call-done, s32[1024]{0:T(1024)S(1)} %pad_clamp_fusion), kind=kCustom, calls=%fused_computation.5 | custom fusion | bytes 6291552 | tf_op jit(solution)/shard_map/gather | solution.py:185
  219.7 8.4 %shard_map.165 = bf16[24,128,512]{2,1,0:T(8,128)(2,1)} custom-call(bf16[24,32,16,128]{3,2,1,0:T(8,128)(2,1)} %gather_fusion.5, bf16[24,128,512]{2,1,0:T(8,128)(2,1)} %copy-done.2, bf16[24,128,128]{2,1,0:T(8,128)(2,1)} %bitcast.126, bf16[24,128,128]{2,1,0:T(8,128)(2,1)} %bitcast.127), custom_call_target="tpu_custom_call" | custom-call | flops 805306368 | bytes 11010048 | tf_op jit(solution)/shard_map/pallas_call | solution.py:67
  (115 shorter events, 34.7 us)
Async XLA Ops:
  7.2 8.2 %copy-start = (bf16[24,128,512]{2,1,0:T(8,128)(2,1)S(1)}, bf16[24,128,512]{2,1,0:T(8,128)(2,1)}, u32[]{:S(2)}) copy-start(bf16[24,128,512]{2,1,0:T(8,128)(2,1)} %param.14) | copy-start | bytes 9437188
  7.2 100.0 %all-gather.3.cloned.1.call-start = ((), (), s32[]{:S(2)}) async-start(), calls=%async_computation.2 | async-start | bytes 2359296 | tf_op jit(solution)/shard_map/all_gather | solution.py:118
  8.9 22.0 %collective-permute-start.6 = (bf16[2,128,128]{2,1,0:T(8,128)(2,1)S(1)}, bf16[2,128,128]{2,1,0:T(8,128)(2,1)S(1)}, u32[]{:S(2)}, u32[]{:S(2)}) collective-permute-start(bf16[2,128,128]{2,1,0:T(8,128)(2,1)S(1)} %constant_dynamic-update-slice_fusion), channel_id=1, source_target_pairs={{0,1},{1,2},{2,3},{3,0},{4,5},{5,6},{6,7},{7,4},{8,9},{9,10},{10,1... | collective-permute-start | bytes 196616 | tf_op jit(solution)/shard_map/ppermute | solution.py:116
  11.0 21.5 %collective-permute-start.7 = (bf16[2,128,128]{2,1,0:T(8,128)(2,1)S(1)}, bf16[2,128,128]{2,1,0:T(8,128)(2,1)S(1)}, u32[]{:S(2)}, u32[]{:S(2)}) collective-permute-start(bf16[2,128,128]{2,1,0:T(8,128)(2,1)S(1)} %constant_dynamic-update-slice_fusion), channel_id=1, source_target_pairs={{0,2},{1,3},{2,0},{3,1},{4,6},{5,7},{6,4},{7,5},{8,10},{9,11},{10,... | collective-permute-start | bytes 196616 | tf_op jit(solution)/shard_map/ppermute | solution.py:116
  13.7 18.9 %collective-permute-start.8 = (bf16[2,128,128]{2,1,0:T(8,128)(2,1)S(1)}, bf16[2,128,128]{2,1,0:T(8,128)(2,1)S(1)}, u32[]{:S(2)}, u32[]{:S(2)}) collective-permute-start(bf16[2,128,128]{2,1,0:T(8,128)(2,1)S(1)} %constant_dynamic-update-slice_fusion), channel_id=1, source_target_pairs={{0,3},{1,0},{2,1},{3,2},{4,7},{5,4},{6,5},{7,6},{8,11},{9,8},{10,9... | collective-permute-start | bytes 196616 | tf_op jit(solution)/shard_map/ppermute | solution.py:116
  15.4 2.2 copy-start.5
  24.0 6.8 %copy-start.3 = (bf16[16,512,128]{2,0,1:T(8,128)(2,1)}, bf16[16,512,128]{2,0,1:T(8,128)(2,1)S(1)}, u32[]{:S(2)}) copy-start(bf16[16,512,128]{2,0,1:T(8,128)(2,1)S(1)} %add_convert_fusion) | copy-start | bytes 6291460
  25.4 24.3 %collective-permute-start.3 = (bf16[8,16,16,128]{3,1,2,0:T(8,128)(2,1)}, bf16[8,16,16,128]{3,1,2,0:T(8,128)(2,1)}, u32[]{:S(2)}, u32[]{:S(2)}) collective-permute-start(bf16[8,16,16,128]{3,1,2,0:T(8,128)(2,1)} %get-tuple-element.38), channel_id=1, source_target_pairs={{0,1},{1,2},{2,3},{3,0},{4,5},{5,6},{6,7},{7,4},{8,9},{9,10},{10,1... | collective-permute-start | bytes 1572872 | tf_op jit(solution)/shard_map/ppermute | solution.py:138
  25.8 26.0 %collective-permute-start.4 = (bf16[8,16,16,128]{3,1,2,0:T(8,128)(2,1)}, bf16[8,16,16,128]{3,1,2,0:T(8,128)(2,1)}, u32[]{:S(2)}, u32[]{:S(2)}) collective-permute-start(bf16[8,16,16,128]{3,1,2,0:T(8,128)(2,1)} %get-tuple-element.39), channel_id=1, source_target_pairs={{0,2},{1,3},{2,0},{3,1},{4,6},{5,7},{6,4},{7,5},{8,10},{9,11},{10,... | collective-permute-start | bytes 1572872 | tf_op jit(solution)/shard_map/ppermute | solution.py:138
  30.9 21.4 %collective-permute-start.5 = (bf16[8,16,16,128]{3,1,2,0:T(8,128)(2,1)}, bf16[8,16,16,128]{3,1,2,0:T(8,128)(2,1)}, u32[]{:S(2)}, u32[]{:S(2)}) collective-permute-start(bf16[8,16,16,128]{3,1,2,0:T(8,128)(2,1)} %get-tuple-element.40), channel_id=1, source_target_pairs={{0,3},{1,0},{2,1},{3,2},{4,7},{5,4},{6,5},{7,6},{8,11},{9,8},{10,9... | collective-permute-start | bytes 1572872 | tf_op jit(solution)/shard_map/ppermute | solution.py:138
  35.7 6.0 %copy-start.11 = (bf16[1,128,512]{2,1,0:T(8,128)(2,1)S(1)}, bf16[1,128,512]{2,1,0:T(8,128)(2,1)}, u32[]{:S(2)}) copy-start(bf16[1,128,512]{2,1,0:T(8,128)(2,1)} %param.18) | copy-start | bytes 393220
  45.7 17.8 %collective-permute-start = (bf16[8,17,16,128]{3,2,1,0:T(8,128)(2,1)}, bf16[8,17,16,128]{3,2,1,0:T(8,128)(2,1)S(1)}, u32[]{:S(2)}, u32[]{:S(2)}) collective-permute-start(bf16[8,17,16,128]{3,2,1,0:T(8,128)(2,1)} %bitcast.120), channel_id=1, source_target_pairs={{0,1},{1,2},{2,3},{3,0},{4,5},{5,6},{6,7},{7,4},{8,9},{9,10},{10,1... | collective-permute-start | bytes 1671176 | tf_op jit(solution)/shard_map/ppermute | solution.py:138
  47.0 25.9 %collective-permute-start.1 = (bf16[8,17,16,128]{3,2,1,0:T(8,128)(2,1)}, bf16[8,17,16,128]{3,2,1,0:T(8,128)(2,1)S(1)}, u32[]{:S(2)}, u32[]{:S(2)}) collective-permute-start(bf16[8,17,16,128]{3,2,1,0:T(8,128)(2,1)} %bitcast.119), channel_id=1, source_target_pairs={{0,2},{1,3},{2,0},{3,1},{4,6},{5,7},{6,4},{7,5},{8,10},{9,11},{10,... | collective-permute-start | bytes 1671176 | tf_op jit(solution)/shard_map/ppermute | solution.py:138
  49.7 25.6 %collective-permute-start.2 = (bf16[8,17,16,128]{3,2,1,0:T(8,128)(2,1)}, bf16[8,17,16,128]{3,2,1,0:T(8,128)(2,1)S(1)}, u32[]{:S(2)}, u32[]{:S(2)}) collective-permute-start(bf16[8,17,16,128]{3,2,1,0:T(8,128)(2,1)} %bitcast.118), channel_id=1, source_target_pairs={{0,3},{1,0},{2,1},{3,2},{4,7},{5,4},{6,5},{7,6},{8,11},{9,8},{10,9... | collective-permute-start | bytes 1671176 | tf_op jit(solution)/shard_map/ppermute | solution.py:138
  54.8 35.0 %copy-start.12 = (s32[8]{0:T(128)S(1)}, s32[8]{0:T(128)}, u32[]{:S(2)}) copy-start(s32[8]{0:T(128)} %param.25) | copy-start | bytes 100
  54.8 35.0 %copy-start.13 = (s32[32]{0:T(128)S(1)}, s32[32]{0:T(128)}, u32[]{:S(2)}) copy-start(s32[32]{0:T(128)} %param.21) | copy-start | bytes 388
  54.8 30.0 %all-to-all-start.1 = ((bf16[8,16,16,128]{3,1,2,0:T(8,128)(2,1)}), bf16[8,16,16,128]{3,1,2,0:T(8,128)(2,1)S(1)}, u32[]{:S(2)}, u32[]{:S(2)}) async-start(bf16[8,16,16,128]{3,1,2,0:T(8,128)(2,1)} %fusion.18), calls=%async_computation.1 | async-start | bytes 1048576 | tf_op jit(solution)/shard_map/all_to_all | solution.py:142
  84.8 21.4 %all-to-all-start = ((bf16[8,20,16,128]{3,2,1,0:T(8,128)(2,1)}), bf16[8,20,16,128]{3,2,1,0:T(8,128)(2,1)S(1)}, u32[]{:S(2)}, u32[]{:S(2)}) async-start(bf16[8,20,16,128]{3,2,1,0:T(8,128)(2,1)} %slice_dynamic-update-slice_fusion), calls=%async_computation | async-start | bytes 1310720 | tf_op jit(solution)/shard_map/all_to_all | solution.py:142
  88.4 119.8 %all-gather.5.cloned.1.call-start = ((), (), s32[]{:S(2)}) async-start(), calls=%async_computation.3 | async-start | bytes 6488064 | tf_op jit(solution)/shard_map/all_gather | solution.py:179
  89.6 21.7 %copy-start.8 = (bf16[8,128,128]{2,1,0:T(8,128)(2,1)S(1)}, bf16[8,128,128]{2,1,0:T(8,128)(2,1)}, u32[]{:S(2)}) copy-start(bf16[8,128,128]{2,1,0:T(8,128)(2,1)} %param.23) | copy-start | bytes 786436
  89.8 21.8 %copy-start.9 = (bf16[8,128,128]{2,1,0:T(8,128)(2,1)S(1)}, bf16[8,128,128]{2,1,0:T(8,128)(2,1)}, u32[]{:S(2)}) copy-start(bf16[8,128,128]{2,1,0:T(8,128)(2,1)} %param.24) | copy-start | bytes 786436
  106.9 17.2 %copy-start.10 = (bf16[4,128,128]{2,1,0:T(8,128)(2,1)S(1)}, bf16[4,128,128]{2,1,0:T(8,128)(2,1)}, u32[]{:S(2)}) copy-start(bf16[4,128,128]{2,1,0:T(8,128)(2,1)} %param.27) | copy-start | bytes 393220
  107.1 18.7 %copy-start.4 = (bf16[32,2,128,128]{3,2,0,1:T(8,128)(2,1)S(1)}, bf16[32,2,128,128]{3,2,0,1:T(8,128)(2,1)}, u32[]{:S(2)}) copy-start(bf16[32,2,128,128]{3,2,0,1:T(8,128)(2,1)} %all-gather.3.cloned.1.call-done) | copy-start | bytes 6291460
  112.1 4.6 %collective-permute-start.9 = (f32[4,16,128]{2,0,1:T(4,128)S(1)}, f32[4,16,128]{2,0,1:T(4,128)S(1)}, u32[]{:S(2)}, u32[]{:S(2)}) collective-permute-start(f32[4,16,128]{2,0,1:T(4,128)S(1)} %convolution_add_fusion.1), channel_id=1, source_target_pairs={{0,32},{32,0},{64,96},{96,64},{128,160},{160,128},{192,224},{224,1... | collective-permute-start | bytes 98312 | tf_op jit(solution)/shard_map/ppermute | solution.py:158
  116.8 2.9 %collective-permute-start.10 = (f32[4,16,128]{2,0,1:T(4,128)S(1)}, f32[4,16,128]{2,0,1:T(4,128)S(1)}, u32[]{:S(2)}, u32[]{:S(2)}) collective-permute-start(f32[4,16,128]{2,0,1:T(4,128)S(1)} %add.184), channel_id=1, source_target_pairs={{0,64},{32,96},{64,0},{96,32},{128,192},{160,224},{192,128},{224,1... | collective-permute-start | bytes 98312 | tf_op jit(solution)/shard_map/ppermute | solution.py:158
  119.7 4.4 %collective-permute-start.11 = (f32[4,16,128]{2,0,1:T(4,128)S(1)}, f32[4,16,128]{2,0,1:T(4,128)S(1)}, u32[]{:S(2)}, u32[]{:S(2)}) collective-permute-start(f32[4,16,128]{2,0,1:T(4,128)S(1)} %add.185), channel_id=1, source_target_pairs={{0,128},{32,160},{64,192},{96,224},{128,0},{160,32},{192,64},{224,... | collective-permute-start | bytes 98312 | tf_op jit(solution)/shard_map/ppermute | solution.py:158
  126.5 13.8 %copy-start.6 = (bf16[24,128,128]{2,1,0:T(8,128)(2,1)S(1)}, bf16[24,128,128]{2,1,0:T(8,128)(2,1)}, u32[]{:S(2)}) copy-start(bf16[24,128,128]{2,1,0:T(8,128)(2,1)} %param.16) | copy-start | bytes 2359300
  126.5 7.9 %collective-permute-start.12 = (bf16[44,16,128]{2,1,0:T(8,128)(2,1)S(1)}, bf16[44,16,128]{2,1,0:T(8,128)(2,1)S(1)}, u32[]{:S(2)}, u32[]{:S(2)}) collective-permute-start(bf16[44,16,128]{2,1,0:T(8,128)(2,1)S(1)} %get-tuple-element.42), channel_id=1, source_target_pairs={{0,1},{1,2},{2,3},{3,0},{4,5},{5,6},{6,7},{7,4},{8,9},{9,10},{10,1... | collective-permute-start | bytes 540680 | tf_op jit(solution)/shard_map/ppermute | solution.py:177
  127.0 11.4 %collective-permute-start.13 = (bf16[44,16,128]{2,1,0:T(8,128)(2,1)S(1)}, bf16[44,16,128]{2,1,0:T(8,128)(2,1)S(1)}, u32[]{:S(2)}, u32[]{:S(2)}) collective-permute-start(bf16[44,16,128]{2,1,0:T(8,128)(2,1)S(1)} %get-tuple-element.42), channel_id=1, source_target_pairs={{0,2},{1,3},{2,0},{3,1},{4,6},{5,7},{6,4},{7,5},{8,10},{9,11},{10,... | collective-permute-start | bytes 540680 | tf_op jit(solution)/shard_map/ppermute | solution.py:177
  132.7 5.8 %collective-permute-start.14 = (bf16[44,16,128]{2,1,0:T(8,128)(2,1)S(1)}, bf16[44,16,128]{2,1,0:T(8,128)(2,1)S(1)}, u32[]{:S(2)}, u32[]{:S(2)}) collective-permute-start(bf16[44,16,128]{2,1,0:T(8,128)(2,1)S(1)} %get-tuple-element.42), channel_id=1, source_target_pairs={{0,3},{1,0},{2,1},{3,2},{4,7},{5,4},{6,5},{7,6},{8,11},{9,8},{10,9... | collective-permute-start | bytes 540680 | tf_op jit(solution)/shard_map/ppermute | solution.py:177
  138.5 3.1 %copy-start.7 = (bf16[24,128,128]{2,1,0:T(8,128)(2,1)S(1)}, bf16[24,128,128]{2,1,0:T(8,128)(2,1)}, u32[]{:S(2)}) copy-start(bf16[24,128,128]{2,1,0:T(8,128)(2,1)} %param.15) | copy-start | bytes 2359300
  219.7 8.4 %copy-start.1 = (bf16[24,128,512]{2,1,0:T(8,128)(2,1)S(1)}, bf16[24,128,512]{2,1,0:T(8,128)(2,1)}, u32[]{:S(2)}) copy-start(bf16[24,128,512]{2,1,0:T(8,128)(2,1)} %param.14) | copy-start | bytes 9437188
  (1 other events, 1.7 us)
Sparse Core Ops, SparseCore 0:
  35.8 51.7 all-gather.2
  140.4 67.7 all-gather.4

commit v14 on v12

--- a/solution.py
+++ b/solution.py
@@ -53,7 +53,7 @@
 
 def leaf_backward(parents, leaf_solved, leaf_link, leaf_inverse):
     count, width, columns = leaf_solved.shape
-    per_step = max(d for d in range(1, 9) if count % d == 0)
+    per_step = max(d for d in range(1, 13) if count % d == 0)
     pieces = parents.shape[1:]
 
     def own(step):

time: 236 us -> 236 us (level)
  no operation moved by 1% of the time
where the time goes in v14:
time: 236 us; the launch traced here: 235 us
  waiting for transfers between devices  109 us (46%)
  starting transfers between devices  38.7 us (16%)
  local copies, waits for them, and re-layouts  28.7 us (12%)
  matrix products  24.6 us (10%)
  between operations  14.5 us (6%)
  other arithmetic  10.7 us (5%)
  Pallas kernels  8.53 us (4%)
    all_gather x1, waiting for transfers between devices, local(): gathered = lax.all_gather(by_y, 'z', axis=0, tiled=True)  65.7 us
    all_to_all x2, waiting for transfers between devices, local(): incoming = lax.all_to_all(partial, 'z', 0, 0, tiled=True)  22.3 us
    ppermute x6, waiting for transfers between devices, local(): arrivals.append(lax.ppermute(outbound, 'y', pairs))  12.5 us
    all_to_all x2, starting transfers between devices, local(): incoming = lax.all_to_all(partial, 'z', 0, 0, tiled=True)  11.9 us
    unnamed x44, local copies, waits for them, and re-layouts  11.6 us
    pallas_call x1, Pallas kernels, leaf_backward(): pl.pallas_call(leaf_backward_kernel, grid=(count // per_step,), in_specs=...  8.53 us
    dot_general x2, matrix products, split_slot_sums(): jnp.einsum('sk,k...->s...', select, high, preferred_element_type=jnp.floa...  8.46 us
    ppermute x3, starting transfers between devices, local(): lax.ppermute(top_sum, ROW, [(i, i ^ step) for i in range(rows)])  7.7 us
  transfers between devices with their start and end apart: 19, of which 11 were waited for; matrix products, arithmetic and copies ran while one was open for 18% of the time, Pallas kernels for 0%

profile of v14, /device:TPU:1, one launch (start us, length us, event | category | flops | bytes accessed | tf_op | source)
XLA Modules:
  0.0 235.1 jit_solution(4041474228148458374)
XLA Ops:
  8.9 2.1 collective-permute-start.6
  11.0 2.6 %collective-permute-start.7 = (bf16[2,128,128]{2,1,0:T(8,128)(2,1)S(1)}, bf16[2,128,128]{2,1,0:T(8,128)(2,1)S(1)}, u32[]{:S(2)}, u32[]{:S(2)}) collective-permute-start(bf16[2,128,128]{2,1,0:T(8,128)(2,1)S(1)} %constant_dynamic-update-slice_fusion), channel_id=1, source_target_pairs={{0,2},{1,3},{2,0},{3,1},{4,6},{5,7},{6,4},{7,5},{8,10},{9,11},{10,... | collective-permute-start | bytes 196616 | tf_op jit(solution)/shard_map/ppermute | solution.py:116
  15.4 2.2 convolution_convert_fusion.solved_ref
  19.3 2.3 fusion
  21.5 2.5 %add_convert_fusion = bf16[16,512,128]{2,0,1:T(8,128)(2,1)S(1)} fusion(f32[16,512,128]{2,0,1:T(8,128)S(1)} %fusion, bf16[24,512,128]{2,1,0:T(8,128)(2,1)S(1)} %get-tuple-element.28, s32[24]{0:T(128)S(1)} %get-tuple-element.25), kind=kOutput, calls=%fused_computation.7 | convolution fusion | flops 52429184 | bytes 9437280 | tf_op jit(solution)/shard_map/sk,k...->s.../dot_general | solution.py:39
  26.6 4.2 %fusion.2 = f32[16,512,128]{2,0,1:T(8,128)} fusion(bf16[24,512,128]{2,1,0:T(8,128)(2,1)S(1)} %get-tuple-element.29, s32[24]{0:T(128)S(1)} %broadcast_add_fusion), kind=kOutput, calls=%fused_computation.12 | convolution fusion | flops 50332032 | bytes 7340128 | tf_op jit(solution)/shard_map/sk,k...->s.../dot_general | solution.py:40
  30.9 1.7 collective-permute-start.5
  33.3 1.5 gather_fusion.1
  35.7 6.0 %add_convert_fusion.1 = bf16[16,512,128]{2,0,1:T(8,128)(2,1)} fusion(f32[16,512,128]{2,0,1:T(8,128)} %fusion.2, bf16[24,512,128]{2,1,0:T(8,128)(2,1)S(1)} %get-tuple-element.28, s32[24]{0:T(128)S(1)} %broadcast_add_fusion), kind=kOutput, calls=%fused_computation.8 | convolution fusion | flops 52429184 | bytes 9437280 | tf_op jit(solution)/shard_map/sk,k...->s.../dot_general | solution.py:39
  41.9 2.3 pad_maximum_fusion
  47.1 1.8 collective-permute-start.1
  49.7 2.1 collective-permute-start.2
  52.2 2.6 %fusion.17 = bf16[8,16,16,128]{3,1,2,0:T(8,128)(2,1)} fusion(bf16[8,16,16,128]{3,1,2,0:T(8,128)(2,1)} %collective-permute-done.5, bf16[8,16,16,128]{3,1,2,0:T(8,128)(2,1)} %collective-permute-done.4, bf16[8,16,16,128]{3,1,2,0:T(8,128)(2,1)} %collective-permute-done.3, bf16[16,8,4,16,128]{4,0,3,2,1:T(8,128)(2,1)} %bitcast.120, s32[]{:T(128)S(6)} %select_n.125), kind=kLoop, calls=%fused_computation.37 | loop fusion | flops 2097152 | bytes 2621444 | tf_op jit(solution)/shard_map/convert_element_type | solution.py:139
  54.8 8.3 %all-to-all-start.1 = ((bf16[8,16,16,128]{3,1,2,0:T(8,128)(2,1)}), bf16[8,16,16,128]{3,1,2,0:T(8,128)(2,1)S(1)}, u32[]{:S(2)}, u32[]{:S(2)}) async-start(bf16[8,16,16,128]{3,1,2,0:T(8,128)(2,1)} %fusion.17), calls=%async_computation.1 | async-start | bytes 1048576 | tf_op jit(solution)/shard_map/all_to_all | solution.py:142
  63.5 9.5 %collective-permute-done.1 = bf16[8,17,16,128]{3,2,1,0:T(8,128)(2,1)S(1)} collective-permute-done((bf16[8,17,16,128]{3,2,1,0:T(8,128)(2,1)}, bf16[8,17,16,128]{3,2,1,0:T(8,128)(2,1)S(1)}, u32[]{:S(2)}, u32[]{:S(2)}) %collective-permute-start.1) | collective-permute-done | bytes 557088 | tf_op jit(solution)/shard_map/ppermute | solution.py:138
  73.0 2.4 %collective-permute-done.2 = bf16[8,17,16,128]{3,2,1,0:T(8,128)(2,1)S(1)} collective-permute-done((bf16[8,17,16,128]{3,2,1,0:T(8,128)(2,1)}, bf16[8,17,16,128]{3,2,1,0:T(8,128)(2,1)S(1)}, u32[]{:S(2)}, u32[]{:S(2)}) %collective-permute-start.2) | collective-permute-done | bytes 557088 | tf_op jit(solution)/shard_map/ppermute | solution.py:138
  78.9 6.0 %all-to-all-done.1 = bf16[8,16,16,128]{3,1,2,0:T(8,128)(2,1)S(1)} async-done(((bf16[8,16,16,128]{3,1,2,0:T(8,128)(2,1)}), bf16[8,16,16,128]{3,1,2,0:T(8,128)(2,1)S(1)}, u32[]{:S(2)}, u32[]{:S(2)}) %all-to-all-start.1) | async-done | bytes 524320 | tf_op jit(solution)/shard_map/all_to_all | solution.py:142
  84.9 3.5 %all-to-all-start = ((bf16[8,20,16,128]{3,2,1,0:T(8,128)(2,1)}), bf16[8,20,16,128]{3,2,1,0:T(8,128)(2,1)S(1)}, u32[]{:S(2)}, u32[]{:S(2)}) async-start(bf16[8,20,16,128]{3,2,1,0:T(8,128)(2,1)} %slice_dynamic-update-slice_fusion), calls=%async_computation | async-start | bytes 1310720 | tf_op jit(solution)/shard_map/all_to_all | solution.py:142
  89.9 16.3 %all-to-all-done = bf16[8,20,16,128]{3,2,1,0:T(8,128)(2,1)S(1)} async-done(((bf16[8,20,16,128]{3,2,1,0:T(8,128)(2,1)}), bf16[8,20,16,128]{3,2,1,0:T(8,128)(2,1)S(1)}, u32[]{:S(2)}, u32[]{:S(2)}) %all-to-all-start) | async-done | bytes 655392 | tf_op jit(solution)/shard_map/all_to_all | solution.py:142
  107.2 2.0 convolution_convert_fusion.2
  109.2 1.9 fusion.18
  112.1 3.7 %collective-permute-start.9 = (f32[4,16,128]{2,0,1:T(4,128)S(1)}, f32[4,16,128]{2,0,1:T(4,128)S(1)}, u32[]{:S(2)}, u32[]{:S(2)}) collective-permute-start(f32[4,16,128]{2,0,1:T(4,128)S(1)} %fusion.24), channel_id=1, source_target_pairs={{0,32},{32,0},{64,96},{96,64},{128,160},{160,128},{192,224},{224,1... | collective-permute-start | bytes 98312 | tf_op jit(solution)/shard_map/ppermute | solution.py:158
  118.0 1.6 collective-permute-done.10
  119.6 2.8 %collective-permute-start.11 = (f32[4,16,128]{2,0,1:T(4,128)S(1)}, f32[4,16,128]{2,0,1:T(4,128)S(1)}, u32[]{:S(2)}, u32[]{:S(2)}) collective-permute-start(f32[4,16,128]{2,0,1:T(4,128)S(1)} %add.177), channel_id=1, source_target_pairs={{0,128},{32,160},{64,192},{96,224},{128,0},{160,32},{192,64},{224,... | collective-permute-start | bytes 98312 | tf_op jit(solution)/shard_map/ppermute | solution.py:158
  122.5 1.5 collective-permute-done.11
  127.1 5.5 %collective-permute-start.13 = (bf16[44,16,128]{2,1,0:T(8,128)(2,1)S(1)}, bf16[44,16,128]{2,1,0:T(8,128)(2,1)S(1)}, u32[]{:S(2)}, u32[]{:S(2)}) collective-permute-start(bf16[44,16,128]{2,1,0:T(8,128)(2,1)S(1)} %get-tuple-element.38), channel_id=1, source_target_pairs={{0,2},{1,3},{2,0},{3,1},{4,6},{5,7},{6,4},{7,5},{8,10},{9,11},{10,... | collective-permute-start | bytes 540680 | tf_op jit(solution)/shard_map/ppermute | solution.py:177
  132.5 1.7 collective-permute-done.12
  134.2 4.1 %collective-permute-done.13 = bf16[44,16,128]{2,1,0:T(8,128)(2,1)S(1)} collective-permute-done((bf16[44,16,128]{2,1,0:T(8,128)(2,1)S(1)}, bf16[44,16,128]{2,1,0:T(8,128)(2,1)S(1)}, u32[]{:S(2)}, u32[]{:S(2)}) %collective-permute-start.13) | collective-permute-done | bytes 180256 | tf_op jit(solution)/shard_map/ppermute | solution.py:177
  142.5 65.7 %all-gather.5.cloned.1.call-done = bf16[32,44,16,128]{3,2,1,0:T(8,128)(2,1)} async-done(((bf16[4,44,16,128]{3,2,1,0:T(8,128)(2,1)}), bf16[32,44,16,128]{3,2,1,0:T(8,128)(2,1)}) %all-gather.5.cloned.1.call-update) | async-done | bytes 5767184 | tf_op jit(solution)/shard_map/all_gather | solution.py:179
  208.2 1.8 copy_bitcast_fusion
  214.2 5.5 %gather_fusion.5 = bf16[24,32,16,128]{3,2,1,0:T(8,128)(2,1)} fusion(bf16[32,44,16,128]{3,2,1,0:T(8,128)(2,1)} %all-gather.5.cloned.1.call-done, s32[1024]{0:T(1024)S(1)} %pad_clamp_fusion), kind=kCustom, calls=%fused_computation.5 | custom fusion | bytes 6291552 | tf_op jit(solution)/shard_map/gather | solution.py:185
  219.7 8.5 %shard_map.165 = bf16[24,128,512]{2,1,0:T(8,128)(2,1)} custom-call(bf16[24,32,16,128]{3,2,1,0:T(8,128)(2,1)} %gather_fusion.5, bf16[24,128,512]{2,1,0:T(8,128)(2,1)} %copy-done.2, bf16[24,128,128]{2,1,0:T(8,128)(2,1)} %bitcast.122, bf16[24,128,128]{2,1,0:T(8,128)(2,1)} %bitcast.123), custom_call_target="tpu_custom_call" | custom-call | flops 805306368 | bytes 11010048 | tf_op jit(solution)/shard_map/pallas_call | solution.py:67
  (113 shorter events, 34.6 us)
Async XLA Ops:
  7.2 8.2 %copy-start = (bf16[24,128,512]{2,1,0:T(8,128)(2,1)S(1)}, bf16[24,128,512]{2,1,0:T(8,128)(2,1)}, u32[]{:S(2)}) copy-start(bf16[24,128,512]{2,1,0:T(8,128)(2,1)} %param.14) | copy-start | bytes 9437188
  7.2 100.0 %all-gather.3.cloned.1.call-start = ((), (), s32[]{:S(2)}) async-start(), calls=%async_computation.2 | async-start | bytes 2359296 | tf_op jit(solution)/shard_map/all_gather | solution.py:118
  8.9 22.0 %collective-permute-start.6 = (bf16[2,128,128]{2,1,0:T(8,128)(2,1)S(1)}, bf16[2,128,128]{2,1,0:T(8,128)(2,1)S(1)}, u32[]{:S(2)}, u32[]{:S(2)}) collective-permute-start(bf16[2,128,128]{2,1,0:T(8,128)(2,1)S(1)} %constant_dynamic-update-slice_fusion), channel_id=1, source_target_pairs={{0,1},{1,2},{2,3},{3,0},{4,5},{5,6},{6,7},{7,4},{8,9},{9,10},{10,1... | collective-permute-start | bytes 196616 | tf_op jit(solution)/shard_map/ppermute | solution.py:116
  11.0 21.5 %collective-permute-start.7 = (bf16[2,128,128]{2,1,0:T(8,128)(2,1)S(1)}, bf16[2,128,128]{2,1,0:T(8,128)(2,1)S(1)}, u32[]{:S(2)}, u32[]{:S(2)}) collective-permute-start(bf16[2,128,128]{2,1,0:T(8,128)(2,1)S(1)} %constant_dynamic-update-slice_fusion), channel_id=1, source_target_pairs={{0,2},{1,3},{2,0},{3,1},{4,6},{5,7},{6,4},{7,5},{8,10},{9,11},{10,... | collective-permute-start | bytes 196616 | tf_op jit(solution)/shard_map/ppermute | solution.py:116
  13.7 18.9 %collective-permute-start.8 = (bf16[2,128,128]{2,1,0:T(8,128)(2,1)S(1)}, bf16[2,128,128]{2,1,0:T(8,128)(2,1)S(1)}, u32[]{:S(2)}, u32[]{:S(2)}) collective-permute-start(bf16[2,128,128]{2,1,0:T(8,128)(2,1)S(1)} %constant_dynamic-update-slice_fusion), channel_id=1, source_target_pairs={{0,3},{1,0},{2,1},{3,2},{4,7},{5,4},{6,5},{7,6},{8,11},{9,8},{10,9... | collective-permute-start | bytes 196616 | tf_op jit(solution)/shard_map/ppermute | solution.py:116
  15.4 2.2 copy-start.5
  24.0 6.9 %copy-start.3 = (bf16[16,512,128]{2,0,1:T(8,128)(2,1)}, bf16[16,512,128]{2,0,1:T(8,128)(2,1)S(1)}, u32[]{:S(2)}) copy-start(bf16[16,512,128]{2,0,1:T(8,128)(2,1)S(1)} %add_convert_fusion) | copy-start | bytes 6291460
  25.4 24.3 %collective-permute-start.3 = (bf16[8,16,16,128]{3,1,2,0:T(8,128)(2,1)}, bf16[8,16,16,128]{3,1,2,0:T(8,128)(2,1)}, u32[]{:S(2)}, u32[]{:S(2)}) collective-permute-start(bf16[8,16,16,128]{3,1,2,0:T(8,128)(2,1)} %get-tuple-element.34), channel_id=1, source_target_pairs={{0,1},{1,2},{2,3},{3,0},{4,5},{5,6},{6,7},{7,4},{8,9},{9,10},{10,1... | collective-permute-start | bytes 1572872 | tf_op jit(solution)/shard_map/ppermute | solution.py:138
  25.8 26.1 %collective-permute-start.4 = (bf16[8,16,16,128]{3,1,2,0:T(8,128)(2,1)}, bf16[8,16,16,128]{3,1,2,0:T(8,128)(2,1)}, u32[]{:S(2)}, u32[]{:S(2)}) collective-permute-start(bf16[8,16,16,128]{3,1,2,0:T(8,128)(2,1)} %get-tuple-element.35), channel_id=1, source_target_pairs={{0,2},{1,3},{2,0},{3,1},{4,6},{5,7},{6,4},{7,5},{8,10},{9,11},{10,... | collective-permute-start | bytes 1572872 | tf_op jit(solution)/shard_map/ppermute | solution.py:138
  30.9 21.3 %collective-permute-start.5 = (bf16[8,16,16,128]{3,1,2,0:T(8,128)(2,1)}, bf16[8,16,16,128]{3,1,2,0:T(8,128)(2,1)}, u32[]{:S(2)}, u32[]{:S(2)}) collective-permute-start(bf16[8,16,16,128]{3,1,2,0:T(8,128)(2,1)} %get-tuple-element.36), channel_id=1, source_target_pairs={{0,3},{1,0},{2,1},{3,2},{4,7},{5,4},{6,5},{7,6},{8,11},{9,8},{10,9... | collective-permute-start | bytes 1572872 | tf_op jit(solution)/shard_map/ppermute | solution.py:138
  35.7 6.0 %copy-start.11 = (bf16[1,128,512]{2,1,0:T(8,128)(2,1)S(1)}, bf16[1,128,512]{2,1,0:T(8,128)(2,1)}, u32[]{:S(2)}) copy-start(bf16[1,128,512]{2,1,0:T(8,128)(2,1)} %param.18) | copy-start | bytes 393220
  45.7 17.8 %collective-permute-start = (bf16[8,17,16,128]{3,2,1,0:T(8,128)(2,1)}, bf16[8,17,16,128]{3,2,1,0:T(8,128)(2,1)S(1)}, u32[]{:S(2)}, u32[]{:S(2)}) collective-permute-start(bf16[8,17,16,128]{3,2,1,0:T(8,128)(2,1)} %bitcast.116), channel_id=1, source_target_pairs={{0,1},{1,2},{2,3},{3,0},{4,5},{5,6},{6,7},{7,4},{8,9},{9,10},{10,1... | collective-permute-start | bytes 1671176 | tf_op jit(solution)/shard_map/ppermute | solution.py:138
  47.1 25.9 %collective-permute-start.1 = (bf16[8,17,16,128]{3,2,1,0:T(8,128)(2,1)}, bf16[8,17,16,128]{3,2,1,0:T(8,128)(2,1)S(1)}, u32[]{:S(2)}, u32[]{:S(2)}) collective-permute-start(bf16[8,17,16,128]{3,2,1,0:T(8,128)(2,1)} %bitcast.115), channel_id=1, source_target_pairs={{0,2},{1,3},{2,0},{3,1},{4,6},{5,7},{6,4},{7,5},{8,10},{9,11},{10,... | collective-permute-start | bytes 1671176 | tf_op jit(solution)/shard_map/ppermute | solution.py:138
  49.7 25.6 %collective-permute-start.2 = (bf16[8,17,16,128]{3,2,1,0:T(8,128)(2,1)}, bf16[8,17,16,128]{3,2,1,0:T(8,128)(2,1)S(1)}, u32[]{:S(2)}, u32[]{:S(2)}) collective-permute-start(bf16[8,17,16,128]{3,2,1,0:T(8,128)(2,1)} %bitcast.114), channel_id=1, source_target_pairs={{0,3},{1,0},{2,1},{3,2},{4,7},{5,4},{6,5},{7,6},{8,11},{9,8},{10,9... | collective-permute-start | bytes 1671176 | tf_op jit(solution)/shard_map/ppermute | solution.py:138
  54.8 35.0 %copy-start.12 = (s32[8]{0:T(128)S(1)}, s32[8]{0:T(128)}, u32[]{:S(2)}) copy-start(s32[8]{0:T(128)} %param.25) | copy-start | bytes 100
  54.8 35.0 %copy-start.13 = (s32[32]{0:T(128)S(1)}, s32[32]{0:T(128)}, u32[]{:S(2)}) copy-start(s32[32]{0:T(128)} %param.21) | copy-start | bytes 388
  54.8 30.1 %all-to-all-start.1 = ((bf16[8,16,16,128]{3,1,2,0:T(8,128)(2,1)}), bf16[8,16,16,128]{3,1,2,0:T(8,128)(2,1)S(1)}, u32[]{:S(2)}, u32[]{:S(2)}) async-start(bf16[8,16,16,128]{3,1,2,0:T(8,128)(2,1)} %fusion.17), calls=%async_computation.1 | async-start | bytes 1048576 | tf_op jit(solution)/shard_map/all_to_all | solution.py:142
  84.9 21.4 %all-to-all-start = ((bf16[8,20,16,128]{3,2,1,0:T(8,128)(2,1)}), bf16[8,20,16,128]{3,2,1,0:T(8,128)(2,1)S(1)}, u32[]{:S(2)}, u32[]{:S(2)}) async-start(bf16[8,20,16,128]{3,2,1,0:T(8,128)(2,1)} %slice_dynamic-update-slice_fusion), calls=%async_computation | async-start | bytes 1310720 | tf_op jit(solution)/shard_map/all_to_all | solution.py:142
  88.4 119.8 %all-gather.5.cloned.1.call-start = ((), (), s32[]{:S(2)}) async-start(), calls=%async_computation.3 | async-start | bytes 6488064 | tf_op jit(solution)/shard_map/all_gather | solution.py:179
  89.7 21.7 %copy-start.8 = (bf16[8,128,128]{2,1,0:T(8,128)(2,1)S(1)}, bf16[8,128,128]{2,1,0:T(8,128)(2,1)}, u32[]{:S(2)}) copy-start(bf16[8,128,128]{2,1,0:T(8,128)(2,1)} %param.23) | copy-start | bytes 786436
  89.9 21.8 %copy-start.9 = (bf16[8,128,128]{2,1,0:T(8,128)(2,1)S(1)}, bf16[8,128,128]{2,1,0:T(8,128)(2,1)}, u32[]{:S(2)}) copy-start(bf16[8,128,128]{2,1,0:T(8,128)(2,1)} %param.24) | copy-start | bytes 786436
  106.9 17.1 %copy-start.10 = (bf16[4,128,128]{2,1,0:T(8,128)(2,1)S(1)}, bf16[4,128,128]{2,1,0:T(8,128)(2,1)}, u32[]{:S(2)}) copy-start(bf16[4,128,128]{2,1,0:T(8,128)(2,1)} %param.27) | copy-start | bytes 393220
  107.2 18.6 %copy-start.4 = (bf16[32,2,128,128]{3,2,0,1:T(8,128)(2,1)S(1)}, bf16[32,2,128,128]{3,2,0,1:T(8,128)(2,1)}, u32[]{:S(2)}) copy-start(bf16[32,2,128,128]{3,2,0,1:T(8,128)(2,1)} %all-gather.3.cloned.1.call-done) | copy-start | bytes 6291460
  112.1 4.7 %collective-permute-start.9 = (f32[4,16,128]{2,0,1:T(4,128)S(1)}, f32[4,16,128]{2,0,1:T(4,128)S(1)}, u32[]{:S(2)}, u32[]{:S(2)}) collective-permute-start(f32[4,16,128]{2,0,1:T(4,128)S(1)} %fusion.24), channel_id=1, source_target_pairs={{0,32},{32,0},{64,96},{96,64},{128,160},{160,128},{192,224},{224,1... | collective-permute-start | bytes 98312 | tf_op jit(solution)/shard_map/ppermute | solution.py:158
  116.8 2.9 %collective-permute-start.10 = (f32[4,16,128]{2,0,1:T(4,128)S(1)}, f32[4,16,128]{2,0,1:T(4,128)S(1)}, u32[]{:S(2)}, u32[]{:S(2)}) collective-permute-start(f32[4,16,128]{2,0,1:T(4,128)S(1)} %add.176), channel_id=1, source_target_pairs={{0,64},{32,96},{64,0},{96,32},{128,192},{160,224},{192,128},{224,1... | collective-permute-start | bytes 98312 | tf_op jit(solution)/shard_map/ppermute | solution.py:158
  119.6 4.4 %collective-permute-start.11 = (f32[4,16,128]{2,0,1:T(4,128)S(1)}, f32[4,16,128]{2,0,1:T(4,128)S(1)}, u32[]{:S(2)}, u32[]{:S(2)}) collective-permute-start(f32[4,16,128]{2,0,1:T(4,128)S(1)} %add.177), channel_id=1, source_target_pairs={{0,128},{32,160},{64,192},{96,224},{128,0},{160,32},{192,64},{224,... | collective-permute-start | bytes 98312 | tf_op jit(solution)/shard_map/ppermute | solution.py:158
  126.4 13.7 %copy-start.6 = (bf16[24,128,128]{2,1,0:T(8,128)(2,1)S(1)}, bf16[24,128,128]{2,1,0:T(8,128)(2,1)}, u32[]{:S(2)}) copy-start(bf16[24,128,128]{2,1,0:T(8,128)(2,1)} %param.16) | copy-start | bytes 2359300
  126.5 7.8 %collective-permute-start.12 = (bf16[44,16,128]{2,1,0:T(8,128)(2,1)S(1)}, bf16[44,16,128]{2,1,0:T(8,128)(2,1)S(1)}, u32[]{:S(2)}, u32[]{:S(2)}) collective-permute-start(bf16[44,16,128]{2,1,0:T(8,128)(2,1)S(1)} %get-tuple-element.38), channel_id=1, source_target_pairs={{0,1},{1,2},{2,3},{3,0},{4,5},{5,6},{6,7},{7,4},{8,9},{9,10},{10,1... | collective-permute-start | bytes 540680 | tf_op jit(solution)/shard_map/ppermute | solution.py:177
  127.1 11.2 %collective-permute-start.13 = (bf16[44,16,128]{2,1,0:T(8,128)(2,1)S(1)}, bf16[44,16,128]{2,1,0:T(8,128)(2,1)S(1)}, u32[]{:S(2)}, u32[]{:S(2)}) collective-permute-start(bf16[44,16,128]{2,1,0:T(8,128)(2,1)S(1)} %get-tuple-element.38), channel_id=1, source_target_pairs={{0,2},{1,3},{2,0},{3,1},{4,6},{5,7},{6,4},{7,5},{8,10},{9,11},{10,... | collective-permute-start | bytes 540680 | tf_op jit(solution)/shard_map/ppermute | solution.py:177
  132.5 5.8 %collective-permute-start.14 = (bf16[44,16,128]{2,1,0:T(8,128)(2,1)S(1)}, bf16[44,16,128]{2,1,0:T(8,128)(2,1)S(1)}, u32[]{:S(2)}, u32[]{:S(2)}) collective-permute-start(bf16[44,16,128]{2,1,0:T(8,128)(2,1)S(1)} %get-tuple-element.38), channel_id=1, source_target_pairs={{0,3},{1,0},{2,1},{3,2},{4,7},{5,4},{6,5},{7,6},{8,11},{9,8},{10,9... | collective-permute-start | bytes 540680 | tf_op jit(solution)/shard_map/ppermute | solution.py:177
  138.3 3.0 %copy-start.7 = (bf16[24,128,128]{2,1,0:T(8,128)(2,1)S(1)}, bf16[24,128,128]{2,1,0:T(8,128)(2,1)}, u32[]{:S(2)}) copy-start(bf16[24,128,128]{2,1,0:T(8,128)(2,1)} %param.15) | copy-start | bytes 2359300
  219.7 8.5 %copy-start.1 = (bf16[24,128,512]{2,1,0:T(8,128)(2,1)S(1)}, bf16[24,128,512]{2,1,0:T(8,128)(2,1)}, u32[]{:S(2)}) copy-start(bf16[24,128,512]{2,1,0:T(8,128)(2,1)} %param.14) | copy-start | bytes 9437188
  (1 other events, 1.7 us)
Sparse Core Ops, SparseCore 0:
  35.8 51.7 all-gather.2
  140.2 67.9 all-gather.4
